TPU v7x, 128 devices: a whole 4x4x4 slice. The times are simulated.
128 devices in a mesh: adapter: 32 (over z, y, x_hi), tensor: 4 (over x_lo, core).
Axes of the slice: x: 4 (x_hi: 2, x_lo: 2; x = x_hi * 2 + x_lo), y: 4, z: 4, core: 2. Of those that a mesh axis runs over, the one named last changes fastest.
Arguments:
- partials: bfloat16 [4, 2048, 8192], P('tensor', 'adapter'), may hold values from -4 to 4
- residual: bfloat16 [2048, 8192], P('adapter'), may hold values from -80 to 80
- attention_norm_gain: bfloat16 [8192], replicated, may hold values from 0.25 to 1.75
- key_value_weight: bfloat16 [8192, 8, 256], P(None, 'tensor'), may hold values from -0.0625 to 0.0625
- adapter_down_weight: bfloat16 [8192, 32768], P('tensor', 'adapter'), may hold values from -0.0625 to 0.0625
- adapter_up_weight: bfloat16 [32768, 8, 256], P('adapter', 'tensor'), may hold values from -0.75 to 0.75
- row_adapter_index: int32 [2048], P('adapter'), may hold values from 0 to 511, as said below
- queries: bfloat16 [2048, 8192], P('adapter', 'tensor'), may hold values from -10 to 10
- key_value_cache: bfloat16 [256, 2, 1024, 1024], P('adapter', None, None, 'tensor'), may hold values from -10 to 10
- prompt_cache_length: int32 [256], P('adapter'), may hold values from 2 to 1024
Outputs:
- hidden_out: bfloat16 [2048, 8192], P('adapter', 'tensor')
- new_kv: bfloat16 [2048, 8, 256], P('adapter', 'tensor')
- attn_out: bfloat16 [2048, 8192], P('adapter', 'tensor')
Inputs may be any that keep to these rules, and one draw needn't show every extreme that they name: `row_adapter_index`: adapter g is held by index g // 16 of the adapter axis. Of the 64 rows on one index of the adapter axis at most 8 use adapters held by one index; in every draw one index receives exactly 8 rows from every index.
All inputs are finite; a program needn't handle non-finite values.
Results may differ from a plain program's by a relative error of at most 0.012.
Values may be sent and summed in bfloat16 or wider, within the bound.
No kernel may reach another device: no remote copies, remote signals or barrier semaphores. Data moves between devices by JAX's collectives and lax.ppermute only.
A program may use at most 128 MiB of HBM per device.

v0:
```python
import jax
import jax.numpy as jnp
from jax import lax
from jax.sharding import PartitionSpec as P

HEAD_SIZE = 128
ADAPTER_RANK = 64
FAN = 8


EPSILON = 1e-05
ADAPTER_SCALE = 0.5


def per_device(
    partials,
    residual,
    attention_norm_gain,
    key_value_weight,
    adapter_down_weight,
    adapter_up_weight,
    row_adapter_index,
    queries,
    key_value_cache,
    prompt_cache_length,
):
    row_dev = residual.shape[0]
    model_width = residual.shape[1]
    tensor_count = lax.axis_size("tensor")
    quarter = model_width // tensor_count
    tensor_index = lax.axis_index("tensor")
    flat_weight = key_value_weight.reshape(model_width, -1)
    partial_own = partials[0].astype(jnp.float32)
    summed = lax.psum(partial_own.astype(jnp.bfloat16), "tensor").astype(jnp.float32)
    hidden_full = (residual.astype(jnp.float32) + summed).astype(jnp.bfloat16)
    hidden_wide = hidden_full.astype(jnp.float32)
    mean_sq = jnp.mean(hidden_wide * hidden_wide, axis=1, keepdims=True)
    normed_full = (
        hidden_wide * lax.rsqrt(mean_sq + EPSILON) * attention_norm_gain.astype(jnp.float32)
    ).astype(jnp.bfloat16)
    hidden_part = lax.dynamic_slice_in_dim(hidden_full, tensor_index * quarter, quarter, 1)
    normed_part = lax.dynamic_slice_in_dim(normed_full, tensor_index * quarter, quarter, 1)
    base_kv = jnp.dot(normed_full, flat_weight, preferred_element_type=jnp.float32)
    adapt_count = lax.axis_size("adapter")
    capacity = max(2, 4 * row_dev // adapt_count)
    slot_count = adapt_count * capacity
    adapter_grouped = adapter_down_weight.shape[1] // ADAPTER_RANK
    owner_index = row_adapter_index // adapter_grouped
    local_id = row_adapter_index % adapter_grouped
    row_order = jnp.arange(row_dev)
    same_owner = owner_index[:, None] == owner_index[None, :]
    earlier = row_order[None, :] < row_order[:, None]
    slot_rank = jnp.sum((same_owner & earlier).astype(jnp.int32), axis=1)
    row_slot = owner_index * capacity + slot_rank
    row_to_slot = jnp.arange(slot_count)[:, None] == row_slot[None, :]
    slot_matrix = row_to_slot.astype(jnp.bfloat16)
    send_rows = (
        jnp.dot(slot_matrix, normed_part, preferred_element_type=jnp.float32)
        .astype(jnp.bfloat16)
        .reshape(adapt_count, capacity, quarter)
    )
    send_ids = (jnp.sum(jnp.where(row_to_slot, local_id[None, :] + 1, 0), axis=1) - 1).reshape(
        adapt_count, capacity
    )
    flattened_up = adapter_up_weight.reshape(adapter_grouped * ADAPTER_RANK, -1)
    rows_in = lax.all_to_all(send_rows, "adapter", split_axis=0, concat_axis=0, tiled=True)
    ids_in = lax.all_to_all(send_ids, "adapter", split_axis=0, concat_axis=0, tiled=True)
    item_count = rows_in.shape[1]
    flattened_rows = rows_in.reshape(-1, rows_in.shape[2])
    adapter_pick = ids_in.reshape(-1)[:, None] == jnp.arange(adapter_grouped)[None, :]
    projected_rows = jnp.dot(
        flattened_rows, adapter_down_weight, preferred_element_type=jnp.float32
    ).reshape(-1, adapter_grouped, ADAPTER_RANK)
    partial_low = jnp.sum(jnp.where(adapter_pick[:, :, None], projected_rows, 0.0), axis=1)
    reduced_rank_rows = lax.psum(partial_low.astype(jnp.bfloat16), "tensor")
    expanded_rows = jnp.where(
        adapter_pick[:, :, None], reduced_rank_rows[:, None, :], jnp.zeros((), jnp.bfloat16)
    ).reshape(-1, adapter_grouped * ADAPTER_RANK)
    adapter_update = (
        ADAPTER_SCALE * jnp.dot(expanded_rows, flattened_up, preferred_element_type=jnp.float32)
    ).astype(jnp.bfloat16)
    adapter_update = adapter_update.reshape(adapt_count, item_count, -1)
    returned = lax.all_to_all(adapter_update, "adapter", split_axis=0, concat_axis=0, tiled=True)
    returned = returned.reshape(slot_count, -1)
    update_rows = lax.dot_general(
        slot_matrix, returned, (((0,), (0,)), ((), ())), preferred_element_type=jnp.float32
    )
    local_heads = key_value_weight.shape[1]
    new_kv = (
        (base_kv + update_rows).astype(jnp.bfloat16).reshape(row_dev, local_heads, 2 * HEAD_SIZE)
    )
    local_prompts = key_value_cache.shape[0]
    cache_length = key_value_cache.shape[2]
    group_size = queries.shape[1] // (local_heads * HEAD_SIZE)
    score_scale = HEAD_SIZE ** (-0.5)
    query_heads = queries.reshape(local_prompts, FAN, local_heads, group_size, HEAD_SIZE)
    cache_keys = key_value_cache[:, 0].reshape(local_prompts, cache_length, local_heads, HEAD_SIZE)
    cache_values = key_value_cache[:, 1].reshape(
        local_prompts, cache_length, local_heads, HEAD_SIZE
    )
    scores = (
        jnp.einsum("pfkgd,pckd->pfkgc", query_heads, cache_keys, preferred_element_type=jnp.float32)
        * score_scale
    )
    valid_mask = jnp.arange(cache_length)[None, :] < prompt_cache_length[:, None]
    scores = jnp.where(valid_mask[:, None, None, None, :], scores, -jnp.inf)
    new_heads = new_kv.reshape(local_prompts, FAN, local_heads, 2 * HEAD_SIZE)
    own_key = new_heads[:, :, :, :HEAD_SIZE]
    own_value = new_heads[:, :, :, HEAD_SIZE:]
    own_score = (
        jnp.einsum("pfkgd,pfkd->pfkg", query_heads, own_key, preferred_element_type=jnp.float32)
        * score_scale
    )
    score_top = jnp.maximum(jnp.max(scores, axis=-1), own_score)
    weights = jnp.exp(scores - score_top[:, :, :, :, None]).astype(jnp.bfloat16)
    own_weight = jnp.exp(own_score - score_top).astype(jnp.bfloat16).astype(jnp.float32)
    weight_total = jnp.sum(weights, axis=-1, dtype=jnp.float32) + own_weight
    weighted = jnp.einsum(
        "pfkgc,pckd->pfkgd", weights, cache_values, preferred_element_type=jnp.float32
    )
    weighted = (
        weighted + own_weight[:, :, :, :, None] * own_value.astype(jnp.float32)[:, :, :, None, :]
    )
    attended = (weighted / weight_total[:, :, :, :, None]).astype(jnp.bfloat16).reshape(row_dev, -1)
    return (hidden_part, new_kv, attended)


def solution(mesh):
    return jax.shard_map(
        per_device,
        mesh=mesh,
        in_specs=(
            P("tensor", "adapter", None),
            P("adapter", None),
            P(),
            P(None, "tensor", None),
            P("tensor", "adapter"),
            P("adapter", "tensor", None),
            P("adapter"),
            P("adapter", "tensor"),
            P("adapter", None, None, "tensor"),
            P("adapter"),
        ),
        out_specs=(P("adapter", "tensor"), P("adapter", "tensor", None), P("adapter", "tensor")),
        check_vma=False,
    )
```

profile of v0, /device:TPU:0, one launch (start us, length us, event | category | flops | bytes accessed | tf_op | source)
XLA Modules:
  0.0 133.9 jit_solution(7817987745715617410)
XLA Ops:
  7.2 0.7 all-reduce.2.cloned.1.call-update
  7.9 0.7 and_select_fusion.1
  8.9 0.7 sub.25
  9.6 10.9 %all-to-all-start = ((s32[32,1,8]{2,1,0:T(1,128)}), s32[32,1,8]{2,1,0:T(1,128)S(1)}, u32[]{:S(2)}, u32[]{:S(2)}) async-start(s32[32,1,8]{2,1,0:T(1,128)} %bitcast.1), calls=%async_computation | async-start | bytes 32768 | tf_op jit(solution)/shard_map/all_to_all | solution.py:67
  20.5 0.7 convert_element_type.58
  21.2 8.1 %copy.49 = bf16[1024,8,2,256]{3,1,2,0:T(8,128)(2,1)} copy(bf16[1024,8,2,256]{3,2,1,0:T(2,128)(2,1)} %bitcast.77) | data formatting | bytes 16777216
  29.3 6.6 %copy.31 = bf16[2048,1024]{0,1:T(8,128)(2,1)} copy(bf16[2048,1024]{1,0:T(8,128)(2,1)} %param.14) | data formatting | bytes 8388608 | tf_op args[4]
  35.9 0.2 copy.50
  36.1 5.7 %fusion.33 = (bf16[8,1,1024,256]{3,2,1,0:T(8,128)(2,1)}, bf16[8,1,1024,256]{3,2,1,0:T(8,128)(2,1)}) fusion(bf16[8,2,1024,256]{3,2,1,0:T(8,128)(2,1)} %param.18), kind=kLoop, calls=%fused_computation.63 | loop fusion | bytes 16777216 | tf_op jit(solution)/shard_map/slice | solution.py:97
  41.8 6.5 %copy.48 = bf16[8,1,1024,256]{2,3,0,1:T(8,128)(2,1)} copy(bf16[8,1,1024,256]{3,2,1,0:T(8,128)(2,1)} %get-tuple-element.8) | data formatting | bytes 8388608
  48.3 6.5 %copy.47 = bf16[8,1,1024,256]{2,3,0,1:T(8,128)(2,1)} copy(bf16[8,1,1024,256]{3,2,1,0:T(8,128)(2,1)} %get-tuple-element.7) | data formatting | bytes 8388608
  54.9 1.7 %fusion.3 = (f32[64]{0:T(128)S(1)}, bf16[64,8192]{1,0:T(8,128)(2,1)S(1)}) fusion(bf16[64,8192]{1,0:T(8,128)(2,1)} %all-reduce.2.cloned.1.call-done, bf16[64,8192]{1,0:T(8,128)(2,1)S(1)} %copy-done.3), kind=kLoop, calls=%fused_computation.10 | loop fusion | flops 3669952 | bytes 3145984 | tf_op jit(solution)/shard_map/reduce_sum | solution.py:37
  56.6 0.3 fusion.5
  56.9 1.5 %fusion.2 = bf16[32,8,2048]{2,1,0:T(8,128)(2,1)} fusion(bf16[64,8192]{1,0:T(8,128)(2,1)S(1)} %fusion.5, s32[]{:T(128)S(6)} %select_n.45, s32[64]{0:T(128)S(1)} %multiply_add_fusion), kind=kOutput, calls=%fused_computation.9 | convolution fusion | flops 67649536 | bytes 1311236 | tf_op jit(solution)/shard_map/dot_general | solution.py:58
  58.4 9.9 %all-to-all-start.1 = ((bf16[32,8,2048]{2,1,0:T(8,128)(2,1)}), bf16[32,8,2048]{2,1,0:T(8,128)(2,1)}, u32[]{:S(2)}, u32[]{:S(2)}) async-start(bf16[32,8,2048]{2,1,0:T(8,128)(2,1)} %fusion.2), calls=%async_computation.1 | async-start | bytes 2097152 | tf_op jit(solution)/shard_map/all_to_all | solution.py:66
  68.5 5.0 %bitcast_reduce_fusion = (f32[8,8,2,8]{3,1,2,0:T(8,128)S(1)}, f32[8,2,1024,8,8]{2,4,3,1,0:T(8,128)}) fusion(pred[8,1024]{1,0:T(8,128)(4,1)S(1)} %iota_compare_fusion.3, bf16[8,1024,2,128,1]{1,3,4,2,0:T(8,128)(2,1)} %bitcast.80, bf16[8,8,2,8,128]{4,1,3,2,0:T(8,128)(2,1)S(1)} %bitcast.74), kind=kOutput, calls=%fused_computation.1 | convolution fusion | flops 271580160 | bytes 8663040 | tf_op jit(solution)/shard_map/pfkgd,pckd->pfkgc/dot_general | solution.py:102
  73.5 0.5 broadcast.111
  74.0 0.7 reduce.3
  74.8 12.5 %all-to-all-done.1 = bf16[32,8,2048]{2,1,0:T(8,128)(2,1)} async-done(((bf16[32,8,2048]{2,1,0:T(8,128)(2,1)}), bf16[32,8,2048]{2,1,0:T(8,128)(2,1)}, u32[]{:S(2)}, u32[]{:S(2)}) %all-to-all-start.1) | async-done | bytes 1048608 | tf_op jit(solution)/shard_map/all_to_all | solution.py:66
  87.3 3.8 %fusion.6 = bf16[256,64]{0,1:T(8,128)(2,1)S(1)} fusion(bf16[16,64,2048]{2,1,0:T(8,128)(2,1)} %bitcast.79, bf16[32,8,2048]{2,1,0:T(8,128)(2,1)} %all-to-all-done.1, pred[256,16]{0,1:T(8,128)(4,1)S(1)} %iota_compare_fusion.5), kind=kOutput, calls=%fused_computation.15 | convolution fusion | flops 1074249728 | bytes 5279744 | tf_op jit(solution)/shard_map/dot_general | solution.py:71
  91.1 10.4 %psum.15 = bf16[256,64]{0,1:T(8,128)(2,1)S(1)} all-reduce(bf16[256,64]{0,1:T(8,128)(2,1)S(1)} %fusion.6), channel_id=1, replica_groups=mesh['adapter'=32,'tensor'=4] {'tensor'}, use_global_device_ids=true, to_apply=%region_5.6 | all-reduce | flops 16384 | bytes 65536 | tf_op jit(solution)/shard_map/psum | solution.py:75
  101.6 1.2 fusion.11
  102.8 4.1 %all-to-all-start.2 = ((bf16[32,8,512]{2,1,0:T(8,128)(2,1)}), bf16[32,8,512]{2,1,0:T(8,128)(2,1)S(1)}, u32[]{:S(2)}, u32[]{:S(2)}) async-start(bf16[32,8,512]{2,1,0:T(8,128)(2,1)} %fusion.11), calls=%async_computation.2 | async-start | bytes 524288 | tf_op jit(solution)/shard_map/all_to_all | solution.py:83
  106.9 4.9 %fusion.34 = f32[64,512]{1,0:T(8,128)S(1)} fusion(bf16[64,8192]{1,0:T(8,128)(2,1)S(1)} %fusion.5, bf16[8192,512]{1,0:T(8,128)(2,1)} %bitcast.76), kind=kOutput, calls=%fused_computation.64 | convolution fusion | flops 536870912 | bytes 9568256 | tf_op jit(solution)/shard_map/dot_general | solution.py:43
  111.8 0.7 constant_dynamic-slice_fusion
  112.5 5.1 %all-to-all-done.2 = bf16[32,8,512]{2,1,0:T(8,128)(2,1)S(1)} async-done(((bf16[32,8,512]{2,1,0:T(8,128)(2,1)}), bf16[32,8,512]{2,1,0:T(8,128)(2,1)S(1)}, u32[]{:S(2)}, u32[]{:S(2)}) %all-to-all-start.2) | async-done | bytes 262176 | tf_op jit(solution)/shard_map/all_to_all | solution.py:83
  117.6 0.2 fusion.12
  117.8 0.7 reshape.131
  118.5 0.3 fusion.18
  118.8 3.4 %convert_reduce_fusion = f32[8,8,2,8]{3,1,2,0:T(8,128)S(1)} fusion(f32[8,8,2,8]{3,1,2,0:T(8,128)S(1)} %fusion.21, f32[8,2,1024,8,8]{2,4,3,1,0:T(8,128)} %get-tuple-element.14, pred[8,1024]{1,0:T(8,128)(4,1)S(1)} %iota_compare_fusion.3), kind=kLoop, calls=%fused_computation.4 | loop fusion | flops 6290432 | bytes 4210688 | tf_op jit(solution)/shard_map/reduce_sum | solution.py:117
  122.2 4.0 %fusion.10 = bf16[8,8,2,8,128]{4,3,1,2,0:T(8,128)(2,1)S(1)} fusion(bf16[8,1024,2,128,1]{1,3,4,2,0:T(8,128)(2,1)S(1)} %bitcast.78, f32[8,8,2,8]{3,1,2,0:T(8,128)S(1)} %get-tuple-element.3, f32[8,8,2,128]{3,1,2,0:T(8,128)S(1)} %get-tuple-element.9, f32[8,8,2,8]{3,1,2,0:T(8,128)S(1)} %get-tuple-element.4, f32[8,2,1024,8,8]{2,4,3,1,0:T(8,128)} %get-tuple-element.14, ...), kind=kOutput, calls=%fused_computation.21 | convolution fusion | flops 273154048 | bytes 8736768 | tf_op jit(solution)/shard_map/pfkgc,pckd->pfkgd/dot_general | solution.py:118
  126.2 0.8 reshape.133
  (26 shorter events, 0.7 us)
Async XLA Ops:
  7.2 61.3 %copy-start = (bf16[64,2048]{1,0:T(8,128)(2,1)S(1)}, bf16[64,2048]{1,0:T(8,128)(2,1)}, u32[]{:S(2)}) copy-start(bf16[64,2048]{1,0:T(8,128)(2,1)} %param.17) | copy-start | bytes 786436
  7.2 47.7 %all-reduce.2.cloned.1.call-start = ((), (), s32[]{:S(2)}) async-start(), calls=%async_computation.3 | async-start | bytes 2097152 | tf_op jit(solution)/shard_map/psum | solution.py:34
  9.6 48.9 %all-to-all-start = ((s32[32,1,8]{2,1,0:T(1,128)}), s32[32,1,8]{2,1,0:T(1,128)S(1)}, u32[]{:S(2)}, u32[]{:S(2)}) async-start(s32[32,1,8]{2,1,0:T(1,128)} %bitcast.1), calls=%async_computation | async-start | bytes 32768 | tf_op jit(solution)/shard_map/all_to_all | solution.py:67
  29.3 6.6 %copy-start.2 = (bf16[1024,2,256]{2,1,0:T(2,128)(2,1)S(1)}, bf16[1024,2,256]{2,1,0:T(2,128)(2,1)}, u32[]{:S(2)}) copy-start(bf16[1024,2,256]{2,1,0:T(2,128)(2,1)} %param.15) | copy-start | bytes 3145732
  48.3 6.6 %copy-start.3 = (bf16[64,8192]{1,0:T(8,128)(2,1)S(1)}, bf16[64,8192]{1,0:T(8,128)(2,1)}, u32[]{:S(2)}) copy-start(bf16[64,8192]{1,0:T(8,128)(2,1)} %param.11) | copy-start | bytes 3145732
  54.9 13.5 %copy-start.4 = (s32[8]{0:T(128)S(1)}, s32[8]{0:T(128)}, u32[]{:S(2)}) copy-start(s32[8]{0:T(128)} %param.19) | copy-start | bytes 100
  58.4 28.9 %all-to-all-start.1 = ((bf16[32,8,2048]{2,1,0:T(8,128)(2,1)}), bf16[32,8,2048]{2,1,0:T(8,128)(2,1)}, u32[]{:S(2)}, u32[]{:S(2)}) async-start(bf16[32,8,2048]{2,1,0:T(8,128)(2,1)} %fusion.2), calls=%async_computation.1 | async-start | bytes 2097152 | tf_op jit(solution)/shard_map/all_to_all | solution.py:66
  102.8 14.8 %all-to-all-start.2 = ((bf16[32,8,512]{2,1,0:T(8,128)(2,1)}), bf16[32,8,512]{2,1,0:T(8,128)(2,1)S(1)}, u32[]{:S(2)}, u32[]{:S(2)}) async-start(bf16[32,8,512]{2,1,0:T(8,128)(2,1)} %fusion.11), calls=%async_computation.2 | async-start | bytes 524288 | tf_op jit(solution)/shard_map/all_to_all | solution.py:83
  118.5 3.7 %copy-start.1 = (bf16[8,1,1024,256]{2,3,0,1:T(8,128)(2,1)S(1)}, bf16[8,1,1024,256]{2,3,0,1:T(8,128)(2,1)}, u32[]{:S(2)}) copy-start(bf16[8,1,1024,256]{2,3,0,1:T(8,128)(2,1)} %copy.48) | copy-start | bytes 12582916
Sparse Core Ops, SparseCore 0:
  10.5 43.8 all-reduce.1
where the time goes:
time: 135 us; the launch traced here: 134 us
  local copies, waits for them, and re-layouts  37.2 us (28%)
  starting transfers between devices  24.9 us (18%)
  matrix products  20.9 us (15%)
  waiting for transfers between devices  18.3 us (14%)
  between operations  14.2 us (11%)
  blocking collectives  10.4 us (8%)
  other arithmetic  7.93 us (6%)
    unnamed x15, local copies, waits for them, and re-layouts  27.9 us
    all_to_all x1, waiting for transfers between devices, per_device(): lax.all_to_all(send_rows, 'adapter', split_axis=0, concat_axis=0, tiled=T...  12.5 us
    all_to_all x1, starting transfers between devices, per_device(): lax.all_to_all(send_ids, 'adapter', split_axis=0, concat_axis=0, tiled=True)  10.9 us
    psum x1, blocking collectives, per_device(): reduced_rank_rows = lax.psum(partial_low.astype(jnp.bfloat16), 'tensor')  10.4 us
    all_to_all x1, starting transfers between devices, per_device(): lax.all_to_all(send_rows, 'adapter', split_axis=0, concat_axis=0, tiled=T...  9.94 us
    slice x1, local copies, waits for them, and re-layouts, per_device(): key_value_cache[:, 0]  5.73 us
    all_to_all x1, waiting for transfers between devices, per_device(): lax.all_to_all(adapter_update, 'adapter', split_axis=0, concat_axis=0, ti...  5.07 us
    dot_general x1, matrix products, per_device(): jnp.einsum('pfkgd,pckd->pfkgc', query_heads, cache_keys, preferred_elemen...  5.04 us
  transfers between devices with their start and end apart: 4, of which 2 were waited for; matrix products, arithmetic and copies ran while one was open for 39% of the time, Pallas kernels for 0%

commit v1 on v0

--- a/solution.py
+++ b/solution.py
@@ -10,6 +10,11 @@
 
 EPSILON = 1e-05
 ADAPTER_SCALE = 0.5
+ID_LANES = 128
+
+
+def _swap(x, mask, count):
+    return lax.ppermute(x, "tensor", perm=[(i, i ^ mask) for i in range(count)])
 
 
 def per_device(
@@ -29,18 +34,36 @@
     tensor_count = lax.axis_size("tensor")
     quarter = model_width // tensor_count
     tensor_index = lax.axis_index("tensor")
+    core = tensor_index % 2
+    chip_x = tensor_index // 2
     flat_weight = key_value_weight.reshape(model_width, -1)
-    partial_own = partials[0].astype(jnp.float32)
-    summed = lax.psum(partial_own.astype(jnp.bfloat16), "tensor").astype(jnp.float32)
-    hidden_full = (residual.astype(jnp.float32) + summed).astype(jnp.bfloat16)
+
+    part4 = partials[0].reshape(row_dev, 2, 2, quarter)
+    res4 = residual.reshape(row_dev, 2, 2, quarter)
+    mine_p = lax.dynamic_index_in_dim(part4, core, axis=2, keepdims=False)
+    other_p = lax.dynamic_index_in_dim(part4, 1 - core, axis=2, keepdims=False)
+    got_p = _swap(other_p, 1, tensor_count)
+    chip_sum = mine_p.astype(jnp.float32) + got_p.astype(jnp.float32)
+    far_sum = _swap(chip_sum.astype(jnp.bfloat16), 2, tensor_count)
+    res_half = lax.dynamic_index_in_dim(res4, core, axis=2, keepdims=False)
+    hidden_half = (
+        res_half.astype(jnp.float32) + (chip_sum + far_sum.astype(jnp.float32))
+    ).astype(jnp.bfloat16)
+    hidden_part = lax.dynamic_index_in_dim(hidden_half, chip_x, axis=1, keepdims=False)
+    hidden_other = _swap(hidden_half, 1, tensor_count)
+    first = core == 0
+    half0 = jnp.where(first, hidden_half, hidden_other)
+    half1 = jnp.where(first, hidden_other, hidden_half)
+    hidden_full = jnp.stack([half0, half1], axis=2).reshape(row_dev, model_width)
+
     hidden_wide = hidden_full.astype(jnp.float32)
     mean_sq = jnp.mean(hidden_wide * hidden_wide, axis=1, keepdims=True)
     normed_full = (
         hidden_wide * lax.rsqrt(mean_sq + EPSILON) * attention_norm_gain.astype(jnp.float32)
     ).astype(jnp.bfloat16)
-    hidden_part = lax.dynamic_slice_in_dim(hidden_full, tensor_index * quarter, quarter, 1)
     normed_part = lax.dynamic_slice_in_dim(normed_full, tensor_index * quarter, quarter, 1)
     base_kv = jnp.dot(normed_full, flat_weight, preferred_element_type=jnp.float32)
+
     adapt_count = lax.axis_size("adapter")
     capacity = max(2, 4 * row_dev // adapt_count)
     slot_count = adapt_count * capacity
@@ -54,25 +77,27 @@
     row_slot = owner_index * capacity + slot_rank
     row_to_slot = jnp.arange(slot_count)[:, None] == row_slot[None, :]
     slot_matrix = row_to_slot.astype(jnp.bfloat16)
-    send_rows = (
-        jnp.dot(slot_matrix, normed_part, preferred_element_type=jnp.float32)
-        .astype(jnp.bfloat16)
-        .reshape(adapt_count, capacity, quarter)
+    send_rows = jnp.dot(slot_matrix, normed_part, preferred_element_type=jnp.float32).astype(
+        jnp.bfloat16
     )
-    send_ids = (jnp.sum(jnp.where(row_to_slot, local_id[None, :] + 1, 0), axis=1) - 1).reshape(
-        adapt_count, capacity
+    send_ids = jnp.sum(jnp.where(row_to_slot, local_id[None, :] + 1, 0), axis=1) - 1
+    id_block = jnp.broadcast_to(send_ids.astype(jnp.bfloat16)[:, None], (slot_count, ID_LANES))
+    payload = jnp.concatenate([send_rows, id_block], axis=1).reshape(
+        adapt_count, capacity, quarter + ID_LANES
     )
     flattened_up = adapter_up_weight.reshape(adapter_grouped * ADAPTER_RANK, -1)
-    rows_in = lax.all_to_all(send_rows, "adapter", split_axis=0, concat_axis=0, tiled=True)
-    ids_in = lax.all_to_all(send_ids, "adapter", split_axis=0, concat_axis=0, tiled=True)
+    rows_in = lax.all_to_all(payload, "adapter", split_axis=0, concat_axis=0, tiled=True)
     item_count = rows_in.shape[1]
-    flattened_rows = rows_in.reshape(-1, rows_in.shape[2])
-    adapter_pick = ids_in.reshape(-1)[:, None] == jnp.arange(adapter_grouped)[None, :]
+    rows_in = rows_in.reshape(slot_count, quarter + ID_LANES)
+    flattened_rows = rows_in[:, :quarter]
+    ids_in = rows_in[:, quarter].astype(jnp.int32)
+    adapter_pick = ids_in[:, None] == jnp.arange(adapter_grouped)[None, :]
     projected_rows = jnp.dot(
         flattened_rows, adapter_down_weight, preferred_element_type=jnp.float32
     ).reshape(-1, adapter_grouped, ADAPTER_RANK)
     partial_low = jnp.sum(jnp.where(adapter_pick[:, :, None], projected_rows, 0.0), axis=1)
-    reduced_rank_rows = lax.psum(partial_low.astype(jnp.bfloat16), "tensor")
+    pair_low = partial_low + _swap(partial_low, 1, tensor_count)
+    reduced_rank_rows = (pair_low + _swap(pair_low, 2, tensor_count)).astype(jnp.bfloat16)
     expanded_rows = jnp.where(
         adapter_pick[:, :, None], reduced_rank_rows[:, None, :], jnp.zeros((), jnp.bfloat16)
     ).reshape(-1, adapter_grouped * ADAPTER_RANK)
@@ -89,6 +114,7 @@
     new_kv = (
         (base_kv + update_rows).astype(jnp.bfloat16).reshape(row_dev, local_heads, 2 * HEAD_SIZE)
     )
+
     local_prompts = key_value_cache.shape[0]
     cache_length = key_value_cache.shape[2]
     group_size = queries.shape[1] // (local_heads * HEAD_SIZE)
@@ -104,6 +130,13 @@
     )
     valid_mask = jnp.arange(cache_length)[None, :] < prompt_cache_length[:, None]
     scores = jnp.where(valid_mask[:, None, None, None, :], scores, -jnp.inf)
+    cache_top = jnp.max(scores, axis=-1)
+    weights = jnp.exp(scores - cache_top[..., None]).astype(jnp.bfloat16)
+    cache_total = jnp.sum(weights, axis=-1, dtype=jnp.float32)
+    cache_weighted = jnp.einsum(
+        "pfkgc,pckd->pfkgd", weights, cache_values, preferred_element_type=jnp.float32
+    )
+
     new_heads = new_kv.reshape(local_prompts, FAN, local_heads, 2 * HEAD_SIZE)
     own_key = new_heads[:, :, :, :HEAD_SIZE]
     own_value = new_heads[:, :, :, HEAD_SIZE:]
@@ -111,17 +144,15 @@
         jnp.einsum("pfkgd,pfkd->pfkg", query_heads, own_key, preferred_element_type=jnp.float32)
         * score_scale
     )
-    score_top = jnp.maximum(jnp.max(scores, axis=-1), own_score)
-    weights = jnp.exp(scores - score_top[:, :, :, :, None]).astype(jnp.bfloat16)
+    score_top = jnp.maximum(cache_top, own_score)
+    rescale = jnp.exp(cache_top - score_top)
     own_weight = jnp.exp(own_score - score_top).astype(jnp.bfloat16).astype(jnp.float32)
-    weight_total = jnp.sum(weights, axis=-1, dtype=jnp.float32) + own_weight
-    weighted = jnp.einsum(
-        "pfkgc,pckd->pfkgd", weights, cache_values, preferred_element_type=jnp.float32
+    weight_total = rescale * cache_total + own_weight
+    weighted = (
+        rescale[..., None] * cache_weighted
+        + own_weight[..., None] * own_value.astype(jnp.float32)[:, :, :, None, :]
     )
-    weighted = (
-        weighted + own_weight[:, :, :, :, None] * own_value.astype(jnp.float32)[:, :, :, None, :]
-    )
-    attended = (weighted / weight_total[:, :, :, :, None]).astype(jnp.bfloat16).reshape(row_dev, -1)
+    attended = (weighted / weight_total[..., None]).astype(jnp.bfloat16).reshape(row_dev, -1)
     return (hidden_part, new_kv, attended)
 
 

time: 135 us -> 122 us (0.904)
  between operations: 14.2 us -> 1.02 us
  blocking collectives: 10.4 us -> 0 us
  local copies, waits for them, and re-layouts: 37.2 us -> 47.2 us
    ppermute x0 -> x5, waiting for transfers between devices: none -> 13.1 us  [_swap(): return lax.ppermute(x, 'tensor', perm=[(i, i ^ mask) for i in range(count)])]
    all_to_all x2 -> x1, waiting for transfers between devices: 12.5 us -> 0.01 us  [per_device(): lax.all_to_all(payload, 'adapter', split_axis=0, concat_axis=0, tiled=True)]
    psum x1 -> x0, blocking collectives: 10.4 us -> none  [per_device(): reduced_rank_rows = lax.psum(partial_low.astype(jnp.bfloat16), 'tensor')]
    all_to_all x2 -> x1, starting transfers between devices: 20.8 us -> 11.1 us  [per_device(): lax.all_to_all(payload, 'adapter', split_axis=0, concat_axis=0, tiled=True)]
    convert_element_type x1 -> x5, local copies, waits for them, and re-layouts: 0.04 us -> 6.43 us  [the longest x2 4.47 us: per_device(): hidden_wide = hidden_full.astype(jnp.float32)]
    all_to_all x1, starting transfers between devices: 4.05 us -> 10 us  [per_device(): lax.all_to_all(adapter_update, 'adapter', split_axis=0, concat_axis=0, ti...]
    dynamic_slice x1 -> x4, local copies, waits for them, and re-layouts: 0.73 us -> 4.57 us  [the longest x1 2.74 us: per_device(): mine_p = lax.dynamic_index_in_dim(part4, core, axis=2, keepdims=False)]
    unnamed x15 -> x24, local copies, waits for them, and re-layouts: 27.9 us -> 24.3 us
  transfers between devices with their start and end apart: 4 -> 7, of which waited for: 2 -> 5; matrix products, arithmetic and copies ran while one was open for 39% -> 36% of each run, Pallas kernels for 0% -> 0%
where the time goes in v1:
time: 122 us; the launch traced here: 121 us
  local copies, waits for them, and re-layouts  47.2 us (39%)
  starting transfers between devices  23.7 us (19%)
  matrix products  21.8 us (18%)
  waiting for transfers between devices  18.9 us (15%)
  other arithmetic  8.27 us (7%)
    unnamed x24, local copies, waits for them, and re-layouts  24.3 us
    ppermute x5, waiting for transfers between devices, _swap(): return lax.ppermute(x, 'tensor', perm=[(i, i ^ mask) for i in range(count)])  13.1 us
    all_to_all x1, starting transfers between devices, per_device(): lax.all_to_all(payload, 'adapter', split_axis=0, concat_axis=0, tiled=True)  11.1 us
    all_to_all x1, starting transfers between devices, per_device(): lax.all_to_all(adapter_update, 'adapter', split_axis=0, concat_axis=0, ti...  10 us
    slice x1, local copies, waits for them, and re-layouts, per_device(): key_value_cache[:, 0]  5.86 us
    all_to_all x1, waiting for transfers between devices, per_device(): lax.all_to_all(adapter_update, 'adapter', split_axis=0, concat_axis=0, ti...  5.76 us
    dot_general x1, matrix products, per_device(): jnp.einsum('pfkgc,pckd->pfkgd', weights, cache_values, preferred_element_...  5.23 us
    dot_general x1, matrix products, per_device(): jnp.dot(normed_full, flat_weight, preferred_element_type=jnp.float32)  4.93 us
  transfers between devices with their start and end apart: 7, of which 5 were waited for; matrix products, arithmetic and copies ran while one was open for 36% of the time, Pallas kernels for 0%

profile of v1, /device:TPU:0, one launch (start us, length us, event | category | flops | bytes accessed | tf_op | source)
XLA Modules:
  0.0 120.8 jit_solution(16505975140981573239)
XLA Ops:
  0.7 1.9 %reshape_squeeze.9 = bf16[64,2,2,2048]{3,2,1,0:T(2,128)(2,1)S(1)} reshape(bf16[1,64,8192]{2,1,0:T(8,128)(2,1)} %param.10) | data formatting | bytes 2097152 | tf_op jit(solution)/shard_map/reshape;squeeze | solution.py:41
  2.6 2.7 %constant_dynamic-slice_fusion.1 = (bf16[64,2,1,2048]{3,2,1,0:T(2,128)(2,1)S(1)}, bf16[64,2,1,2048]{3,2,1,0:T(2,128)(2,1)S(1)}) fusion(bf16[64,2,2,2048]{3,2,1,0:T(2,128)(2,1)S(1)} %reshape_squeeze.9, s32[]{:T(128)S(6)} %select_n.79, s32[]{:T(128)S(6)} %select_n.80), kind=kLoop, calls=%fused_computation.71 | loop fusion | bytes 2097160 | tf_op jit(solution)/shard_map/jit(dynamic_index_in_dim)/dynamic_slice | solution.py:43
  6.2 1.7 %collective-permute-done = bf16[64,2,2048]{2,0,1:T(8,128)(2,1)S(1)} collective-permute-done((bf16[64,2,2048]{2,0,1:T(8,128)(2,1)S(1)}, bf16[64,2,2048]{2,0,1:T(8,128)(2,1)S(1)}, u32[]{:S(2)}, u32[]{:S(2)}) %collective-permute-start) | collective-permute-done | bytes 524320 | tf_op jit(solution)/shard_map/ppermute | solution.py:17
  7.9 1.4 %fusion.12 = bf16[64,2,2048]{2,0,1:T(8,128)(2,1)} fusion(bf16[64,2,2048]{2,0,1:T(8,128)(2,1)S(1)} %collective-permute-done, bf16[64,2,1,2048]{3,2,1,0:T(2,128)(2,1)S(1)} %get-tuple-element.10), kind=kLoop, calls=%fused_computation.27 | loop fusion | flops 1048576 | bytes 1572864 | tf_op jit(solution)/shard_map/convert_element_type | solution.py:47
  9.3 1.6 %collective-permute-start.1 = (bf16[64,2,2048]{2,0,1:T(8,128)(2,1)}, bf16[64,2,2048]{2,0,1:T(8,128)(2,1)S(1)}, u32[]{:S(2)}, u32[]{:S(2)}) collective-permute-start(bf16[64,2,2048]{2,0,1:T(8,128)(2,1)} %fusion.12), channel_id=1, source_target_pairs={{0,2},{1,3},{2,0},{3,1},{4,6},{5,7},{6,4},{7,5},{8,10},{9,11},{10,... | collective-permute-start | bytes 1572872 | tf_op jit(solution)/shard_map/ppermute | solution.py:17
  11.0 1.8 %reshape.173 = bf16[64,2,2,2048]{3,2,1,0:T(2,128)(2,1)S(1)} reshape(bf16[64,8192]{1,0:T(8,128)(2,1)} %param.11) | data formatting | bytes 2097152 | tf_op jit(solution)/shard_map/reshape | solution.py:42
  12.8 1.3 %constant_dynamic-slice_fusion.2 = bf16[64,2,1,2048]{3,2,1,0:T(2,128)(2,1)S(1)} fusion(bf16[64,2,2,2048]{3,2,1,0:T(2,128)(2,1)S(1)} %reshape.173, s32[]{:T(128)S(6)} %select_n.79), kind=kLoop, calls=%fused_computation.72 | loop fusion | bytes 1048580 | tf_op jit(solution)/shard_map/jit(dynamic_index_in_dim)/dynamic_slice | solution.py:48
  14.1 9.3 %collective-permute-done.1 = bf16[64,2,2048]{2,0,1:T(8,128)(2,1)S(1)} collective-permute-done((bf16[64,2,2048]{2,0,1:T(8,128)(2,1)}, bf16[64,2,2048]{2,0,1:T(8,128)(2,1)S(1)}, u32[]{:S(2)}, u32[]{:S(2)}) %collective-permute-start.1) | collective-permute-done | bytes 524320 | tf_op jit(solution)/shard_map/ppermute | solution.py:17
  23.4 1.7 %fusion.11 = bf16[64,2,2048]{2,0,1:T(8,128)(2,1)S(1)} fusion(bf16[64,2,2048]{2,0,1:T(8,128)(2,1)S(1)} %collective-permute-done.1, bf16[64,2,2048]{2,0,1:T(8,128)(2,1)S(1)} %collective-permute-done, bf16[64,2,1,2048]{3,2,1,0:T(2,128)(2,1)S(1)} %constant_dynamic-slice_fusion.2, bf16[64,2,1,2048]{3,2,1,0:T(2,128)(2,1)S(1)} %get-tuple-element.10), kind=kLoop, calls=%fused_computation.25 | loop fusion | flops 2097152 | bytes 2621440 | tf_op jit(solution)/shard_map/convert_element_type | solution.py:51
  25.3 5.9 %fusion.38 = (bf16[8,1,1024,256]{3,2,1,0:T(8,128)(2,1)}, bf16[8,1,1024,256]{3,2,1,0:T(8,128)(2,1)}) fusion(bf16[8,2,1024,256]{3,2,1,0:T(8,128)(2,1)} %param.18), kind=kLoop, calls=%fused_computation.82 | loop fusion | bytes 16777216 | tf_op jit(solution)/shard_map/slice | solution.py:123
  31.7 1.6 %copy.73 = f32[64,2,2,2048]{3,2,1,0:T(2,128)S(1)} copy(f32[64,2,2,2048]{3,0,2,1:T(8,128)S(1)} %maximum_convert_fusion) | data formatting | bytes 4194304 | tf_op jit(solution)/shard_map/convert_element_type | solution.py:59
  33.3 2.9 %reshape.186 = f32[64,8192]{1,0:T(8,128)} reshape(f32[64,2,2,2048]{3,2,1,0:T(2,128)S(1)} %copy.73) | data formatting | bytes 4194304 | tf_op jit(solution)/shard_map/convert_element_type | solution.py:59
  36.2 1.6 %convolution_convert_fusion = bf16[256,2048]{1,0:T(8,128)(2,1)S(1)} fusion(f32[64,8192]{1,0:T(8,128)} %reshape.186, s32[]{:T(128)S(6)} %select_n.87, f32[2048]{0:T(1024)S(1)} %dynamic-slice, f32[64]{0:T(128)S(1)} %add_rsqrt_fusion, s32[64]{0:T(128)S(1)} %multiply_add_fusion.1), kind=kOutput, calls=%fused_computation.6 | convolution fusion | flops 68042752 | bytes 1581572 | tf_op jit(solution)/shard_map/dot_general | solution.py:80
  37.9 1.1 maximum_bitcast_fusion
  39.0 11.1 %all-to-all-start = ((bf16[32,8,2176]{2,1,0:T(8,128)(2,1)}), bf16[32,8,2176]{2,1,0:T(8,128)(2,1)S(1)}, u32[]{:S(2)}, u32[]{:S(2)}) async-start(bf16[32,8,2176]{2,1,0:T(8,128)(2,1)} %maximum_bitcast_fusion), calls=%async_computation | async-start | bytes 2228224 | tf_op jit(solution)/shard_map/all_to_all | solution.py:89
  50.2 8.1 %copy.95 = bf16[1024,8,2,256]{3,1,2,0:T(8,128)(2,1)} copy(bf16[1024,8,2,256]{3,2,1,0:T(2,128)(2,1)} %bitcast.91) | data formatting | bytes 16777216
  58.3 1.2 %copy.96 = bf16[128,8,2,256]{3,1,2,0:T(8,128)(2,1)} copy(bf16[128,8,2,256]{3,2,1,0:T(2,128)(2,1)S(1)} %bitcast.96) | data formatting | bytes 2097152
  59.5 6.5 %copy.94 = bf16[8,1,1024,256]{2,3,0,1:T(8,128)(2,1)} copy(bf16[8,1,1024,256]{3,2,1,0:T(8,128)(2,1)} %get-tuple-element.7) | data formatting | bytes 8388608
  66.0 6.5 %copy.93 = bf16[8,1,1024,256]{2,3,0,1:T(8,128)(2,1)} copy(bf16[8,1,1024,256]{3,2,1,0:T(8,128)(2,1)} %get-tuple-element.6) | data formatting | bytes 8388608
  72.5 3.2 %bitcast_reduce_fusion = (f32[8,8,2,8]{3,1,2,0:T(8,128)S(1)}, f32[8,2,1024,8,8]{2,4,3,1,0:T(8,128)S(1)}) fusion(pred[8,1024]{1,0:T(8,128)(4,1)S(1)} %iota_compare_fusion.3, bf16[8,1024,2,128,1]{1,3,4,2,0:T(8,128)(2,1)} %bitcast.93, bf16[8,8,2,8,128]{4,1,3,2,0:T(8,128)(2,1)S(1)} %bitcast.88), kind=kOutput, calls=%fused_computation.1 | convolution fusion | flops 271580160 | bytes 8663040 | tf_op jit(solution)/shard_map/pfkgd,pckd->pfkgc/dot_general | solution.py:128
  75.7 1.9 %copy-done.1 = f32[8,2,1024,8,8]{2,4,3,1,0:T(8,128)} copy-done((f32[8,2,1024,8,8]{2,4,3,1,0:T(8,128)}, f32[8,2,1024,8,8]{2,4,3,1,0:T(8,128)S(1)}, u32[]{:S(2)}) %copy-start.1) | copy-done | bytes 4194328
  77.6 1.1 convert_reduce_fusion
  78.8 4.0 %fusion.9 = f32[256,1024]{0,1:T(8,128)S(1)} fusion(bf16[2048,1024]{1,0:T(8,128)(2,1)} %param.14, bf16[256,2176]{1,0:T(8,128)(2,1)S(1)} %bitcast.95), kind=kOutput, calls=%fused_computation.20 | convolution fusion | flops 1073741824 | bytes 6291456 | tf_op jit(solution)/shard_map/dot_general | solution.py:95
  85.8 1.1 copy.72
  86.9 0.8 convert_element_type.115
  87.8 1.7 %collective-permute-done.4 = f32[256,64]{0,1:T(8,128)} collective-permute-done((f32[256,64]{0,1:T(8,128)}, f32[256,64]{0,1:T(8,128)}, u32[]{:S(2)}, u32[]{:S(2)}) %collective-permute-start.4) | collective-permute-done | bytes 65568 | tf_op jit(solution)/shard_map/ppermute | solution.py:17
  89.5 0.9 add_convert_fusion
  90.4 2.4 %fusion.7 = bf16[32,8,512]{2,1,0:T(8,128)(2,1)} fusion(bf16[256,1024]{0,1:T(8,128)(2,1)S(1)} %bitcast.101, bf16[1024,512]{1,0:T(8,128)(2,1)} %bitcast.97), kind=kOutput, calls=%fused_computation.16 | convolution fusion | flops 268697600 | bytes 1835008 | tf_op jit(solution)/shard_map/dot_general | solution.py:105
  92.8 10.0 %all-to-all-start.1 = ((bf16[32,8,512]{2,1,0:T(8,128)(2,1)}), bf16[32,8,512]{2,1,0:T(8,128)(2,1)S(1)}, u32[]{:S(2)}, u32[]{:S(2)}) async-start(bf16[32,8,512]{2,1,0:T(8,128)(2,1)} %fusion.7), calls=%async_computation.1 | async-start | bytes 524288 | tf_op jit(solution)/shard_map/all_to_all | solution.py:108
  102.8 4.9 %fusion.39 = f32[64,512]{1,0:T(8,128)S(1)} fusion(bf16[64,8192]{1,0:T(8,128)(2,1)S(1)} %convert_element_type.115, bf16[8192,512]{1,0:T(8,128)(2,1)} %bitcast.90), kind=kOutput, calls=%fused_computation.83 | convolution fusion | flops 536870912 | bytes 9568256 | tf_op jit(solution)/shard_map/dot_general | solution.py:65
  107.8 5.8 %all-to-all-done.1 = bf16[32,8,512]{2,1,0:T(8,128)(2,1)S(1)} async-done(((bf16[32,8,512]{2,1,0:T(8,128)(2,1)}), bf16[32,8,512]{2,1,0:T(8,128)(2,1)S(1)}, u32[]{:S(2)}, u32[]{:S(2)}) %all-to-all-start.1) | async-done | bytes 262176 | tf_op jit(solution)/shard_map/all_to_all | solution.py:108
  114.7 5.2 %fusion.6 = bf16[8,8,2,8,128]{4,3,1,2,0:T(8,128)(2,1)S(1)} fusion(bf16[8,1024,2,128,1]{1,3,4,2,0:T(8,128)(2,1)} %bitcast.92, f32[8,8,2,8]{3,1,2,0:T(8,128)S(1)} %get-tuple-element.3, f32[8,8,2,128]{3,1,2,0:T(8,128)S(1)} %get-tuple-element.12, f32[8,8,2,8]{3,1,2,0:T(8,128)S(1)} %get-tuple-element.5, f32[8,8,2,8]{3,1,2,0:T(8,128)S(1)} %get-tuple-element.4, ...), kind=kOutput, calls=%fused_computation.15 | convolution fusion | flops 273285120 | bytes 8740864 | tf_op jit(solution)/shard_map/pfkgc,pckd->pfkgd/dot_general | solution.py:136
  (54 shorter events, 7.0 us)
Async XLA Ops:
  0.6 71.9 %copy-start = (bf16[64,2048]{1,0:T(8,128)(2,1)S(1)}, bf16[64,2048]{1,0:T(8,128)(2,1)}, u32[]{:S(2)}) copy-start(bf16[64,2048]{1,0:T(8,128)(2,1)} %param.17) | copy-start | bytes 786436
  0.6 5.3 %copy-start.9 = (s32[64]{0:T(128)S(1)}, s32[64]{0:T(128)}, u32[]{:S(2)}) copy-start(s32[64]{0:T(128)} %param.16) | copy-start | bytes 772
  2.6 10.2 %copy-start.5 = (bf16[8192]{0:T(1024)(128)(2,1)S(1)}, bf16[8192]{0:T(1024)(128)(2,1)}, u32[]{:S(2)}) copy-start(bf16[8192]{0:T(1024)(128)(2,1)} %param.12) | copy-start | bytes 49156
  5.9 2.0 %collective-permute-start = (bf16[64,2,2048]{2,0,1:T(8,128)(2,1)S(1)}, bf16[64,2,2048]{2,0,1:T(8,128)(2,1)S(1)}, u32[]{:S(2)}, u32[]{:S(2)}) collective-permute-start(bf16[64,2,2048]{2,0,1:T(8,128)(2,1)S(1)} %bitcast.100), channel_id=1, source_target_pairs={{0,1},{1,0},{2,3},{3,2},{4,5},{5,4},{6,7},{7,6},{8,9},{9,8},{10,11... | collective-permute-start | bytes 1572872 | tf_op jit(solution)/shard_map/ppermute | solution.py:17
  9.3 14.2 %collective-permute-start.1 = (bf16[64,2,2048]{2,0,1:T(8,128)(2,1)}, bf16[64,2,2048]{2,0,1:T(8,128)(2,1)S(1)}, u32[]{:S(2)}, u32[]{:S(2)}) collective-permute-start(bf16[64,2,2048]{2,0,1:T(8,128)(2,1)} %fusion.12), channel_id=1, source_target_pairs={{0,2},{1,3},{2,0},{3,1},{4,6},{5,7},{6,4},{7,5},{8,10},{9,11},{10,... | collective-permute-start | bytes 1572872 | tf_op jit(solution)/shard_map/ppermute | solution.py:17
  25.2 6.0 %copy-start.2 = (bf16[64,2,2048]{2,0,1:T(8,128)(2,1)}, bf16[64,2,2048]{2,0,1:T(8,128)(2,1)S(1)}, u32[]{:S(2)}) copy-start(bf16[64,2,2048]{2,0,1:T(8,128)(2,1)S(1)} %fusion.11) | copy-start | bytes 1572868
  25.2 6.0 %collective-permute-start.2 = (bf16[64,2,2048]{2,0,1:T(8,128)(2,1)S(1)}, bf16[64,2,2048]{2,0,1:T(8,128)(2,1)S(1)}, u32[]{:S(2)}, u32[]{:S(2)}) collective-permute-start(bf16[64,2,2048]{2,0,1:T(8,128)(2,1)S(1)} %fusion.11), channel_id=1, source_target_pairs={{0,1},{1,0},{2,3},{3,2},{4,5},{5,4},{6,7},{7,6},{8,9},{9,8},{10,11... | collective-permute-start | bytes 1572872 | tf_op jit(solution)/shard_map/ppermute | solution.py:17
  31.7 4.5 %copy-start.6 = (f32[64]{0:T(128)}, f32[64]{0:T(128)S(1)}, u32[]{:S(2)}) copy-start(f32[64]{0:T(128)S(1)} %add_rsqrt_fusion) | copy-start | bytes 772
  33.3 16.7 %copy-start.8 = (s32[8]{0:T(128)S(1)}, s32[8]{0:T(128)}, u32[]{:S(2)}) copy-start(s32[8]{0:T(128)} %param.19) | copy-start | bytes 100
  39.0 39.7 %all-to-all-start = ((bf16[32,8,2176]{2,1,0:T(8,128)(2,1)}), bf16[32,8,2176]{2,1,0:T(8,128)(2,1)S(1)}, u32[]{:S(2)}, u32[]{:S(2)}) async-start(bf16[32,8,2176]{2,1,0:T(8,128)(2,1)} %maximum_bitcast_fusion), calls=%async_computation | async-start | bytes 2228224 | tf_op jit(solution)/shard_map/all_to_all | solution.py:89
  50.2 8.1 %copy-start.4 = (bf16[1024,2,256]{2,1,0:T(2,128)(2,1)S(1)}, bf16[1024,2,256]{2,1,0:T(2,128)(2,1)}, u32[]{:S(2)}) copy-start(bf16[1024,2,256]{2,1,0:T(2,128)(2,1)} %param.15) | copy-start | bytes 3145732
  75.7 1.9 %copy-start.1 = (f32[8,2,1024,8,8]{2,4,3,1,0:T(8,128)}, f32[8,2,1024,8,8]{2,4,3,1,0:T(8,128)S(1)}, u32[]{:S(2)}) copy-start(f32[8,2,1024,8,8]{2,4,3,1,0:T(8,128)S(1)} %get-tuple-element.17) | copy-start | bytes 12582916
  78.8 4.3 %copy-start.3 = (bf16[64,2,2048]{2,0,1:T(8,128)(2,1)S(1)}, bf16[64,2,2048]{2,0,1:T(8,128)(2,1)}, u32[]{:S(2)}) copy-start(bf16[64,2,2048]{2,0,1:T(8,128)(2,1)} %copy-done.2) | copy-start | bytes 1572868
  78.8 6.7 %copy-start.7 = (f32[64]{0:T(128)S(1)}, f32[64]{0:T(128)}, u32[]{:S(2)}) copy-start(f32[64]{0:T(128)} %copy-done.6) | copy-start | bytes 772
  82.9 1.3 %collective-permute-start.3 = (f32[256,64]{0,1:T(8,128)S(1)}, f32[256,64]{0,1:T(8,128)S(1)}, u32[]{:S(2)}, u32[]{:S(2)}) collective-permute-start(f32[256,64]{0,1:T(8,128)S(1)} %select_reduce_fusion), channel_id=1, source_target_pairs={{0,1},{1,0},{2,3},{3,2},{4,5},{5,4},{6,7},{7,6},{8,9},{9,8},{10,11... | collective-permute-start | bytes 196616 | tf_op jit(solution)/shard_map/ppermute | solution.py:17
  84.9 4.6 %collective-permute-start.4 = (f32[256,64]{0,1:T(8,128)}, f32[256,64]{0,1:T(8,128)}, u32[]{:S(2)}, u32[]{:S(2)}) collective-permute-start(f32[256,64]{0,1:T(8,128)} %add.89), channel_id=1, source_target_pairs={{0,2},{1,3},{2,0},{3,1},{4,6},{5,7},{6,4},{7,5},{8,10},{9,11},{10,... | collective-permute-start | bytes 196616 | tf_op jit(solution)/shard_map/ppermute | solution.py:17
  92.8 20.7 %all-to-all-start.1 = ((bf16[32,8,512]{2,1,0:T(8,128)(2,1)}), bf16[32,8,512]{2,1,0:T(8,128)(2,1)S(1)}, u32[]{:S(2)}, u32[]{:S(2)}) async-start(bf16[32,8,512]{2,1,0:T(8,128)(2,1)} %fusion.7), calls=%async_computation.1 | async-start | bytes 524288 | tf_op jit(solution)/shard_map/all_to_all | solution.py:108

commit v2 on v1

--- a/solution.py
+++ b/solution.py
@@ -1,6 +1,10 @@
+import functools
+
 import jax
 import jax.numpy as jnp
 from jax import lax
+from jax.experimental import pallas as pl
+from jax.experimental.pallas import tpu as pltpu
 from jax.sharding import PartitionSpec as P
 
 HEAD_SIZE = 128
@@ -11,6 +15,51 @@
 EPSILON = 1e-05
 ADAPTER_SCALE = 0.5
 ID_LANES = 128
+
+
+def _attn_kernel(len_ref, q_ref, k_ref, v_ref, num_ref, top_ref, tot_ref, *, group, scale):
+    p = pl.program_id(0)
+    length = len_ref[p]
+    q = q_ref[...]
+    fan = q.shape[0]
+    qs = jnp.concatenate([q[:, g * HEAD_SIZE:(g + 1) * HEAD_SIZE] for g in range(group)], axis=0)
+    kb = k_ref[0, 0]
+    s = lax.dot_general(qs, kb, (((1,), (1,)), ((), ())), preferred_element_type=jnp.float32) * scale
+    col = lax.broadcasted_iota(jnp.int32, s.shape, 1)
+    s = jnp.where(col < length, s, -jnp.inf)
+    m = jnp.max(s, axis=1, keepdims=True)
+    w = jnp.exp(s - m).astype(jnp.bfloat16)
+    tot = jnp.sum(w.astype(jnp.float32), axis=1, keepdims=True)
+    num = jnp.dot(w, v_ref[0, 0], preferred_element_type=jnp.float32)
+    num_ref[...] = jnp.concatenate([num[g * fan:(g + 1) * fan] for g in range(group)], axis=1)
+    top_ref[...] = jnp.concatenate(
+        [jnp.broadcast_to(m[g * fan:(g + 1) * fan], (fan, HEAD_SIZE)) for g in range(group)], axis=1)
+    tot_ref[...] = jnp.concatenate(
+        [jnp.broadcast_to(tot[g * fan:(g + 1) * fan], (fan, HEAD_SIZE)) for g in range(group)], axis=1)
+
+
+def cache_attention(queries, key_value_cache, prompt_cache_length, local_heads, fan):
+    prompts, _, cache_len, _ = key_value_cache.shape
+    rows, width = queries.shape
+    head_width = width // local_heads
+    group = head_width // HEAD_SIZE
+    kernel = functools.partial(_attn_kernel, group=group, scale=HEAD_SIZE ** (-0.5))
+    out = jax.ShapeDtypeStruct((rows, width), jnp.float32)
+    spec_q = pl.BlockSpec((fan, head_width), lambda p, k, lens: (p, k))
+    return pl.pallas_call(
+        kernel,
+        out_shape=(out, out, out),
+        grid_spec=pltpu.PrefetchScalarGridSpec(
+            num_scalar_prefetch=1,
+            grid=(prompts, local_heads),
+            in_specs=[
+                spec_q,
+                pl.BlockSpec((1, 1, cache_len, HEAD_SIZE), lambda p, k, lens: (p, 0, 0, k)),
+                pl.BlockSpec((1, 1, cache_len, HEAD_SIZE), lambda p, k, lens: (p, 1, 0, k)),
+            ],
+            out_specs=[spec_q, spec_q, spec_q],
+        ),
+    )(prompt_cache_length, queries, key_value_cache, key_value_cache)
 
 
 def _swap(x, mask, count):
@@ -36,33 +85,55 @@
     tensor_index = lax.axis_index("tensor")
     core = tensor_index % 2
     chip_x = tensor_index // 2
-    flat_weight = key_value_weight.reshape(model_width, -1)
-
-    part4 = partials[0].reshape(row_dev, 2, 2, quarter)
-    res4 = residual.reshape(row_dev, 2, 2, quarter)
-    mine_p = lax.dynamic_index_in_dim(part4, core, axis=2, keepdims=False)
-    other_p = lax.dynamic_index_in_dim(part4, 1 - core, axis=2, keepdims=False)
+    local_heads = key_value_weight.shape[1]
+    head_weight = jnp.transpose(key_value_weight, (1, 0, 2))
+
+    half_rows = row_dev // 2
+    part2 = partials[0].reshape(2, half_rows, model_width)
+    mine_p = lax.dynamic_index_in_dim(part2, core, axis=0, keepdims=False)
+    other_p = lax.dynamic_index_in_dim(part2, 1 - core, axis=0, keepdims=False)
     got_p = _swap(other_p, 1, tensor_count)
     chip_sum = mine_p.astype(jnp.float32) + got_p.astype(jnp.float32)
     far_sum = _swap(chip_sum.astype(jnp.bfloat16), 2, tensor_count)
-    res_half = lax.dynamic_index_in_dim(res4, core, axis=2, keepdims=False)
+    attention_parts = cache_attention(
+        queries, key_value_cache, prompt_cache_length, local_heads, FAN
+    )
+    far_sum, head_weight, attention_parts = lax.optimization_barrier(
+        (far_sum, head_weight, attention_parts)
+    )
+    res_half = lax.dynamic_index_in_dim(
+        residual.reshape(2, half_rows, model_width), core, axis=0, keepdims=False
+    )
     hidden_half = (
         res_half.astype(jnp.float32) + (chip_sum + far_sum.astype(jnp.float32))
     ).astype(jnp.bfloat16)
-    hidden_part = lax.dynamic_index_in_dim(hidden_half, chip_x, axis=1, keepdims=False)
-    hidden_other = _swap(hidden_half, 1, tensor_count)
-    first = core == 0
-    half0 = jnp.where(first, hidden_half, hidden_other)
-    half1 = jnp.where(first, hidden_other, hidden_half)
-    hidden_full = jnp.stack([half0, half1], axis=2).reshape(row_dev, model_width)
-
-    hidden_wide = hidden_full.astype(jnp.float32)
+    hidden_wide = hidden_half.astype(jnp.float32)
     mean_sq = jnp.mean(hidden_wide * hidden_wide, axis=1, keepdims=True)
-    normed_full = (
+    normed_half = (
         hidden_wide * lax.rsqrt(mean_sq + EPSILON) * attention_norm_gain.astype(jnp.float32)
     ).astype(jnp.bfloat16)
+    partner_quarter = lax.dynamic_slice_in_dim(
+        hidden_half, (tensor_index ^ 1) * quarter, quarter, 1
+    )
+    swap_in = _swap(jnp.concatenate([normed_half, partner_quarter], axis=1), 1, tensor_count)
+    normed_other = swap_in[:, :model_width]
+    hidden_other = swap_in[:, model_width:]
+    hidden_mine = lax.dynamic_slice_in_dim(hidden_half, tensor_index * quarter, quarter, 1)
+    first = core == 0
+    hidden_part = jnp.where(
+        first,
+        jnp.concatenate([hidden_mine, hidden_other], axis=0),
+        jnp.concatenate([hidden_other, hidden_mine], axis=0),
+    )
+    normed_full = jnp.where(
+        first,
+        jnp.concatenate([normed_half, normed_other], axis=0),
+        jnp.concatenate([normed_other, normed_half], axis=0),
+    )
     normed_part = lax.dynamic_slice_in_dim(normed_full, tensor_index * quarter, quarter, 1)
-    base_kv = jnp.dot(normed_full, flat_weight, preferred_element_type=jnp.float32)
+    base_kv = jnp.einsum(
+        "rf,hfd->rhd", normed_full, head_weight, preferred_element_type=jnp.float32
+    ).reshape(row_dev, -1)
 
     adapt_count = lax.axis_size("adapter")
     capacity = max(2, 4 * row_dev // adapt_count)
@@ -97,7 +168,8 @@
     ).reshape(-1, adapter_grouped, ADAPTER_RANK)
     partial_low = jnp.sum(jnp.where(adapter_pick[:, :, None], projected_rows, 0.0), axis=1)
     pair_low = partial_low + _swap(partial_low, 1, tensor_count)
-    reduced_rank_rows = (pair_low + _swap(pair_low, 2, tensor_count)).astype(jnp.bfloat16)
+    far_low, base_kv = lax.optimization_barrier((_swap(pair_low, 2, tensor_count), base_kv))
+    reduced_rank_rows = (pair_low + far_low).astype(jnp.bfloat16)
     expanded_rows = jnp.where(
         adapter_pick[:, :, None], reduced_rank_rows[:, None, :], jnp.zeros((), jnp.bfloat16)
     ).reshape(-1, adapter_grouped * ADAPTER_RANK)
@@ -110,38 +182,23 @@
     update_rows = lax.dot_general(
         slot_matrix, returned, (((0,), (0,)), ((), ())), preferred_element_type=jnp.float32
     )
-    local_heads = key_value_weight.shape[1]
     new_kv = (
         (base_kv + update_rows).astype(jnp.bfloat16).reshape(row_dev, local_heads, 2 * HEAD_SIZE)
     )
 
     local_prompts = key_value_cache.shape[0]
-    cache_length = key_value_cache.shape[2]
     group_size = queries.shape[1] // (local_heads * HEAD_SIZE)
     score_scale = HEAD_SIZE ** (-0.5)
-    query_heads = queries.reshape(local_prompts, FAN, local_heads, group_size, HEAD_SIZE)
-    cache_keys = key_value_cache[:, 0].reshape(local_prompts, cache_length, local_heads, HEAD_SIZE)
-    cache_values = key_value_cache[:, 1].reshape(
-        local_prompts, cache_length, local_heads, HEAD_SIZE
-    )
-    scores = (
-        jnp.einsum("pfkgd,pckd->pfkgc", query_heads, cache_keys, preferred_element_type=jnp.float32)
-        * score_scale
-    )
-    valid_mask = jnp.arange(cache_length)[None, :] < prompt_cache_length[:, None]
-    scores = jnp.where(valid_mask[:, None, None, None, :], scores, -jnp.inf)
-    cache_top = jnp.max(scores, axis=-1)
-    weights = jnp.exp(scores - cache_top[..., None]).astype(jnp.bfloat16)
-    cache_total = jnp.sum(weights, axis=-1, dtype=jnp.float32)
-    cache_weighted = jnp.einsum(
-        "pfkgc,pckd->pfkgd", weights, cache_values, preferred_element_type=jnp.float32
-    )
-
-    new_heads = new_kv.reshape(local_prompts, FAN, local_heads, 2 * HEAD_SIZE)
-    own_key = new_heads[:, :, :, :HEAD_SIZE]
-    own_value = new_heads[:, :, :, HEAD_SIZE:]
+    num_c, top_c, tot_c = attention_parts
+    view = (row_dev, local_heads, group_size, HEAD_SIZE)
+    cache_weighted = num_c.reshape(view)
+    cache_top = top_c.reshape(view)[..., 0]
+    cache_total = tot_c.reshape(view)[..., 0]
+    query_heads = queries.reshape(view)
+    own_key = new_kv[:, :, :HEAD_SIZE]
+    own_value = new_kv[:, :, HEAD_SIZE:]
     own_score = (
-        jnp.einsum("pfkgd,pfkd->pfkg", query_heads, own_key, preferred_element_type=jnp.float32)
+        jnp.einsum("rkgd,rkd->rkg", query_heads, own_key, preferred_element_type=jnp.float32)
         * score_scale
     )
     score_top = jnp.maximum(cache_top, own_score)
@@ -150,7 +207,7 @@
     weight_total = rescale * cache_total + own_weight
     weighted = (
         rescale[..., None] * cache_weighted
-        + own_weight[..., None] * own_value.astype(jnp.float32)[:, :, :, None, :]
+        + own_weight[..., None] * own_value.astype(jnp.float32)[:, :, None, :]
     )
     attended = (weighted / weight_total[..., None]).astype(jnp.bfloat16).reshape(row_dev, -1)
     return (hidden_part, new_kv, attended)

time: 122 us -> 84.2 us (0.69)
  local copies, waits for them, and re-layouts: 47.2 us -> 3.12 us
  blocking collectives: 0 us -> 30.9 us
  starting transfers between devices: 23.7 us -> 6.11 us
  matrix products: 21.8 us -> 5.49 us
  Pallas kernels: 0 us -> 14.5 us
  waiting for transfers between devices: 18.9 us -> 16.4 us
  other arithmetic: 8.27 us -> 5.94 us
    all_to_all x0 -> x1, blocking collectives: none -> 30.9 us  [per_device(): lax.all_to_all(payload, 'adapter', split_axis=0, concat_axis=0, tiled=True)]
    unnamed x24 -> x30, local copies, waits for them, and re-layouts: 24.3 us -> 1.06 us
    pallas_call x0 -> x1, Pallas kernels: none -> 14.5 us  [cache_attention(): pl.pallas_call(kernel, out_shape=(out, out, out), grid_spec=pltpu.Prefetc...]
    dot_general x4 -> x2, matrix products: 13.6 us -> 1.84 us  [the longest x1 1.57 us: per_device(): jnp.einsum('rf,hfd->rhd', normed_full, head_weight, preferred_element_typ...]
    all_to_all x1 -> x0, starting transfers between devices: 11.1 us -> none  [per_device(): lax.all_to_all(payload, 'adapter', split_axis=0, concat_axis=0, tiled=True)]
    convert_element_type x5 -> x1, local copies, waits for them, and re-layouts: 6.43 us -> 0.1 us  [per_device(): jnp.exp(own_score - score_top).astype(jnp.bfloat16).astype(jnp.float32)]
    all_to_all x1, starting transfers between devices: 10 us -> 3.87 us  [per_device(): lax.all_to_all(adapter_update, 'adapter', split_axis=0, concat_axis=0, ti...]
    ppermute x5, waiting for transfers between devices: 13.1 us -> 7.09 us  [_swap(): return lax.ppermute(x, 'tensor', perm=[(i, i ^ mask) for i in range(count)])]
  transfers between devices with their start and end apart: 7 -> 6, of which waited for: 5 -> 5; matrix products, arithmetic and copies ran while one was open for 36% -> 4% of each run, Pallas kernels for 0% -> 17%
where the time goes in v2:
time: 84.2 us; the launch traced here: 83.6 us
  blocking collectives  30.9 us (37%)
  waiting for transfers between devices  16.4 us (19%)
  Pallas kernels  14.5 us (17%)
  starting transfers between devices  6.11 us (7%)
  other arithmetic  5.94 us (7%)
  matrix products  5.49 us (7%)
  local copies, waits for them, and re-layouts  3.12 us (4%)
  between operations  1.07 us (1%)
    all_to_all x1, blocking collectives, per_device(): lax.all_to_all(payload, 'adapter', split_axis=0, concat_axis=0, tiled=True)  30.9 us
    pallas_call x1, Pallas kernels, cache_attention(): pl.pallas_call(kernel, out_shape=(out, out, out), grid_spec=pltpu.Prefetc...  14.5 us
    all_to_all x1, waiting for transfers between devices, per_device(): lax.all_to_all(adapter_update, 'adapter', split_axis=0, concat_axis=0, ti...  9.34 us
    ppermute x5, waiting for transfers between devices, _swap(): return lax.ppermute(x, 'tensor', perm=[(i, i ^ mask) for i in range(count)])  7.09 us
    all_to_all x1, starting transfers between devices, per_device(): lax.all_to_all(adapter_update, 'adapter', split_axis=0, concat_axis=0, ti...  3.87 us
    ppermute x5, starting transfers between devices, _swap(): return lax.ppermute(x, 'tensor', perm=[(i, i ^ mask) for i in range(count)])  2.24 us
    dot_general x1, matrix products, per_device(): jnp.dot(flattened_rows, adapter_down_weight, preferred_element_type=jnp.f...  1.74 us
  transfers between devices with their start and end apart: 6, of which 5 were waited for; matrix products, arithmetic and copies ran while one was open for 4% of the time, Pallas kernels for 17%

profile of v2, /device:TPU:0, one launch (start us, length us, event | category | flops | bytes accessed | tf_op | source)
XLA Modules:
  0.0 83.6 jit_solution(18440159687050002230)
XLA Ops:
  0.7 1.1 %dynamic-slice_bitcast_fusion = bf16[32,8192]{1,0:T(8,128)(2,1)S(1)} fusion(bf16[2,32,8192]{2,1,0:T(8,128)(2,1)} %bitcast.88, s32[]{:T(128)S(6)} %select_n.74), kind=kLoop, calls=%fused_computation.27 | loop fusion | bytes 1048580 | tf_op jit(solution)/shard_map/jit(dynamic_index_in_dim)/squeeze | solution.py:94
  1.8 1.9 %collective-permute-done = bf16[32,8192]{1,0:T(8,128)(2,1)S(1)} collective-permute-done((bf16[32,8192]{1,0:T(8,128)(2,1)S(1)}, bf16[32,8192]{1,0:T(8,128)(2,1)S(1)}, u32[]{:S(2)}, u32[]{:S(2)}) %collective-permute-start) | collective-permute-done | bytes 524320 | tf_op jit(solution)/shard_map/ppermute | solution.py:66
  3.7 1.2 %fusion.14 = bf16[32,8192]{1,0:T(8,128)(2,1)S(1)} fusion(bf16[32,8192]{1,0:T(8,128)(2,1)S(1)} %collective-permute-done, bf16[2,32,8192]{2,1,0:T(8,128)(2,1)} %bitcast.89, s32[]{:T(128)S(6)} %select_n.73), kind=kLoop, calls=%fused_computation.21 | loop fusion | flops 1048576 | bytes 1572868 | tf_op jit(solution)/shard_map/convert_element_type | solution.py:97
  4.9 1.7 %collective-permute-start.1 = (bf16[32,8192]{1,0:T(8,128)(2,1)S(1)}, bf16[32,8192]{1,0:T(8,128)(2,1)S(1)}, u32[]{:S(2)}, u32[]{:S(2)}) collective-permute-start(bf16[32,8192]{1,0:T(8,128)(2,1)S(1)} %fusion.14), channel_id=1, source_target_pairs={{0,2},{1,3},{2,0},{3,1},{4,6},{5,7},{6,4},{7,5},{8,10},{9,11},{10,... | collective-permute-start | bytes 1572872 | tf_op jit(solution)/shard_map/ppermute | solution.py:66
  6.6 14.5 %shard_map.121 = (f32[64,2048]{1,0:T(8,128)}, f32[64,2048]{1,0:T(8,128)}, f32[64,2048]{1,0:T(8,128)}) custom-call(s32[8]{0:T(128)} %len_ref.1, bf16[64,2048]{1,0:T(8,128)(2,1)} %q_ref.1, bf16[8,2,1024,256]{3,2,1,0:T(8,128)(2,1)} %v_ref.1, bf16[8,2,1024,256]{3,2,1,0:T(8,128)(2,1)} %v_ref.1), custom_call_target="tpu_custom_call" | custom-call | tf_op jit(solution)/shard_map/pallas_call | solution.py:49
  21.2 1.5 %fusion.7 = (f32[32]{0:T(128)S(1)}, bf16[32,8192]{1,0:T(8,128)(2,1)S(1)}) fusion(bf16[32,8192]{1,0:T(8,128)(2,1)S(1)} %collective-permute-done.1, bf16[32,8192]{1,0:T(8,128)(2,1)S(1)} %collective-permute-done, bf16[2,32,8192]{2,1,0:T(8,128)(2,1)S(1)} %bitcast.90, s32[]{:T(128)S(6)} %select_n.73, bf16[2,32,8192]{2,1,0:T(8,128)(2,1)} %bitcast.106), kind=kLoop, calls=%fused_computation.10 | loop fusion | flops 2883552 | bytes 2621572 | tf_op jit(solution)/shard_map/reduce_sum | solution.py:111
  22.7 0.2 fusion.9
  23.0 0.2 convert_reduce_fusion.1
  23.3 1.8 %collective-permute-done.2 = bf16[32,10240]{1,0:T(8,128)(2,1)S(1)} collective-permute-done((bf16[32,10240]{1,0:T(8,128)(2,1)S(1)}, bf16[32,10240]{1,0:T(8,128)(2,1)S(1)}, u32[]{:S(2)}, u32[]{:S(2)}) %collective-permute-start.2) | collective-permute-done | bytes 655392 | tf_op jit(solution)/shard_map/ppermute | solution.py:66
  25.2 0.2 maximum_select_fusion
  25.4 0.5 convolution_convert_fusion
  26.1 30.9 %all_to_all.10 = bf16[32,8,2176]{2,1,0:T(8,128)(2,1)S(1)} all-to-all(bf16[32,8,2176]{2,1,0:T(8,128)(2,1)S(1)} %maximum_bitcast_fusion), channel_id=1, replica_groups=mesh['adapter'=32,'tensor'=4] {'adapter'}, dimensions={0} | all-to-all | bytes 2228224 | tf_op jit(solution)/shard_map/all_to_all | solution.py:160
  57.0 0.1 convert_reduce_fusion
  57.2 1.7 %fusion.10 = f32[256,1024]{0,1:T(8,128)S(1)} fusion(bf16[2048,1024]{1,0:T(8,128)(2,1)S(1)} %copy-done.8, bf16[256,2176]{1,0:T(8,128)(2,1)S(1)} %bitcast.97), kind=kOutput, calls=%fused_computation.13 | convolution fusion | flops 1073741824 | bytes 6291456 | tf_op jit(solution)/shard_map/dot_general | solution.py:166
  59.1 0.2 copy.46
  59.4 1.0 %collective-permute-done.3 = f32[256,64]{0,1:T(8,128)S(1)} collective-permute-done((f32[256,64]{0,1:T(8,128)S(1)}, f32[256,64]{0,1:T(8,128)S(1)}, u32[]{:S(2)}, u32[]{:S(2)}) %collective-permute-start.3) | collective-permute-done | bytes 65568 | tf_op jit(solution)/shard_map/ppermute | solution.py:66
  60.4 0.3 collective-permute-start.4
  60.7 1.6 %fusion.4 = f32[2,8,8,256]{3,2,1,0:T(8,128)S(1)} fusion(bf16[2,8192,256]{2,0,1:T(2,128)(2,1)S(1)} %bitcast.110, bf16[64,8192]{1,0:T(8,128)(2,1)S(1)} %maximum_select_fusion), kind=kOutput, calls=%fused_computation.8 | convolution fusion | flops 536870912 | bytes 9568256 | tf_op jit(solution)/shard_map/rf,hfd->rhd/dot_general | solution.py:134
  62.3 2.4 %collective-permute-done.4 = f32[256,64]{0,1:T(8,128)S(1)} collective-permute-done((f32[256,64]{0,1:T(8,128)S(1)}, f32[256,64]{0,1:T(8,128)S(1)}, u32[]{:S(2)}, u32[]{:S(2)}) %collective-permute-start.4) | collective-permute-done | bytes 65568 | tf_op jit(solution)/shard_map/ppermute | solution.py:66
  64.8 1.2 %fusion.3 = bf16[32,8,512]{2,1,0:T(8,128)(2,1)} fusion(bf16[256,1024]{0,1:T(8,128)(2,1)S(1)} %bitcast.104, bf16[1024,512]{1,0:T(8,128)(2,1)S(1)} %bitcast.100), kind=kOutput, calls=%fused_computation.7 | convolution fusion | flops 268697600 | bytes 1835008 | tf_op jit(solution)/shard_map/dot_general | solution.py:177
  66.0 3.9 %all-to-all-start.1 = ((bf16[32,8,512]{2,1,0:T(8,128)(2,1)}), bf16[32,8,512]{2,1,0:T(8,128)(2,1)S(1)}, u32[]{:S(2)}, u32[]{:S(2)}) async-start(bf16[32,8,512]{2,1,0:T(8,128)(2,1)} %fusion.3), calls=%async_computation.1 | async-start | bytes 524288 | tf_op jit(solution)/shard_map/all_to_all | solution.py:180
  70.0 0.3 copy.43
  70.4 0.3 copy.44
  70.7 0.8 maximum_select_fusion.1
  71.4 9.3 %all-to-all-done.1 = bf16[32,8,512]{2,1,0:T(8,128)(2,1)S(1)} async-done(((bf16[32,8,512]{2,1,0:T(8,128)(2,1)}), bf16[32,8,512]{2,1,0:T(8,128)(2,1)S(1)}, u32[]{:S(2)}, u32[]{:S(2)}) %all-to-all-start.1) | async-done | bytes 262176 | tf_op jit(solution)/shard_map/all_to_all | solution.py:180
  80.8 0.2 fusion.16
  81.1 0.3 fusion.19
  81.5 0.1 copy.39
  81.8 0.2 broadcast_multiply_fusion
  82.0 0.2 mul.88
  82.2 0.2 div.35
  82.4 1.2 %fusion.15 = bf16[64,2048]{1,0:T(8,128)(2,1)} fusion(f32[8,8,16,128]{3,2,1,0:T(8,128)S(1)} %bitcast.95, f32[8,8,16,128]{3,2,1,0:T(8,128)S(1)} %bitcast.91, f32[64,2048]{1,0:T(8,128)S(1)} %copy-done.5, f32[8,8,16,128]{3,2,1,0:T(8,128)S(1)} %bitcast.94), kind=kLoop, calls=%fused_computation.24 | loop fusion | flops 524288 | bytes 2359296 | tf_op jit(solution)/shard_map/convert_element_type | solution.py:212
  (57 shorter events, 1.6 us)
Async XLA Ops:
  0.6 6.0 %copy-start.7 = (bf16[8192]{0:T(1024)(128)(2,1)S(1)}, bf16[8192]{0:T(1024)(128)(2,1)}, u32[]{:S(2)}) copy-start(bf16[8192]{0:T(1024)(128)(2,1)} %param.12) | copy-start | bytes 49156
  1.7 2.0 %collective-permute-start = (bf16[32,8192]{1,0:T(8,128)(2,1)S(1)}, bf16[32,8192]{1,0:T(8,128)(2,1)S(1)}, u32[]{:S(2)}, u32[]{:S(2)}) collective-permute-start(bf16[32,8192]{1,0:T(8,128)(2,1)S(1)} %dynamic-slice_bitcast_fusion), channel_id=1, source_target_pairs={{0,1},{1,0},{2,3},{3,2},{4,5},{5,4},{6,7},{7,6},{8,9},{9,8},{10,11... | collective-permute-start | bytes 1572872 | tf_op jit(solution)/shard_map/ppermute | solution.py:66
  4.9 16.3 %collective-permute-start.1 = (bf16[32,8192]{1,0:T(8,128)(2,1)S(1)}, bf16[32,8192]{1,0:T(8,128)(2,1)S(1)}, u32[]{:S(2)}, u32[]{:S(2)}) collective-permute-start(bf16[32,8192]{1,0:T(8,128)(2,1)S(1)} %fusion.14), channel_id=1, source_target_pairs={{0,2},{1,3},{2,0},{3,1},{4,6},{5,7},{6,4},{7,5},{8,10},{9,11},{10,... | collective-permute-start | bytes 1572872 | tf_op jit(solution)/shard_map/ppermute | solution.py:66
  6.6 14.5 %copy-start.9 = (s32[64]{0:T(128)S(1)}, s32[64]{0:T(128)}, u32[]{:S(2)}) copy-start(s32[64]{0:T(128)} %param.16) | copy-start | bytes 772
  6.6 14.6 %copy-start = (bf16[1,64,8192]{2,1,0:T(8,128)(2,1)S(1)}, bf16[1,64,8192]{2,1,0:T(8,128)(2,1)}, u32[]{:S(2)}) copy-start(bf16[1,64,8192]{2,1,0:T(8,128)(2,1)} %param.10) | copy-start | bytes 3145732
  22.9 2.2 %collective-permute-start.2 = (bf16[32,10240]{1,0:T(8,128)(2,1)S(1)}, bf16[32,10240]{1,0:T(8,128)(2,1)S(1)}, u32[]{:S(2)}, u32[]{:S(2)}) collective-permute-start(bf16[32,10240]{1,0:T(8,128)(2,1)S(1)} %pad_maximum_fusion), channel_id=1, source_target_pairs={{0,1},{1,0},{2,3},{3,2},{4,5},{5,4},{6,7},{7,6},{8,9},{9,8},{10,11... | collective-permute-start | bytes 1966088 | tf_op jit(solution)/shard_map/ppermute | solution.py:66
  25.2 32.0 %copy-start.8 = (bf16[2048,1024]{1,0:T(8,128)(2,1)S(1)}, bf16[2048,1024]{1,0:T(8,128)(2,1)}, u32[]{:S(2)}) copy-start(bf16[2048,1024]{1,0:T(8,128)(2,1)} %param.14) | copy-start | bytes 12582916
  25.3 35.3 %slice-start = ((s8[8388608]{0:T(1024)(128)(4,1)}), s8[4194304]{0:T(1024)(128)(4,1)S(1)}, s32[]{:S(2)}) async-start(s8[8388608]{0:T(1024)(128)(4,1)} %bitcast.108), calls=%async_computation.2 | async-start | bytes 8388608
  57.2 2.0 %copy-start.2 = (bf16[1024,2,256]{2,1,0:T(2,128)(2,1)S(1)}, bf16[1024,2,256]{2,1,0:T(2,128)(2,1)}, u32[]{:S(2)}) copy-start(bf16[1024,2,256]{2,1,0:T(2,128)(2,1)} %param.15) | copy-start | bytes 3145732
  57.2 3.5 %slice-start.1 = ((s8[8388608]{0:T(1024)(128)(4,1)}), s8[4194304]{0:T(1024)(128)(4,1)S(1)}, s32[]{:S(2)}) async-start(s8[8388608]{0:T(1024)(128)(4,1)} %bitcast.108), calls=%async_computation.3 | async-start | bytes 8388608
  59.0 1.3 %collective-permute-start.3 = (f32[256,64]{0,1:T(8,128)S(1)}, f32[256,64]{0,1:T(8,128)S(1)}, u32[]{:S(2)}, u32[]{:S(2)}) collective-permute-start(f32[256,64]{0,1:T(8,128)S(1)} %select_reduce_fusion), channel_id=1, source_target_pairs={{0,1},{1,0},{2,3},{3,2},{4,5},{5,4},{6,7},{7,6},{8,9},{9,8},{10,11... | collective-permute-start | bytes 196616 | tf_op jit(solution)/shard_map/ppermute | solution.py:66
  60.4 4.3 %collective-permute-start.4 = (f32[256,64]{0,1:T(8,128)S(1)}, f32[256,64]{0,1:T(8,128)S(1)}, u32[]{:S(2)}, u32[]{:S(2)}) collective-permute-start(f32[256,64]{0,1:T(8,128)S(1)} %add.89), channel_id=1, source_target_pairs={{0,2},{1,3},{2,0},{3,1},{4,6},{5,7},{6,4},{7,5},{8,10},{9,11},{10,... | collective-permute-start | bytes 196616 | tf_op jit(solution)/shard_map/ppermute | solution.py:66
  62.3 7.6 %copy-start.1 = (bf16[64,2048]{1,0:T(8,128)(2,1)S(1)}, bf16[64,2048]{1,0:T(8,128)(2,1)}, u32[]{:S(2)}) copy-start(bf16[64,2048]{1,0:T(8,128)(2,1)} %q_ref.1) | copy-start | bytes 786436
  62.3 7.6 %copy-start.4 = (f32[64,2048]{1,0:T(8,128)S(1)}, f32[64,2048]{1,0:T(8,128)}, u32[]{:S(2)}) copy-start(f32[64,2048]{1,0:T(8,128)} %get-tuple-element.20) | copy-start | bytes 1572868
  64.8 5.5 %copy-start.3 = (f32[64,2048]{1,0:T(8,128)S(1)}, f32[64,2048]{1,0:T(8,128)}, u32[]{:S(2)}) copy-start(f32[64,2048]{1,0:T(8,128)} %get-tuple-element.22) | copy-start | bytes 1572868
  66.0 14.8 %all-to-all-start.1 = ((bf16[32,8,512]{2,1,0:T(8,128)(2,1)}), bf16[32,8,512]{2,1,0:T(8,128)(2,1)S(1)}, u32[]{:S(2)}, u32[]{:S(2)}) async-start(bf16[32,8,512]{2,1,0:T(8,128)(2,1)} %fusion.3), calls=%async_computation.1 | async-start | bytes 524288 | tf_op jit(solution)/shard_map/all_to_all | solution.py:180
  70.7 11.8 %copy-start.5 = (f32[64,2048]{1,0:T(8,128)S(1)}, f32[64,2048]{1,0:T(8,128)}, u32[]{:S(2)}) copy-start(f32[64,2048]{1,0:T(8,128)} %get-tuple-element.21) | copy-start | bytes 1572868
  81.0 2.6 %copy-start.6 = (bf16[64,2,256]{2,1,0:T(2,128)(2,1)}, bf16[64,2,256]{2,1,0:T(2,128)(2,1)S(1)}, u32[]{:S(2)}) copy-start(bf16[64,2,256]{2,1,0:T(2,128)(2,1)S(1)} %reshape.120) | copy-start | bytes 196612

commit v3 on v2

--- a/solution.py
+++ b/solution.py
@@ -17,47 +17,56 @@
 ID_LANES = 128
 
 
-def _attn_kernel(len_ref, q_ref, k_ref, v_ref, num_ref, top_ref, tot_ref, *, group, scale):
-    p = pl.program_id(0)
+def _attn_kernel(len_ref, q_ref, k_ref, v_ref, num_ref, top_ref, tot_ref, *, heads, group, scale, first):
+    p = pl.program_id(0) + first
     length = len_ref[p]
-    q = q_ref[...]
-    fan = q.shape[0]
-    qs = jnp.concatenate([q[:, g * HEAD_SIZE:(g + 1) * HEAD_SIZE] for g in range(group)], axis=0)
-    kb = k_ref[0, 0]
-    s = lax.dot_general(qs, kb, (((1,), (1,)), ((), ())), preferred_element_type=jnp.float32) * scale
-    col = lax.broadcasted_iota(jnp.int32, s.shape, 1)
-    s = jnp.where(col < length, s, -jnp.inf)
-    m = jnp.max(s, axis=1, keepdims=True)
-    w = jnp.exp(s - m).astype(jnp.bfloat16)
-    tot = jnp.sum(w.astype(jnp.float32), axis=1, keepdims=True)
-    num = jnp.dot(w, v_ref[0, 0], preferred_element_type=jnp.float32)
-    num_ref[...] = jnp.concatenate([num[g * fan:(g + 1) * fan] for g in range(group)], axis=1)
-    top_ref[...] = jnp.concatenate(
-        [jnp.broadcast_to(m[g * fan:(g + 1) * fan], (fan, HEAD_SIZE)) for g in range(group)], axis=1)
-    tot_ref[...] = jnp.concatenate(
-        [jnp.broadcast_to(tot[g * fan:(g + 1) * fan], (fan, HEAD_SIZE)) for g in range(group)], axis=1)
-
-
-def cache_attention(queries, key_value_cache, prompt_cache_length, local_heads, fan):
-    prompts, _, cache_len, _ = key_value_cache.shape
-    rows, width = queries.shape
-    head_width = width // local_heads
-    group = head_width // HEAD_SIZE
-    kernel = functools.partial(_attn_kernel, group=group, scale=HEAD_SIZE ** (-0.5))
-    out = jax.ShapeDtypeStruct((rows, width), jnp.float32)
-    spec_q = pl.BlockSpec((fan, head_width), lambda p, k, lens: (p, k))
+    fan = q_ref.shape[0]
+    head_width = group * HEAD_SIZE
+    for k in range(heads):
+        lanes = pl.ds(k * HEAD_SIZE, HEAD_SIZE)
+        qs = jnp.concatenate(
+            [q_ref[:, pl.ds(k * head_width + g * HEAD_SIZE, HEAD_SIZE)] for g in range(group)], axis=0)
+        kb = k_ref[0, 0, :, lanes]
+        s = lax.dot_general(qs, kb, (((1,), (1,)), ((), ())), preferred_element_type=jnp.float32) * scale
+        col = lax.broadcasted_iota(jnp.int32, s.shape, 1)
+        s = jnp.where(col < length, s, -jnp.inf)
+        m = jnp.max(s, axis=1, keepdims=True)
+        w = jnp.exp(s - m).astype(jnp.bfloat16)
+        tot = jnp.sum(w.astype(jnp.float32), axis=1, keepdims=True)
+        num = jnp.dot(w, v_ref[0, 0, :, lanes], preferred_element_type=jnp.float32)
+        for g in range(group):
+            out_lanes = pl.ds(k * head_width + g * HEAD_SIZE, HEAD_SIZE)
+            rows = slice(g * fan, (g + 1) * fan)
+            num_ref[:, out_lanes] = num[rows]
+            top_ref[:, out_lanes] = jnp.broadcast_to(m[rows], (fan, HEAD_SIZE))
+            tot_ref[:, out_lanes] = jnp.broadcast_to(tot[rows], (fan, HEAD_SIZE))
+
+
+def cache_attention(queries, key_value_cache, prompt_cache_length, local_heads, fan, first, count):
+    _, _, cache_len, kv_width = key_value_cache.shape
+    width = queries.shape[1]
+    group = width // (local_heads * HEAD_SIZE)
+    kernel = functools.partial(
+        _attn_kernel, heads=local_heads, group=group, scale=HEAD_SIZE ** (-0.5), first=first)
+    out = jax.ShapeDtypeStruct((count * fan, width), jnp.float32)
+    spec_out = pl.BlockSpec((fan, width), lambda p, lens: (p, 0))
     return pl.pallas_call(
         kernel,
         out_shape=(out, out, out),
         grid_spec=pltpu.PrefetchScalarGridSpec(
             num_scalar_prefetch=1,
-            grid=(prompts, local_heads),
+            grid=(count,),
             in_specs=[
-                spec_q,
-                pl.BlockSpec((1, 1, cache_len, HEAD_SIZE), lambda p, k, lens: (p, 0, 0, k)),
-                pl.BlockSpec((1, 1, cache_len, HEAD_SIZE), lambda p, k, lens: (p, 1, 0, k)),
+                pl.BlockSpec((fan, width), lambda p, lens: (p + first, 0)),
+                pl.BlockSpec((1, 1, cache_len, kv_width), lambda p, lens: (p + first, 0, 0, 0)),
+                pl.BlockSpec((1, 1, cache_len, kv_width), lambda p, lens: (p + first, 1, 0, 0)),
             ],
-            out_specs=[spec_q, spec_q, spec_q],
+            out_specs=[spec_out, spec_out, spec_out],
+        ),
+        cost_estimate=pl.CostEstimate(
+            flops=4 * count * fan * width * cache_len,
+            transcendentals=count * fan * width * cache_len // HEAD_SIZE,
+            bytes_accessed=count * (2 * cache_len * kv_width * 2 + fan * width * 14),
         ),
     )(prompt_cache_length, queries, key_value_cache, key_value_cache)
 
@@ -95,11 +104,13 @@
     got_p = _swap(other_p, 1, tensor_count)
     chip_sum = mine_p.astype(jnp.float32) + got_p.astype(jnp.float32)
     far_sum = _swap(chip_sum.astype(jnp.bfloat16), 2, tensor_count)
-    attention_parts = cache_attention(
-        queries, key_value_cache, prompt_cache_length, local_heads, FAN
-    )
-    far_sum, head_weight, attention_parts = lax.optimization_barrier(
-        (far_sum, head_weight, attention_parts)
+    local_prompts = key_value_cache.shape[0]
+    early_prompts = local_prompts // 2
+    attention_early = cache_attention(
+        queries, key_value_cache, prompt_cache_length, local_heads, FAN, 0, early_prompts
+    )
+    far_sum, head_weight, attention_early = lax.optimization_barrier(
+        (far_sum, head_weight, attention_early)
     )
     res_half = lax.dynamic_index_in_dim(
         residual.reshape(2, half_rows, model_width), core, axis=0, keepdims=False
@@ -178,6 +189,16 @@
     ).astype(jnp.bfloat16)
     adapter_update = adapter_update.reshape(adapt_count, item_count, -1)
     returned = lax.all_to_all(adapter_update, "adapter", split_axis=0, concat_axis=0, tiled=True)
+    attention_late = cache_attention(
+        queries,
+        key_value_cache,
+        prompt_cache_length,
+        local_heads,
+        FAN,
+        early_prompts,
+        local_prompts - early_prompts,
+    )
+    returned, attention_late = lax.optimization_barrier((returned, attention_late))
     returned = returned.reshape(slot_count, -1)
     update_rows = lax.dot_general(
         slot_matrix, returned, (((0,), (0,)), ((), ())), preferred_element_type=jnp.float32
@@ -186,10 +207,12 @@
         (base_kv + update_rows).astype(jnp.bfloat16).reshape(row_dev, local_heads, 2 * HEAD_SIZE)
     )
 
-    local_prompts = key_value_cache.shape[0]
     group_size = queries.shape[1] // (local_heads * HEAD_SIZE)
     score_scale = HEAD_SIZE ** (-0.5)
-    num_c, top_c, tot_c = attention_parts
+    num_c, top_c, tot_c = [
+        jnp.concatenate([early, late], axis=0)
+        for early, late in zip(attention_early, attention_late)
+    ]
     view = (row_dev, local_heads, group_size, HEAD_SIZE)
     cache_weighted = num_c.reshape(view)
     cache_top = top_c.reshape(view)[..., 0]

time: 84.2 us -> 84.2 us (level)
  Pallas kernels: 14.5 us -> 12.8 us
  other arithmetic: 5.94 us -> 7.06 us
    all_to_all x1, waiting for transfers between devices: 9.34 us -> 3.74 us  [per_device(): lax.all_to_all(adapter_update, 'adapter', split_axis=0, concat_axis=0, ti...]
    ppermute x5, waiting for transfers between devices: 7.09 us -> 12.1 us  [_swap(): return lax.ppermute(x, 'tensor', perm=[(i, i ^ mask) for i in range(count)])]
    pallas_call x1 -> x2, Pallas kernels: 14.5 us -> 12.8 us  [cache_attention(): pl.pallas_call(kernel, out_shape=(out, out, out), grid_spec=pltpu.Prefetc...]
    unnamed x1 -> x2, other arithmetic: 0.01 us -> 1.13 us
  transfers between devices with their start and end apart: 6 -> 6, of which waited for: 5 -> 6; matrix products, arithmetic and copies ran while one was open for 4% -> 3% of each run, Pallas kernels for 17% -> 15%
where the time goes in v3:
time: 84.2 us; the launch traced here: 83.7 us
  blocking collectives  31.3 us (37%)
  waiting for transfers between devices  15.9 us (19%)
  Pallas kernels  12.8 us (15%)
  other arithmetic  7.06 us (8%)
  starting transfers between devices  6.48 us (8%)
  matrix products  5.48 us (7%)
  local copies, waits for them, and re-layouts  3.62 us (4%)
  between operations  1.08 us (1%)
    all_to_all x1, blocking collectives, per_device(): lax.all_to_all(payload, 'adapter', split_axis=0, concat_axis=0, tiled=True)  31.3 us
    pallas_call x2, Pallas kernels, cache_attention(): pl.pallas_call(kernel, out_shape=(out, out, out), grid_spec=pltpu.Prefetc...  12.8 us
    ppermute x5, waiting for transfers between devices, _swap(): return lax.ppermute(x, 'tensor', perm=[(i, i ^ mask) for i in range(count)])  12.1 us
    all_to_all x1, starting transfers between devices, per_device(): lax.all_to_all(adapter_update, 'adapter', split_axis=0, concat_axis=0, ti...  3.87 us
    all_to_all x1, waiting for transfers between devices, per_device(): lax.all_to_all(adapter_update, 'adapter', split_axis=0, concat_axis=0, ti...  3.74 us
    ppermute x5, starting transfers between devices, _swap(): return lax.ppermute(x, 'tensor', perm=[(i, i ^ mask) for i in range(count)])  2.61 us
    dot_general x1, matrix products, per_device(): jnp.dot(flattened_rows, adapter_down_weight, preferred_element_type=jnp.f...  1.74 us
  transfers between devices with their start and end apart: 6, of which 6 were waited for; matrix products, arithmetic and copies ran while one was open for 3% of the time, Pallas kernels for 15%

profile of v3, /device:TPU:0, one launch (start us, length us, event | category | flops | bytes accessed | tf_op | source)
XLA Modules:
  0.0 83.7 jit_solution(2553859452544525835)
XLA Ops:
  0.7 1.1 %dynamic-slice_bitcast_fusion = bf16[32,8192]{1,0:T(8,128)(2,1)S(1)} fusion(bf16[2,32,8192]{2,1,0:T(8,128)(2,1)} %bitcast.91, s32[]{:T(128)S(6)} %select_n.74), kind=kLoop, calls=%fused_computation.29 | loop fusion | bytes 1048580 | tf_op jit(solution)/shard_map/jit(dynamic_index_in_dim)/squeeze | solution.py:103
  1.8 1.9 %collective-permute-done = bf16[32,8192]{1,0:T(8,128)(2,1)S(1)} collective-permute-done((bf16[32,8192]{1,0:T(8,128)(2,1)S(1)}, bf16[32,8192]{1,0:T(8,128)(2,1)S(1)}, u32[]{:S(2)}, u32[]{:S(2)}) %collective-permute-start) | collective-permute-done | bytes 524320 | tf_op jit(solution)/shard_map/ppermute | solution.py:75
  3.7 1.2 %fusion.14 = bf16[32,8192]{1,0:T(8,128)(2,1)S(1)} fusion(bf16[32,8192]{1,0:T(8,128)(2,1)S(1)} %collective-permute-done, bf16[2,32,8192]{2,1,0:T(8,128)(2,1)} %bitcast.92, s32[]{:T(128)S(6)} %select_n.73), kind=kLoop, calls=%fused_computation.21 | loop fusion | flops 1048576 | bytes 1572868 | tf_op jit(solution)/shard_map/convert_element_type | solution.py:106
  4.9 1.7 %collective-permute-start.1 = (bf16[32,8192]{1,0:T(8,128)(2,1)S(1)}, bf16[32,8192]{1,0:T(8,128)(2,1)S(1)}, u32[]{:S(2)}, u32[]{:S(2)}) collective-permute-start(bf16[32,8192]{1,0:T(8,128)(2,1)S(1)} %fusion.14), channel_id=1, source_target_pairs={{0,2},{1,3},{2,0},{3,1},{4,6},{5,7},{6,4},{7,5},{8,10},{9,11},{10,... | collective-permute-start | bytes 1572872 | tf_op jit(solution)/shard_map/ppermute | solution.py:75
  6.6 6.4 %shard_map.121 = (f32[32,2048]{1,0:T(8,128)}, f32[32,2048]{1,0:T(8,128)}, f32[32,2048]{1,0:T(8,128)}) custom-call(s32[8]{0:T(128)} %len_ref.3, bf16[64,2048]{1,0:T(8,128)(2,1)} %q_ref.3, bf16[8,2,1024,256]{3,2,1,0:T(8,128)(2,1)} %v_ref.3, bf16[8,2,1024,256]{3,2,1,0:T(8,128)(2,1)} %v_ref.3), custom_call_target="tpu_custom_call" | custom-call | flops 268435456 | bytes 5111808 | tf_op jit(solution)/shard_map/pallas_call | solution.py:53
  13.0 5.9 %collective-permute-done.1 = bf16[32,8192]{1,0:T(8,128)(2,1)S(1)} collective-permute-done((bf16[32,8192]{1,0:T(8,128)(2,1)S(1)}, bf16[32,8192]{1,0:T(8,128)(2,1)S(1)}, u32[]{:S(2)}, u32[]{:S(2)}) %collective-permute-start.1) | collective-permute-done | bytes 524320 | tf_op jit(solution)/shard_map/ppermute | solution.py:75
  18.9 1.5 %fusion.7 = (f32[32]{0:T(128)S(1)}, bf16[32,8192]{1,0:T(8,128)(2,1)S(1)}) fusion(bf16[32,8192]{1,0:T(8,128)(2,1)S(1)} %collective-permute-done.1, bf16[32,8192]{1,0:T(8,128)(2,1)S(1)} %collective-permute-done, bf16[2,32,8192]{2,1,0:T(8,128)(2,1)S(1)} %bitcast.93, s32[]{:T(128)S(6)} %select_n.73, bf16[2,32,8192]{2,1,0:T(8,128)(2,1)} %bitcast.106), kind=kLoop, calls=%fused_computation.10 | loop fusion | flops 2883552 | bytes 2621572 | tf_op jit(solution)/shard_map/reduce_sum | solution.py:122
  20.5 0.2 fusion.9
  21.1 1.8 %collective-permute-done.2 = bf16[32,10240]{1,0:T(8,128)(2,1)S(1)} collective-permute-done((bf16[32,10240]{1,0:T(8,128)(2,1)S(1)}, bf16[32,10240]{1,0:T(8,128)(2,1)S(1)}, u32[]{:S(2)}, u32[]{:S(2)}) %collective-permute-start.2) | collective-permute-done | bytes 655392 | tf_op jit(solution)/shard_map/ppermute | solution.py:75
  23.1 0.5 convolution_convert_fusion
  23.9 31.3 %all_to_all.10 = bf16[32,8,2176]{2,1,0:T(8,128)(2,1)S(1)} all-to-all(bf16[32,8,2176]{2,1,0:T(8,128)(2,1)S(1)} %maximum_bitcast_fusion), channel_id=1, replica_groups=mesh['adapter'=32,'tensor'=4] {'adapter'}, dimensions={0} | all-to-all | bytes 2228224 | tf_op jit(solution)/shard_map/all_to_all | solution.py:171
  55.4 1.7 %fusion.10 = f32[256,1024]{0,1:T(8,128)S(1)} fusion(bf16[2048,1024]{1,0:T(8,128)(2,1)S(1)} %copy-done.9, bf16[256,2176]{1,0:T(8,128)(2,1)S(1)} %bitcast.100), kind=kOutput, calls=%fused_computation.13 | convolution fusion | flops 1073741824 | bytes 6291456 | tf_op jit(solution)/shard_map/dot_general | solution.py:177
  57.3 0.2 copy.46
  57.6 0.5 copy-done
  58.1 0.5 collective-permute-done.3
  58.6 0.7 collective-permute-start.4
  59.3 1.6 %fusion.4 = f32[2,8,8,256]{3,2,1,0:T(8,128)S(1)} fusion(bf16[2,8192,256]{2,0,1:T(2,128)(2,1)S(1)} %bitcast.110, bf16[64,8192]{1,0:T(8,128)(2,1)S(1)} %maximum_select_fusion), kind=kOutput, calls=%fused_computation.8 | convolution fusion | flops 536870912 | bytes 9568256 | tf_op jit(solution)/shard_map/rf,hfd->rhd/dot_general | solution.py:145
  60.8 2.1 %collective-permute-done.4 = f32[256,64]{0,1:T(8,128)S(1)} collective-permute-done((f32[256,64]{0,1:T(8,128)S(1)}, f32[256,64]{0,1:T(8,128)S(1)}, u32[]{:S(2)}, u32[]{:S(2)}) %collective-permute-start.4) | collective-permute-done | bytes 65568 | tf_op jit(solution)/shard_map/ppermute | solution.py:75
  63.0 1.2 %fusion.3 = bf16[32,8,512]{2,1,0:T(8,128)(2,1)} fusion(bf16[256,1024]{0,1:T(8,128)(2,1)S(1)} %bitcast.104, bf16[1024,512]{1,0:T(8,128)(2,1)S(1)} %bitcast.102), kind=kOutput, calls=%fused_computation.7 | convolution fusion | flops 268697600 | bytes 1835008 | tf_op jit(solution)/shard_map/dot_general | solution.py:188
  64.1 3.9 %all-to-all-start.1 = ((bf16[32,8,512]{2,1,0:T(8,128)(2,1)}), bf16[32,8,512]{2,1,0:T(8,128)(2,1)S(1)}, u32[]{:S(2)}, u32[]{:S(2)}) async-start(bf16[32,8,512]{2,1,0:T(8,128)(2,1)} %fusion.3), calls=%async_computation.1 | async-start | bytes 524288 | tf_op jit(solution)/shard_map/all_to_all | solution.py:191
  68.0 6.4 %shard_map.122 = (f32[32,2048]{1,0:T(8,128)}, f32[32,2048]{1,0:T(8,128)}, f32[32,2048]{1,0:T(8,128)}) custom-call(s32[8]{0:T(128)} %len_ref.3, bf16[64,2048]{1,0:T(8,128)(2,1)} %q_ref.3, bf16[8,2,1024,256]{3,2,1,0:T(8,128)(2,1)} %v_ref.3, bf16[8,2,1024,256]{3,2,1,0:T(8,128)(2,1)} %v_ref.3), custom_call_target="tpu_custom_call" | custom-call | flops 268435456 | bytes 5111808 | tf_op jit(solution)/shard_map/pallas_call | solution.py:53
  74.5 0.8 maximum_select_fusion.1
  75.2 3.7 %all-to-all-done.1 = bf16[32,8,512]{2,1,0:T(8,128)(2,1)S(1)} async-done(((bf16[32,8,512]{2,1,0:T(8,128)(2,1)}), bf16[32,8,512]{2,1,0:T(8,128)(2,1)S(1)}, u32[]{:S(2)}, u32[]{:S(2)}) %all-to-all-start.1) | async-done | bytes 262176 | tf_op jit(solution)/shard_map/all_to_all | solution.py:191
  78.9 0.2 fusion.16
  79.2 1.1 %maximum_bitcast_fusion.1 = (f32[8,8,16,128]{3,1,2,0:T(8,128)S(1)}, f32[8,8,16,128]{3,1,2,0:T(8,128)S(1)}) fusion(f32[32,2048]{1,0:T(8,128)} %get-tuple-element.32, f32[32,2048]{1,0:T(8,128)S(1)} %copy-done.6, f32[32,2048]{1,0:T(8,128)} %get-tuple-element.36, f32[32,2048]{1,0:T(8,128)S(1)} %copy-done.7), kind=kLoop, calls=%fused_computation.27 | loop fusion | flops 262144 | bytes 2097152
  80.5 0.3 copy.44
  80.8 0.3 fusion.19
  81.3 0.3 copy.43
  81.9 0.2 broadcast_multiply_fusion
  82.1 0.2 div.35
  82.3 0.2 mul.88
  82.5 1.2 %fusion.15 = bf16[64,2048]{1,0:T(8,128)(2,1)} fusion(f32[8,8,16,128]{3,2,1,0:T(8,128)S(1)} %bitcast.97, f32[8,8,16,128]{3,2,1,0:T(8,128)S(1)} %bitcast.94, f32[8,8,16,128]{3,2,1,0:T(8,128)S(1)} %bitcast.98, f32[32,2048]{1,0:T(8,128)S(1)} %copy-done.4, f32[32,2048]{1,0:T(8,128)S(1)} %copy-done.3), kind=kLoop, calls=%fused_computation.24 | loop fusion | flops 655360 | bytes 2359296 | tf_op jit(solution)/shard_map/convert_element_type | solution.py:235
  (61 shorter events, 2.1 us)
Async XLA Ops:
  0.6 6.0 %copy-start.8 = (bf16[8192]{0:T(1024)(128)(2,1)S(1)}, bf16[8192]{0:T(1024)(128)(2,1)}, u32[]{:S(2)}) copy-start(bf16[8192]{0:T(1024)(128)(2,1)} %param.12) | copy-start | bytes 49156
  1.7 2.0 %collective-permute-start = (bf16[32,8192]{1,0:T(8,128)(2,1)S(1)}, bf16[32,8192]{1,0:T(8,128)(2,1)S(1)}, u32[]{:S(2)}, u32[]{:S(2)}) collective-permute-start(bf16[32,8192]{1,0:T(8,128)(2,1)S(1)} %dynamic-slice_bitcast_fusion), channel_id=1, source_target_pairs={{0,1},{1,0},{2,3},{3,2},{4,5},{5,4},{6,7},{7,6},{8,9},{9,8},{10,11... | collective-permute-start | bytes 1572872 | tf_op jit(solution)/shard_map/ppermute | solution.py:75
  4.9 14.0 %collective-permute-start.1 = (bf16[32,8192]{1,0:T(8,128)(2,1)S(1)}, bf16[32,8192]{1,0:T(8,128)(2,1)S(1)}, u32[]{:S(2)}, u32[]{:S(2)}) collective-permute-start(bf16[32,8192]{1,0:T(8,128)(2,1)S(1)} %fusion.14), channel_id=1, source_target_pairs={{0,2},{1,3},{2,0},{3,1},{4,6},{5,7},{6,4},{7,5},{8,10},{9,11},{10,... | collective-permute-start | bytes 1572872 | tf_op jit(solution)/shard_map/ppermute | solution.py:75
  6.6 6.4 %copy-start.10 = (s32[64]{0:T(128)S(1)}, s32[64]{0:T(128)}, u32[]{:S(2)}) copy-start(s32[64]{0:T(128)} %param.16) | copy-start | bytes 772
  6.6 12.3 %copy-start.1 = (bf16[1,64,8192]{2,1,0:T(8,128)(2,1)S(1)}, bf16[1,64,8192]{2,1,0:T(8,128)(2,1)}, u32[]{:S(2)}) copy-start(bf16[1,64,8192]{2,1,0:T(8,128)(2,1)} %param.10) | copy-start | bytes 3145732
  20.7 2.2 %collective-permute-start.2 = (bf16[32,10240]{1,0:T(8,128)(2,1)S(1)}, bf16[32,10240]{1,0:T(8,128)(2,1)S(1)}, u32[]{:S(2)}, u32[]{:S(2)}) collective-permute-start(bf16[32,10240]{1,0:T(8,128)(2,1)S(1)} %pad_maximum_fusion), channel_id=1, source_target_pairs={{0,1},{1,0},{2,3},{3,2},{4,5},{5,4},{6,7},{7,6},{8,9},{9,8},{10,11... | collective-permute-start | bytes 1966088 | tf_op jit(solution)/shard_map/ppermute | solution.py:75
  22.9 32.4 %copy-start.9 = (bf16[2048,1024]{1,0:T(8,128)(2,1)S(1)}, bf16[2048,1024]{1,0:T(8,128)(2,1)}, u32[]{:S(2)}) copy-start(bf16[2048,1024]{1,0:T(8,128)(2,1)} %param.14) | copy-start | bytes 12582916
  23.1 36.1 %slice-start = ((s8[8388608]{0:T(1024)(128)(4,1)}), s8[4194304]{0:T(1024)(128)(4,1)S(1)}, s32[]{:S(2)}) async-start(s8[8388608]{0:T(1024)(128)(4,1)} %bitcast.108), calls=%async_computation.2 | async-start | bytes 8388608
  55.3 2.0 %copy-start.2 = (bf16[1024,2,256]{2,1,0:T(2,128)(2,1)S(1)}, bf16[1024,2,256]{2,1,0:T(2,128)(2,1)}, u32[]{:S(2)}) copy-start(bf16[1024,2,256]{2,1,0:T(2,128)(2,1)} %param.15) | copy-start | bytes 3145732
  55.3 3.9 %slice-start.1 = ((s8[8388608]{0:T(1024)(128)(4,1)}), s8[4194304]{0:T(1024)(128)(4,1)S(1)}, s32[]{:S(2)}) async-start(s8[8388608]{0:T(1024)(128)(4,1)} %bitcast.108), calls=%async_computation.3 | async-start | bytes 8388608
  57.1 1.0 %copy-start = (bf16[64,2048]{1,0:T(8,128)(2,1)S(1)}, bf16[64,2048]{1,0:T(8,128)(2,1)}, u32[]{:S(2)}) copy-start(bf16[64,2048]{1,0:T(8,128)(2,1)} %q_ref.3) | copy-start | bytes 786436
  57.2 1.3 %collective-permute-start.3 = (f32[256,64]{0,1:T(8,128)S(1)}, f32[256,64]{0,1:T(8,128)S(1)}, u32[]{:S(2)}, u32[]{:S(2)}) collective-permute-start(f32[256,64]{0,1:T(8,128)S(1)} %select_reduce_fusion), channel_id=1, source_target_pairs={{0,1},{1,0},{2,3},{3,2},{4,5},{5,4},{6,7},{7,6},{8,9},{9,8},{10,11... | collective-permute-start | bytes 196616 | tf_op jit(solution)/shard_map/ppermute | solution.py:75
  58.6 4.3 %collective-permute-start.4 = (f32[256,64]{0,1:T(8,128)S(1)}, f32[256,64]{0,1:T(8,128)S(1)}, u32[]{:S(2)}, u32[]{:S(2)}) collective-permute-start(f32[256,64]{0,1:T(8,128)S(1)} %add.89), channel_id=1, source_target_pairs={{0,2},{1,3},{2,0},{3,1},{4,6},{5,7},{6,4},{7,5},{8,10},{9,11},{10,... | collective-permute-start | bytes 196616 | tf_op jit(solution)/shard_map/ppermute | solution.py:75
  64.1 14.8 %all-to-all-start.1 = ((bf16[32,8,512]{2,1,0:T(8,128)(2,1)}), bf16[32,8,512]{2,1,0:T(8,128)(2,1)S(1)}, u32[]{:S(2)}, u32[]{:S(2)}) async-start(bf16[32,8,512]{2,1,0:T(8,128)(2,1)} %fusion.3), calls=%async_computation.1 | async-start | bytes 524288 | tf_op jit(solution)/shard_map/all_to_all | solution.py:191
  68.0 11.2 %copy-start.6 = (f32[32,2048]{1,0:T(8,128)S(1)}, f32[32,2048]{1,0:T(8,128)}, u32[]{:S(2)}) copy-start(f32[32,2048]{1,0:T(8,128)} %get-tuple-element.31) | copy-start | bytes 786436
  68.0 11.2 %copy-start.7 = (f32[32,2048]{1,0:T(8,128)S(1)}, f32[32,2048]{1,0:T(8,128)}, u32[]{:S(2)}) copy-start(f32[32,2048]{1,0:T(8,128)} %get-tuple-element.35) | copy-start | bytes 786436
  79.2 1.9 %copy-start.5 = (bf16[64,2,256]{2,1,0:T(2,128)(2,1)}, bf16[64,2,256]{2,1,0:T(2,128)(2,1)S(1)}, u32[]{:S(2)}) copy-start(bf16[64,2,256]{2,1,0:T(2,128)(2,1)S(1)} %reshape.120) | copy-start | bytes 196612
  80.8 1.7 %copy-start.3 = (f32[32,2048]{1,0:T(8,128)S(1)}, f32[32,2048]{1,0:T(8,128)}, u32[]{:S(2)}) copy-start(f32[32,2048]{1,0:T(8,128)} %get-tuple-element.33) | copy-start | bytes 786436
  80.8 1.7 %copy-start.4 = (f32[32,2048]{1,0:T(8,128)S(1)}, f32[32,2048]{1,0:T(8,128)}, u32[]{:S(2)}) copy-start(f32[32,2048]{1,0:T(8,128)} %get-tuple-element.34) | copy-start | bytes 786436

commit v4 on v3

--- a/solution.py
+++ b/solution.py
@@ -98,11 +98,16 @@
     head_weight = jnp.transpose(key_value_weight, (1, 0, 2))
 
     half_rows = row_dev // 2
-    part2 = partials[0].reshape(2, half_rows, model_width)
-    mine_p = lax.dynamic_index_in_dim(part2, core, axis=0, keepdims=False)
-    other_p = lax.dynamic_index_in_dim(part2, 1 - core, axis=0, keepdims=False)
-    got_p = _swap(other_p, 1, tensor_count)
-    chip_sum = mine_p.astype(jnp.float32) + got_p.astype(jnp.float32)
+    own_partial = partials[0]
+    rows_lo = own_partial[:half_rows]
+    rows_hi = own_partial[half_rows:]
+    to_core1 = [(i, i ^ 1) for i in range(0, tensor_count, 2)]
+    to_core0 = [(i, i ^ 1) for i in range(1, tensor_count, 2)]
+    got_hi = lax.ppermute(rows_hi, "tensor", perm=to_core1)
+    got_lo = lax.ppermute(rows_lo, "tensor", perm=to_core0)
+    first = core == 0
+    mine_p = jnp.where(first, rows_lo, rows_hi)
+    chip_sum = mine_p.astype(jnp.float32) + (got_lo.astype(jnp.float32) + got_hi.astype(jnp.float32))
     far_sum = _swap(chip_sum.astype(jnp.bfloat16), 2, tensor_count)
     local_prompts = key_value_cache.shape[0]
     early_prompts = local_prompts // 2
@@ -130,7 +135,6 @@
     normed_other = swap_in[:, :model_width]
     hidden_other = swap_in[:, model_width:]
     hidden_mine = lax.dynamic_slice_in_dim(hidden_half, tensor_index * quarter, quarter, 1)
-    first = core == 0
     hidden_part = jnp.where(
         first,
         jnp.concatenate([hidden_mine, hidden_other], axis=0),
@@ -214,25 +218,24 @@
         for early, late in zip(attention_early, attention_late)
     ]
     view = (row_dev, local_heads, group_size, HEAD_SIZE)
-    cache_weighted = num_c.reshape(view)
-    cache_top = top_c.reshape(view)[..., 0]
-    cache_total = tot_c.reshape(view)[..., 0]
-    query_heads = queries.reshape(view)
-    own_key = new_kv[:, :, :HEAD_SIZE]
-    own_value = new_kv[:, :, HEAD_SIZE:]
-    own_score = (
-        jnp.einsum("rkgd,rkd->rkg", query_heads, own_key, preferred_element_type=jnp.float32)
-        * score_scale
-    )
+    flat = (row_dev, local_heads * group_size, HEAD_SIZE)
+    query_wide = queries.reshape(view).astype(jnp.float32)
+    own_key = new_kv[:, :, :HEAD_SIZE].astype(jnp.float32)[:, :, None, :]
+    own_value = jnp.broadcast_to(
+        new_kv[:, :, HEAD_SIZE:].astype(jnp.float32)[:, :, None, :], view
+    ).reshape(flat)
+    own_score = (jnp.sum(query_wide * own_key, axis=-1) * score_scale).reshape(
+        row_dev, local_heads * group_size, 1
+    )
+    cache_weighted = num_c.reshape(flat)
+    cache_top = top_c.reshape(flat)
+    cache_total = tot_c.reshape(flat)
     score_top = jnp.maximum(cache_top, own_score)
     rescale = jnp.exp(cache_top - score_top)
     own_weight = jnp.exp(own_score - score_top).astype(jnp.bfloat16).astype(jnp.float32)
     weight_total = rescale * cache_total + own_weight
-    weighted = (
-        rescale[..., None] * cache_weighted
-        + own_weight[..., None] * own_value.astype(jnp.float32)[:, :, None, :]
-    )
-    attended = (weighted / weight_total[..., None]).astype(jnp.bfloat16).reshape(row_dev, -1)
+    weighted = rescale * cache_weighted + own_weight * own_value
+    attended = (weighted / weight_total).astype(jnp.bfloat16).reshape(row_dev, -1)
     return (hidden_part, new_kv, attended)
 
 

time: 84.2 us -> 93.7 us (1.11)
  starting transfers between devices: 6.48 us -> 11.3 us
  matrix products: 5.48 us -> 8.59 us
  waiting for transfers between devices: 15.9 us -> 18.6 us
  other arithmetic: 7.06 us -> 5.3 us
    all_to_all x1, waiting for transfers between devices: 3.74 us -> 9.14 us  [per_device(): lax.all_to_all(adapter_update, 'adapter', split_axis=0, concat_axis=0, ti...]
    ppermute x0 -> x2, starting transfers between devices: none -> 4.38 us  [the longest x1 3.09 us: per_device(): got_hi = lax.ppermute(rows_hi, 'tensor', perm=to_core1)]
    ppermute x5 -> x4, waiting for transfers between devices: 12.1 us -> 7.95 us  [_swap(): return lax.ppermute(x, 'tensor', perm=[(i, i ^ mask) for i in range(count)])]
    dot_general x1, matrix products: 1.57 us -> 4.95 us  [per_device(): jnp.einsum('rf,hfd->rhd', normed_full, head_weight, preferred_element_typ...]
    ppermute x0 -> x2, waiting for transfers between devices: none -> 1.46 us  [the longest x1 1.46 us: per_device(): got_hi = lax.ppermute(rows_hi, 'tensor', perm=to_core1)]
    slice x0 -> x1, local copies, waits for them, and re-layouts: none -> 1.35 us  [per_device(): rows_lo = own_partial[:half_rows]]
    unnamed x2 -> x1, other arithmetic: 1.13 us -> 0.04 us
    squeeze x1 -> x0, local copies, waits for them, and re-layouts: 1.08 us -> none  [per_device(): other_p = lax.dynamic_index_in_dim(part2, 1 - core, axis=0, keepdims=False)]
  transfers between devices with their start and end apart: 6 -> 7, of which waited for: 6 -> 4; matrix products, arithmetic and copies ran while one was open for 3% -> 8% of each run, Pallas kernels for 15% -> 14%
where the time goes in v4:
time: 93.7 us; the launch traced here: 93.1 us
  blocking collectives  31.3 us (33%)
  waiting for transfers between devices  18.6 us (20%)
  Pallas kernels  12.7 us (14%)
  starting transfers between devices  11.3 us (12%)
  matrix products  8.59 us (9%)
  other arithmetic  5.3 us (6%)
  local copies, waits for them, and re-layouts  4.26 us (5%)
  between operations  1.08 us (1%)
    all_to_all x1, blocking collectives, per_device(): lax.all_to_all(payload, 'adapter', split_axis=0, concat_axis=0, tiled=True)  31.3 us
    pallas_call x2, Pallas kernels, cache_attention(): pl.pallas_call(kernel, out_shape=(out, out, out), grid_spec=pltpu.Prefetc...  12.7 us
    all_to_all x1, waiting for transfers between devices, per_device(): lax.all_to_all(adapter_update, 'adapter', split_axis=0, concat_axis=0, ti...  9.14 us
    ppermute x4, waiting for transfers between devices, _swap(): return lax.ppermute(x, 'tensor', perm=[(i, i ^ mask) for i in range(count)])  7.95 us
    dot_general x1, matrix products, per_device(): jnp.einsum('rf,hfd->rhd', normed_full, head_weight, preferred_element_typ...  4.95 us
    all_to_all x1, starting transfers between devices, per_device(): lax.all_to_all(adapter_update, 'adapter', split_axis=0, concat_axis=0, ti...  4.4 us
    ppermute x1, starting transfers between devices, per_device(): got_hi = lax.ppermute(rows_hi, 'tensor', perm=to_core1)  3.09 us
    ppermute x4, starting transfers between devices, _swap(): return lax.ppermute(x, 'tensor', perm=[(i, i ^ mask) for i in range(count)])  2.52 us
  transfers between devices with their start and end apart: 7, of which 4 were waited for; matrix products, arithmetic and copies ran while one was open for 8% of the time, Pallas kernels for 14%

profile of v4, /device:TPU:0, one launch (start us, length us, event | category | flops | bytes accessed | tf_op | source)
XLA Modules:
  0.0 93.1 jit_solution(17954558328300248300)
XLA Ops:
  0.6 1.4 %slice_bitcast_fusion.1 = (bf16[32,8192]{1,0:T(8,128)(2,1)S(1)}, bf16[32,8192]{1,0:T(8,128)(2,1)S(1)}) fusion(bf16[1,64,8192]{2,1,0:T(8,128)(2,1)} %param.10), kind=kLoop, calls=%fused_computation.38 | loop fusion | bytes 2097152 | tf_op jit(solution)/shard_map/slice | solution.py:102
  2.0 1.3 %collective-permute-start = (bf16[32,8192]{1,0:T(8,128)(2,1)S(1)}, bf16[32,8192]{1,0:T(8,128)(2,1)S(1)}, u32[]{:S(2)}, u32[]{:S(2)}) collective-permute-start(bf16[32,8192]{1,0:T(8,128)(2,1)S(1)} %get-tuple-element.39), channel_id=1, source_target_pairs={{1,0},{3,2},{5,4},{7,6},{9,8},{11,10},{13,12},{15,14},{17,16},{19,... | collective-permute-start | bytes 1572872 | tf_op jit(solution)/shard_map/ppermute | solution.py:107
  3.3 3.1 %collective-permute-start.1 = (bf16[32,8192]{1,0:T(8,128)(2,1)S(1)}, bf16[32,8192]{1,0:T(8,128)(2,1)S(1)}, u32[]{:S(2)}, u32[]{:S(2)}) collective-permute-start(bf16[32,8192]{1,0:T(8,128)(2,1)S(1)} %get-tuple-element.40), channel_id=1, source_target_pairs={{0,1},{2,3},{4,5},{6,7},{8,9},{10,11},{12,13},{14,15},{16,17},{18,... | collective-permute-start | bytes 1572872 | tf_op jit(solution)/shard_map/ppermute | solution.py:106
  6.4 1.5 %collective-permute-done.1 = bf16[32,8192]{1,0:T(8,128)(2,1)S(1)} collective-permute-done((bf16[32,8192]{1,0:T(8,128)(2,1)S(1)}, bf16[32,8192]{1,0:T(8,128)(2,1)S(1)}, u32[]{:S(2)}, u32[]{:S(2)}) %collective-permute-start.1) | collective-permute-done | bytes 524320 | tf_op jit(solution)/shard_map/ppermute | solution.py:106
  7.9 0.3 fusion.14
  8.2 1.7 %collective-permute-start.2 = (bf16[32,8192]{1,0:T(8,128)(2,1)S(1)}, bf16[32,8192]{1,0:T(8,128)(2,1)S(1)}, u32[]{:S(2)}, u32[]{:S(2)}) collective-permute-start(bf16[32,8192]{1,0:T(8,128)(2,1)S(1)} %fusion.14), channel_id=1, source_target_pairs={{0,2},{1,3},{2,0},{3,1},{4,6},{5,7},{6,4},{7,5},{8,10},{9,11},{10,... | collective-permute-start | bytes 1572872 | tf_op jit(solution)/shard_map/ppermute | solution.py:75
  9.9 6.4 %shard_map.121 = (f32[32,2048]{1,0:T(8,128)}, f32[32,2048]{1,0:T(8,128)}, f32[32,2048]{1,0:T(8,128)}) custom-call(s32[8]{0:T(128)} %len_ref.3, bf16[64,2048]{1,0:T(8,128)(2,1)} %q_ref.3, bf16[8,2,1024,256]{3,2,1,0:T(8,128)(2,1)} %v_ref.3, bf16[8,2,1024,256]{3,2,1,0:T(8,128)(2,1)} %v_ref.3), custom_call_target="tpu_custom_call" | custom-call | flops 268435456 | bytes 5111808 | tf_op jit(solution)/shard_map/pallas_call | solution.py:53
  16.3 6.2 %collective-permute-done.2 = bf16[32,8192]{1,0:T(8,128)(2,1)S(1)} collective-permute-done((bf16[32,8192]{1,0:T(8,128)(2,1)S(1)}, bf16[32,8192]{1,0:T(8,128)(2,1)S(1)}, u32[]{:S(2)}, u32[]{:S(2)}) %collective-permute-start.2) | collective-permute-done | bytes 524320 | tf_op jit(solution)/shard_map/ppermute | solution.py:75
  22.4 1.6 %fusion.7 = (f32[32]{0:T(128)S(1)}, bf16[32,8192]{1,0:T(8,128)(2,1)S(1)}) fusion(bf16[32,8192]{1,0:T(8,128)(2,1)S(1)} %collective-permute-done.2, bf16[32,8192]{1,0:T(8,128)(2,1)S(1)} %collective-permute-done.1, bf16[32,8192]{1,0:T(8,128)(2,1)S(1)} %collective-permute-done, bf16[1,64,8192]{2,1,0:T(8,128)(2,1)S(1)} %copy-done, pred[]{:T(512)S(6)} %eq.50, ...), kind=kLoop, calls=%fused_computation.10 | loop fusion | flops 3669984 | bytes 3670149 | tf_op jit(solution)/shard_map/reduce_sum | solution.py:127
  24.1 0.2 fusion.9
  24.4 0.2 convert_reduce_fusion.1
  24.6 0.1 select_reduce_fusion.1
  24.7 1.8 %collective-permute-done.3 = bf16[32,10240]{1,0:T(8,128)(2,1)S(1)} collective-permute-done((bf16[32,10240]{1,0:T(8,128)(2,1)S(1)}, bf16[32,10240]{1,0:T(8,128)(2,1)S(1)}, u32[]{:S(2)}, u32[]{:S(2)}) %collective-permute-start.3) | collective-permute-done | bytes 655392 | tf_op jit(solution)/shard_map/ppermute | solution.py:75
  26.6 0.2 maximum_select_fusion
  26.8 0.5 convolution_convert_fusion
  27.5 31.3 %all_to_all.10 = bf16[32,8,2176]{2,1,0:T(8,128)(2,1)S(1)} all-to-all(bf16[32,8,2176]{2,1,0:T(8,128)(2,1)S(1)} %maximum_bitcast_fusion), channel_id=1, replica_groups=mesh['adapter'=32,'tensor'=4] {'adapter'}, dimensions={0} | all-to-all | bytes 2228224 | tf_op jit(solution)/shard_map/all_to_all | solution.py:175
  58.8 0.1 convert_reduce_fusion
  59.0 1.7 %fusion.10 = f32[256,1024]{0,1:T(8,128)S(1)} fusion(bf16[2048,1024]{1,0:T(8,128)(2,1)S(1)} %copy-done.10, bf16[256,2176]{1,0:T(8,128)(2,1)S(1)} %bitcast.63), kind=kOutput, calls=%fused_computation.13 | convolution fusion | flops 1073741824 | bytes 6291456 | tf_op jit(solution)/shard_map/dot_general | solution.py:181
  61.0 1.0 %copy-done.2 = bf16[1024,2,256]{2,1,0:T(2,128)(2,1)S(1)} copy-done((bf16[1024,2,256]{2,1,0:T(2,128)(2,1)S(1)}, bf16[1024,2,256]{2,1,0:T(2,128)(2,1)}, u32[]{:S(2)}) %copy-start.2) | copy-done | bytes 1048600
  62.0 0.2 copy.40
  62.3 6.3 %shard_map.122 = (f32[32,2048]{1,0:T(8,128)}, f32[32,2048]{1,0:T(8,128)}, f32[32,2048]{1,0:T(8,128)}) custom-call(s32[8]{0:T(128)} %len_ref.3, bf16[64,2048]{1,0:T(8,128)(2,1)} %q_ref.3, bf16[8,2,1024,256]{3,2,1,0:T(8,128)(2,1)} %v_ref.3, bf16[8,2,1024,256]{3,2,1,0:T(8,128)(2,1)} %v_ref.3), custom_call_target="tpu_custom_call" | custom-call | flops 268435456 | bytes 5111808 | tf_op jit(solution)/shard_map/pallas_call | solution.py:53
  68.6 0.7 collective-permute-start.5
  69.3 4.9 %fusion.4 = f32[2,8,8,256]{3,2,1,0:T(8,128)S(1)} fusion(bf16[2,8192,256]{2,0,1:T(2,128)(2,1)} %bitcast.70, bf16[64,8192]{1,0:T(8,128)(2,1)S(1)} %maximum_select_fusion), kind=kOutput, calls=%fused_computation.8 | convolution fusion | flops 536870912 | bytes 9568256 | tf_op jit(solution)/shard_map/rf,hfd->rhd/dot_general | solution.py:149
  74.3 1.2 %fusion.3 = bf16[32,8,512]{2,1,0:T(8,128)(2,1)} fusion(bf16[256,1024]{0,1:T(8,128)(2,1)S(1)} %bitcast.67, bf16[1024,512]{1,0:T(8,128)(2,1)S(1)} %bitcast.65), kind=kOutput, calls=%fused_computation.7 | convolution fusion | flops 268697600 | bytes 1835008 | tf_op jit(solution)/shard_map/dot_general | solution.py:192
  75.5 4.4 %all-to-all-start.1 = ((bf16[32,8,512]{2,1,0:T(8,128)(2,1)}), bf16[32,8,512]{2,1,0:T(8,128)(2,1)S(1)}, u32[]{:S(2)}, u32[]{:S(2)}) async-start(bf16[32,8,512]{2,1,0:T(8,128)(2,1)} %fusion.3), calls=%async_computation.1 | async-start | bytes 524288 | tf_op jit(solution)/shard_map/all_to_all | solution.py:195
  79.9 1.0 %constant_dynamic-update-slice_fusion.1 = f32[64,2048]{1,0:T(8,128)S(1)} fusion(f32[32,2048]{1,0:T(8,128)} %get-tuple-element.31), kind=kLoop, calls=%fused_computation.60 | loop fusion | bytes 524288
  80.9 0.8 maximum_select_fusion.1
  81.7 9.1 %all-to-all-done.1 = bf16[32,8,512]{2,1,0:T(8,128)(2,1)S(1)} async-done(((bf16[32,8,512]{2,1,0:T(8,128)(2,1)}), bf16[32,8,512]{2,1,0:T(8,128)(2,1)S(1)}, u32[]{:S(2)}, u32[]{:S(2)}) %all-to-all-start.1) | async-done | bytes 262176 | tf_op jit(solution)/shard_map/all_to_all | solution.py:195
  90.8 0.2 fusion.21
  91.1 0.3 multiply_reduce_fusion
  91.6 0.2 max.11
  91.9 1.2 %fusion.17 = bf16[64,2048]{1,0:T(8,128)(2,1)} fusion(f32[8,8,16,128]{3,2,1,0:T(8,128)S(1)} %bitcast.61, f32[32,2048]{1,0:T(8,128)S(1)} %copy-done.7, f32[32,2048]{1,0:T(8,128)S(1)} %copy-done.5, f32[64,2048]{1,0:T(8,128)S(1)} %constant_dynamic-update-slice_fusion, f32[32,2048]{1,0:T(8,128)S(1)} %copy-done.8, f32[32,2048]{1,0:T(8,128)S(1)} %copy-done.6, ...), kind=kLoop, calls=%fused_computation.29 | loop fusion | flops 1835008 | bytes 2883584 | tf_op jit(solution)/shard_map/convert_element_type | solution.py:238
  (55 shorter events, 1.2 us)
Async XLA Ops:
  0.6 7.3 %copy-start = (bf16[1,64,8192]{2,1,0:T(8,128)(2,1)S(1)}, bf16[1,64,8192]{2,1,0:T(8,128)(2,1)}, u32[]{:S(2)}) copy-start(bf16[1,64,8192]{2,1,0:T(8,128)(2,1)} %param.10) | copy-start | bytes 3145732
  0.6 9.2 %copy-start.9 = (bf16[8192]{0:T(1024)(128)(2,1)S(1)}, bf16[8192]{0:T(1024)(128)(2,1)}, u32[]{:S(2)}) copy-start(bf16[8192]{0:T(1024)(128)(2,1)} %param.12) | copy-start | bytes 49156
  2.0 4.4 %collective-permute-start = (bf16[32,8192]{1,0:T(8,128)(2,1)S(1)}, bf16[32,8192]{1,0:T(8,128)(2,1)S(1)}, u32[]{:S(2)}, u32[]{:S(2)}) collective-permute-start(bf16[32,8192]{1,0:T(8,128)(2,1)S(1)} %get-tuple-element.39), channel_id=1, source_target_pairs={{1,0},{3,2},{5,4},{7,6},{9,8},{11,10},{13,12},{15,14},{17,16},{19,... | collective-permute-start | bytes 1572872 | tf_op jit(solution)/shard_map/ppermute | solution.py:107
  3.3 4.6 %collective-permute-start.1 = (bf16[32,8192]{1,0:T(8,128)(2,1)S(1)}, bf16[32,8192]{1,0:T(8,128)(2,1)S(1)}, u32[]{:S(2)}, u32[]{:S(2)}) collective-permute-start(bf16[32,8192]{1,0:T(8,128)(2,1)S(1)} %get-tuple-element.40), channel_id=1, source_target_pairs={{0,1},{2,3},{4,5},{6,7},{8,9},{10,11},{12,13},{14,15},{16,17},{18,... | collective-permute-start | bytes 1572872 | tf_op jit(solution)/shard_map/ppermute | solution.py:106
  8.2 14.3 %collective-permute-start.2 = (bf16[32,8192]{1,0:T(8,128)(2,1)S(1)}, bf16[32,8192]{1,0:T(8,128)(2,1)S(1)}, u32[]{:S(2)}, u32[]{:S(2)}) collective-permute-start(bf16[32,8192]{1,0:T(8,128)(2,1)S(1)} %fusion.14), channel_id=1, source_target_pairs={{0,2},{1,3},{2,0},{3,1},{4,6},{5,7},{6,4},{7,5},{8,10},{9,11},{10,... | collective-permute-start | bytes 1572872 | tf_op jit(solution)/shard_map/ppermute | solution.py:75
  9.8 6.4 %copy-start.11 = (s32[64]{0:T(128)S(1)}, s32[64]{0:T(128)}, u32[]{:S(2)}) copy-start(s32[64]{0:T(128)} %param.16) | copy-start | bytes 772
  24.4 2.2 %collective-permute-start.3 = (bf16[32,10240]{1,0:T(8,128)(2,1)S(1)}, bf16[32,10240]{1,0:T(8,128)(2,1)S(1)}, u32[]{:S(2)}, u32[]{:S(2)}) collective-permute-start(bf16[32,10240]{1,0:T(8,128)(2,1)S(1)} %pad_maximum_fusion), channel_id=1, source_target_pairs={{0,1},{1,0},{2,3},{3,2},{4,5},{5,4},{6,7},{7,6},{8,9},{9,8},{10,11... | collective-permute-start | bytes 1966088 | tf_op jit(solution)/shard_map/ppermute | solution.py:75
  27.4 31.6 %copy-start.10 = (bf16[2048,1024]{1,0:T(8,128)(2,1)S(1)}, bf16[2048,1024]{1,0:T(8,128)(2,1)}, u32[]{:S(2)}) copy-start(bf16[2048,1024]{1,0:T(8,128)(2,1)} %param.14) | copy-start | bytes 12582916
  59.0 2.0 %copy-start.1 = (bf16[64,2048]{1,0:T(8,128)(2,1)S(1)}, bf16[64,2048]{1,0:T(8,128)(2,1)}, u32[]{:S(2)}) copy-start(bf16[64,2048]{1,0:T(8,128)(2,1)} %q_ref.3) | copy-start | bytes 786436
  60.7 1.2 %copy-start.2 = (bf16[1024,2,256]{2,1,0:T(2,128)(2,1)S(1)}, bf16[1024,2,256]{2,1,0:T(2,128)(2,1)}, u32[]{:S(2)}) copy-start(bf16[1024,2,256]{2,1,0:T(2,128)(2,1)} %param.15) | copy-start | bytes 3145732
  60.8 7.7 %collective-permute-start.4 = (f32[256,64]{0,1:T(8,128)S(1)}, f32[256,64]{0,1:T(8,128)S(1)}, u32[]{:S(2)}, u32[]{:S(2)}) collective-permute-start(f32[256,64]{0,1:T(8,128)S(1)} %select_reduce_fusion), channel_id=1, source_target_pairs={{0,1},{1,0},{2,3},{3,2},{4,5},{5,4},{6,7},{7,6},{8,9},{9,8},{10,11... | collective-permute-start | bytes 196616 | tf_op jit(solution)/shard_map/ppermute | solution.py:75
  68.6 5.6 %collective-permute-start.5 = (f32[256,64]{0,1:T(8,128)S(1)}, f32[256,64]{0,1:T(8,128)S(1)}, u32[]{:S(2)}, u32[]{:S(2)}) collective-permute-start(f32[256,64]{0,1:T(8,128)S(1)} %add.88), channel_id=1, source_target_pairs={{0,2},{1,3},{2,0},{3,1},{4,6},{5,7},{6,4},{7,5},{8,10},{9,11},{10,... | collective-permute-start | bytes 196616 | tf_op jit(solution)/shard_map/ppermute | solution.py:75
  75.5 16.1 %copy-start.4 = (f32[32,2048]{1,0:T(8,128)S(1)}, f32[32,2048]{1,0:T(8,128)}, u32[]{:S(2)}) copy-start(f32[32,2048]{1,0:T(8,128)} %get-tuple-element.32) | copy-start | bytes 786436
  75.5 15.3 %all-to-all-start.1 = ((bf16[32,8,512]{2,1,0:T(8,128)(2,1)}), bf16[32,8,512]{2,1,0:T(8,128)(2,1)S(1)}, u32[]{:S(2)}, u32[]{:S(2)}) async-start(bf16[32,8,512]{2,1,0:T(8,128)(2,1)} %fusion.3), calls=%async_computation.1 | async-start | bytes 524288 | tf_op jit(solution)/shard_map/all_to_all | solution.py:195
  80.9 11.0 %copy-start.5 = (f32[32,2048]{1,0:T(8,128)S(1)}, f32[32,2048]{1,0:T(8,128)}, u32[]{:S(2)}) copy-start(f32[32,2048]{1,0:T(8,128)} %get-tuple-element.33) | copy-start | bytes 786436
  80.9 11.0 %copy-start.6 = (f32[32,2048]{1,0:T(8,128)S(1)}, f32[32,2048]{1,0:T(8,128)}, u32[]{:S(2)}) copy-start(f32[32,2048]{1,0:T(8,128)} %get-tuple-element.35) | copy-start | bytes 786436
  80.9 11.0 %copy-start.7 = (f32[32,2048]{1,0:T(8,128)S(1)}, f32[32,2048]{1,0:T(8,128)}, u32[]{:S(2)}) copy-start(f32[32,2048]{1,0:T(8,128)} %get-tuple-element.34) | copy-start | bytes 786436
  80.9 11.0 %copy-start.8 = (f32[32,2048]{1,0:T(8,128)S(1)}, f32[32,2048]{1,0:T(8,128)}, u32[]{:S(2)}) copy-start(f32[32,2048]{1,0:T(8,128)} %get-tuple-element.36) | copy-start | bytes 786436
  91.1 2.0 %copy-start.3 = (bf16[64,2,256]{2,1,0:T(2,128)(2,1)}, bf16[64,2,256]{2,1,0:T(2,128)(2,1)S(1)}, u32[]{:S(2)}) copy-start(bf16[64,2,256]{2,1,0:T(2,128)(2,1)S(1)} %reshape.123) | copy-start | bytes 196612

commit v5 on v4

--- a/solution.py
+++ b/solution.py
@@ -98,16 +98,11 @@
     head_weight = jnp.transpose(key_value_weight, (1, 0, 2))
 
     half_rows = row_dev // 2
-    own_partial = partials[0]
-    rows_lo = own_partial[:half_rows]
-    rows_hi = own_partial[half_rows:]
-    to_core1 = [(i, i ^ 1) for i in range(0, tensor_count, 2)]
-    to_core0 = [(i, i ^ 1) for i in range(1, tensor_count, 2)]
-    got_hi = lax.ppermute(rows_hi, "tensor", perm=to_core1)
-    got_lo = lax.ppermute(rows_lo, "tensor", perm=to_core0)
-    first = core == 0
-    mine_p = jnp.where(first, rows_lo, rows_hi)
-    chip_sum = mine_p.astype(jnp.float32) + (got_lo.astype(jnp.float32) + got_hi.astype(jnp.float32))
+    part2 = partials[0].reshape(2, half_rows, model_width)
+    mine_p = lax.dynamic_index_in_dim(part2, core, axis=0, keepdims=False)
+    other_p = lax.dynamic_index_in_dim(part2, 1 - core, axis=0, keepdims=False)
+    got_p = _swap(other_p, 1, tensor_count)
+    chip_sum = mine_p.astype(jnp.float32) + got_p.astype(jnp.float32)
     far_sum = _swap(chip_sum.astype(jnp.bfloat16), 2, tensor_count)
     local_prompts = key_value_cache.shape[0]
     early_prompts = local_prompts // 2
@@ -135,6 +130,7 @@
     normed_other = swap_in[:, :model_width]
     hidden_other = swap_in[:, model_width:]
     hidden_mine = lax.dynamic_slice_in_dim(hidden_half, tensor_index * quarter, quarter, 1)
+    first = core == 0
     hidden_part = jnp.where(
         first,
         jnp.concatenate([hidden_mine, hidden_other], axis=0),
@@ -193,8 +189,9 @@
     ).astype(jnp.bfloat16)
     adapter_update = adapter_update.reshape(adapt_count, item_count, -1)
     returned = lax.all_to_all(adapter_update, "adapter", split_axis=0, concat_axis=0, tiled=True)
+    adapter_update, queries_late = lax.optimization_barrier((adapter_update, queries))
     attention_late = cache_attention(
-        queries,
+        queries_late,
         key_value_cache,
         prompt_cache_length,
         local_heads,

time: 93.7 us -> 87.9 us (0.938)
  blocking collectives: 31.3 us -> 0 us
  waiting for transfers between devices: 18.6 us -> 32.6 us
  starting transfers between devices: 11.3 us -> 17.8 us
  matrix products: 8.59 us -> 10.8 us
  other arithmetic: 5.3 us -> 7.12 us
    all_to_all x1 -> x0, blocking collectives: 31.3 us -> none  [per_device(): lax.all_to_all(payload, 'adapter', split_axis=0, concat_axis=0, tiled=True)]
    all_to_all x0 -> x1, waiting for transfers between devices: none -> 17.9 us  [per_device(): lax.all_to_all(payload, 'adapter', split_axis=0, concat_axis=0, tiled=True)]
    all_to_all x0 -> x1, starting transfers between devices: none -> 10.9 us  [per_device(): lax.all_to_all(payload, 'adapter', split_axis=0, concat_axis=0, tiled=True)]
    all_to_all x1, waiting for transfers between devices: 9.14 us -> 3.9 us  [per_device(): lax.all_to_all(adapter_update, 'adapter', split_axis=0, concat_axis=0, ti...]
    ppermute x2 -> x0, starting transfers between devices: 4.38 us -> none  [the longest x1 3.09 us: per_device(): got_hi = lax.ppermute(rows_hi, 'tensor', perm=to_core1)]
    ppermute x4 -> x5, waiting for transfers between devices: 7.95 us -> 10.8 us  [_swap(): return lax.ppermute(x, 'tensor', perm=[(i, i ^ mask) for i in range(count)])]
    dot_general x1, matrix products: 1.74 us -> 3.97 us  [per_device(): jnp.dot(flattened_rows, adapter_down_weight, preferred_element_type=jnp.f...]
    ppermute x2 -> x0, waiting for transfers between devices: 1.46 us -> none  [the longest x1 1.46 us: per_device(): got_hi = lax.ppermute(rows_hi, 'tensor', perm=to_core1)]
  transfers between devices with their start and end apart: 7 -> 7, of which waited for: 4 -> 6; matrix products, arithmetic and copies ran while one was open for 8% -> 8% of each run, Pallas kernels for 14% -> 15%
where the time goes in v5:
time: 87.9 us; the launch traced here: 87.2 us
  waiting for transfers between devices  32.6 us (37%)
  starting transfers between devices  17.8 us (20%)
  Pallas kernels  12.7 us (14%)
  matrix products  10.8 us (12%)
  other arithmetic  7.12 us (8%)
  local copies, waits for them, and re-layouts  5.1 us (6%)
  between operations  1.06 us (1%)
    all_to_all x1, waiting for transfers between devices, per_device(): lax.all_to_all(payload, 'adapter', split_axis=0, concat_axis=0, tiled=True)  17.9 us
    pallas_call x2, Pallas kernels, cache_attention(): pl.pallas_call(kernel, out_shape=(out, out, out), grid_spec=pltpu.Prefetc...  12.7 us
    all_to_all x1, starting transfers between devices, per_device(): lax.all_to_all(payload, 'adapter', split_axis=0, concat_axis=0, tiled=True)  10.9 us
    ppermute x5, waiting for transfers between devices, _swap(): return lax.ppermute(x, 'tensor', perm=[(i, i ^ mask) for i in range(count)])  10.8 us
    dot_general x1, matrix products, per_device(): jnp.einsum('rf,hfd->rhd', normed_full, head_weight, preferred_element_typ...  4.95 us
    all_to_all x1, starting transfers between devices, per_device(): lax.all_to_all(adapter_update, 'adapter', split_axis=0, concat_axis=0, ti...  4.32 us
    dot_general x1, matrix products, per_device(): jnp.dot(flattened_rows, adapter_down_weight, preferred_element_type=jnp.f...  3.97 us
    all_to_all x1, waiting for transfers between devices, per_device(): lax.all_to_all(adapter_update, 'adapter', split_axis=0, concat_axis=0, ti...  3.9 us
  transfers between devices with their start and end apart: 7, of which 6 were waited for; matrix products, arithmetic and copies ran while one was open for 8% of the time, Pallas kernels for 15%

profile of v5, /device:TPU:0, one launch (start us, length us, event | category | flops | bytes accessed | tf_op | source)
XLA Modules:
  0.0 87.2 jit_solution(8178311165142861762)
XLA Ops:
  0.7 1.1 %dynamic-slice_bitcast_fusion = bf16[32,8192]{1,0:T(8,128)(2,1)S(1)} fusion(bf16[2,32,8192]{2,1,0:T(8,128)(2,1)} %bitcast.53, s32[]{:T(128)S(6)} %select_n.74), kind=kLoop, calls=%fused_computation.37 | loop fusion | bytes 1048580 | tf_op jit(solution)/shard_map/jit(dynamic_index_in_dim)/squeeze | solution.py:103
  1.8 1.9 %collective-permute-done = bf16[32,8192]{1,0:T(8,128)(2,1)S(1)} collective-permute-done((bf16[32,8192]{1,0:T(8,128)(2,1)S(1)}, bf16[32,8192]{1,0:T(8,128)(2,1)S(1)}, u32[]{:S(2)}, u32[]{:S(2)}) %collective-permute-start) | collective-permute-done | bytes 524320 | tf_op jit(solution)/shard_map/ppermute | solution.py:75
  3.7 1.2 %fusion.14 = bf16[32,8192]{1,0:T(8,128)(2,1)S(1)} fusion(bf16[32,8192]{1,0:T(8,128)(2,1)S(1)} %collective-permute-done, bf16[2,32,8192]{2,1,0:T(8,128)(2,1)} %bitcast.54, s32[]{:T(128)S(6)} %select_n.73), kind=kLoop, calls=%fused_computation.21 | loop fusion | flops 1048576 | bytes 1572868 | tf_op jit(solution)/shard_map/convert_element_type | solution.py:106
  4.9 1.7 %collective-permute-start.1 = (bf16[32,8192]{1,0:T(8,128)(2,1)S(1)}, bf16[32,8192]{1,0:T(8,128)(2,1)S(1)}, u32[]{:S(2)}, u32[]{:S(2)}) collective-permute-start(bf16[32,8192]{1,0:T(8,128)(2,1)S(1)} %fusion.14), channel_id=1, source_target_pairs={{0,2},{1,3},{2,0},{3,1},{4,6},{5,7},{6,4},{7,5},{8,10},{9,11},{10,... | collective-permute-start | bytes 1572872 | tf_op jit(solution)/shard_map/ppermute | solution.py:75
  6.6 6.4 %shard_map.121 = (f32[32,2048]{1,0:T(8,128)}, f32[32,2048]{1,0:T(8,128)}, f32[32,2048]{1,0:T(8,128)}) custom-call(s32[8]{0:T(128)} %len_ref.3, bf16[64,2048]{1,0:T(8,128)(2,1)} %q_ref.2, bf16[8,2,1024,256]{3,2,1,0:T(8,128)(2,1)} %v_ref.3, bf16[8,2,1024,256]{3,2,1,0:T(8,128)(2,1)} %v_ref.3), custom_call_target="tpu_custom_call" | custom-call | flops 268435456 | bytes 5111808 | tf_op jit(solution)/shard_map/pallas_call | solution.py:53
  13.0 5.9 %collective-permute-done.1 = bf16[32,8192]{1,0:T(8,128)(2,1)S(1)} collective-permute-done((bf16[32,8192]{1,0:T(8,128)(2,1)S(1)}, bf16[32,8192]{1,0:T(8,128)(2,1)S(1)}, u32[]{:S(2)}, u32[]{:S(2)}) %collective-permute-start.1) | collective-permute-done | bytes 524320 | tf_op jit(solution)/shard_map/ppermute | solution.py:75
  18.9 1.5 %fusion.7 = (f32[32]{0:T(128)S(1)}, bf16[32,8192]{1,0:T(8,128)(2,1)S(1)}) fusion(bf16[32,8192]{1,0:T(8,128)(2,1)S(1)} %collective-permute-done.1, bf16[32,8192]{1,0:T(8,128)(2,1)S(1)} %collective-permute-done, bf16[2,32,8192]{2,1,0:T(8,128)(2,1)S(1)} %bitcast.55, s32[]{:T(128)S(6)} %select_n.73, bf16[2,32,8192]{2,1,0:T(8,128)(2,1)} %bitcast.66), kind=kLoop, calls=%fused_computation.10 | loop fusion | flops 2883552 | bytes 2621572 | tf_op jit(solution)/shard_map/reduce_sum | solution.py:122
  20.5 0.2 fusion.9
  20.8 0.2 convert_reduce_fusion.1
  21.1 1.8 %collective-permute-done.2 = bf16[32,10240]{1,0:T(8,128)(2,1)S(1)} collective-permute-done((bf16[32,10240]{1,0:T(8,128)(2,1)S(1)}, bf16[32,10240]{1,0:T(8,128)(2,1)S(1)}, u32[]{:S(2)}, u32[]{:S(2)}) %collective-permute-start.2) | collective-permute-done | bytes 655392 | tf_op jit(solution)/shard_map/ppermute | solution.py:75
  22.9 0.2 maximum_select_fusion
  23.1 0.5 convolution_convert_fusion
  23.8 1.1 %maximum_bitcast_fusion = bf16[32,8,2176]{2,1,0:T(8,128)(2,1)} fusion(bf16[256,128]{1,0:T(8,128)(2,1)S(1)} %broadcast_in_dim.48, bf16[256,2048]{1,0:T(8,128)(2,1)S(1)} %convolution_convert_fusion), kind=kLoop, calls=%fused_computation.9 | loop fusion | flops 2228224 | bytes 2228224 | tf_op jit(solution)/shard_map/reshape | solution.py:167
  24.9 10.9 %all-to-all-start = ((bf16[32,8,2176]{2,1,0:T(8,128)(2,1)}), bf16[32,8,2176]{2,1,0:T(8,128)(2,1)S(1)}, u32[]{:S(2)}, u32[]{:S(2)}) async-start(bf16[32,8,2176]{2,1,0:T(8,128)(2,1)} %maximum_bitcast_fusion), calls=%async_computation | async-start | bytes 2228224 | tf_op jit(solution)/shard_map/all_to_all | solution.py:171
  35.9 1.1 %copy-done.2 = bf16[1024,2,256]{2,1,0:T(2,128)(2,1)S(1)} copy-done((bf16[1024,2,256]{2,1,0:T(2,128)(2,1)S(1)}, bf16[1024,2,256]{2,1,0:T(2,128)(2,1)}, u32[]{:S(2)}) %copy-start.2) | copy-done | bytes 1048600
  37.0 1.2 %copy.40 = bf16[128,8,2,256]{3,1,2,0:T(8,128)(2,1)} copy(bf16[128,8,2,256]{3,2,1,0:T(2,128)(2,1)S(1)} %bitcast.61) | data formatting | bytes 2097152
  38.2 17.9 %all-to-all-done = bf16[32,8,2176]{2,1,0:T(8,128)(2,1)S(1)} async-done(((bf16[32,8,2176]{2,1,0:T(8,128)(2,1)}), bf16[32,8,2176]{2,1,0:T(8,128)(2,1)S(1)}, u32[]{:S(2)}, u32[]{:S(2)}) %all-to-all-start) | async-done | bytes 1114144 | tf_op jit(solution)/shard_map/all_to_all | solution.py:171
  56.1 0.1 convert_reduce_fusion
  56.2 4.0 %fusion.10 = f32[256,1024]{0,1:T(8,128)S(1)} fusion(bf16[2048,1024]{1,0:T(8,128)(2,1)} %param.14, bf16[256,2176]{1,0:T(8,128)(2,1)S(1)} %bitcast.60), kind=kOutput, calls=%fused_computation.13 | convolution fusion | flops 1073741824 | bytes 6291456 | tf_op jit(solution)/shard_map/dot_general | solution.py:177
  60.5 1.2 %collective-permute-done.3 = f32[256,64]{0,1:T(8,128)S(1)} collective-permute-done((f32[256,64]{0,1:T(8,128)S(1)}, f32[256,64]{0,1:T(8,128)S(1)}, u32[]{:S(2)}, u32[]{:S(2)}) %collective-permute-start.3) | collective-permute-done | bytes 65568 | tf_op jit(solution)/shard_map/ppermute | solution.py:75
  61.7 0.7 collective-permute-start.4
  62.4 4.9 %fusion.4 = f32[2,8,8,256]{3,2,1,0:T(8,128)S(1)} fusion(bf16[2,8192,256]{2,0,1:T(2,128)(2,1)} %bitcast.67, bf16[64,8192]{1,0:T(8,128)(2,1)S(1)} %maximum_select_fusion), kind=kOutput, calls=%fused_computation.8 | convolution fusion | flops 536870912 | bytes 9568256 | tf_op jit(solution)/shard_map/rf,hfd->rhd/dot_general | solution.py:145
  67.4 1.2 %fusion.3 = bf16[32,8,512]{2,1,0:T(8,128)(2,1)} fusion(bf16[256,1024]{0,1:T(8,128)(2,1)S(1)} %bitcast.64, bf16[1024,512]{1,0:T(8,128)(2,1)S(1)} %bitcast.62), kind=kOutput, calls=%fused_computation.7 | convolution fusion | flops 268697600 | bytes 1835008 | tf_op jit(solution)/shard_map/dot_general | solution.py:188
  68.6 4.3 %all-to-all-start.1 = ((bf16[32,8,512]{2,1,0:T(8,128)(2,1)}), bf16[32,8,512]{2,1,0:T(8,128)(2,1)S(1)}, u32[]{:S(2)}, u32[]{:S(2)}) async-start(bf16[32,8,512]{2,1,0:T(8,128)(2,1)} %fusion.3), calls=%async_computation.1 | async-start | bytes 524288 | tf_op jit(solution)/shard_map/all_to_all | solution.py:191
  72.9 0.8 maximum_select_fusion.1
  73.7 6.3 %shard_map.122 = (f32[32,2048]{1,0:T(8,128)}, f32[32,2048]{1,0:T(8,128)}, f32[32,2048]{1,0:T(8,128)}) custom-call(s32[8]{0:T(128)} %len_ref.3, bf16[64,2048]{1,0:T(8,128)(2,1)} %q_ref.2, bf16[8,2,1024,256]{3,2,1,0:T(8,128)(2,1)} %v_ref.3, bf16[8,2,1024,256]{3,2,1,0:T(8,128)(2,1)} %v_ref.3), custom_call_target="tpu_custom_call" | custom-call | flops 268435456 | bytes 5111808 | tf_op jit(solution)/shard_map/pallas_call | solution.py:53
  80.0 3.9 %all-to-all-done.1 = bf16[32,8,512]{2,1,0:T(8,128)(2,1)S(1)} async-done(((bf16[32,8,512]{2,1,0:T(8,128)(2,1)}), bf16[32,8,512]{2,1,0:T(8,128)(2,1)S(1)}, u32[]{:S(2)}, u32[]{:S(2)}) %all-to-all-start.1) | async-done | bytes 262176 | tf_op jit(solution)/shard_map/all_to_all | solution.py:191
  83.9 0.2 fusion.21
  84.2 0.3 multiply_reduce_fusion
  84.6 1.0 %constant_dynamic-update-slice_fusion = f32[64,2048]{1,0:T(8,128)S(1)} fusion(f32[64,2048]{1,0:T(8,128)S(1)} %constant_dynamic-update-slice_fusion.1, f32[32,2048]{1,0:T(8,128)} %get-tuple-element.34), kind=kLoop, calls=%fused_computation.57 | loop fusion | bytes 524288 | tf_op jit(solution)/shard_map/concatenate | solution.py:214
  85.6 0.2 max.11
  85.9 1.3 %fusion.17 = bf16[64,2048]{1,0:T(8,128)(2,1)} fusion(f32[8,8,16,128]{3,2,1,0:T(8,128)S(1)} %bitcast.58, f32[32,2048]{1,0:T(8,128)S(1)} %copy-done.9, f32[32,2048]{1,0:T(8,128)S(1)} %copy-done.7, f32[64,2048]{1,0:T(8,128)S(1)} %constant_dynamic-update-slice_fusion, f32[32,2048]{1,0:T(8,128)S(1)} %copy-done.10, f32[32,2048]{1,0:T(8,128)S(1)} %copy-done.8, ...), kind=kLoop, calls=%fused_computation.29 | loop fusion | flops 1835008 | bytes 2883584 | tf_op jit(solution)/shard_map/convert_element_type | solution.py:235
  (57 shorter events, 1.3 us)
Async XLA Ops:
  0.6 6.0 %copy-start.11 = (bf16[8192]{0:T(1024)(128)(2,1)S(1)}, bf16[8192]{0:T(1024)(128)(2,1)}, u32[]{:S(2)}) copy-start(bf16[8192]{0:T(1024)(128)(2,1)} %param.12) | copy-start | bytes 49156
  1.7 2.0 %collective-permute-start = (bf16[32,8192]{1,0:T(8,128)(2,1)S(1)}, bf16[32,8192]{1,0:T(8,128)(2,1)S(1)}, u32[]{:S(2)}, u32[]{:S(2)}) collective-permute-start(bf16[32,8192]{1,0:T(8,128)(2,1)S(1)} %dynamic-slice_bitcast_fusion), channel_id=1, source_target_pairs={{0,1},{1,0},{2,3},{3,2},{4,5},{5,4},{6,7},{7,6},{8,9},{9,8},{10,11... | collective-permute-start | bytes 1572872 | tf_op jit(solution)/shard_map/ppermute | solution.py:75
  4.9 14.0 %collective-permute-start.1 = (bf16[32,8192]{1,0:T(8,128)(2,1)S(1)}, bf16[32,8192]{1,0:T(8,128)(2,1)S(1)}, u32[]{:S(2)}, u32[]{:S(2)}) collective-permute-start(bf16[32,8192]{1,0:T(8,128)(2,1)S(1)} %fusion.14), channel_id=1, source_target_pairs={{0,2},{1,3},{2,0},{3,1},{4,6},{5,7},{6,4},{7,5},{8,10},{9,11},{10,... | collective-permute-start | bytes 1572872 | tf_op jit(solution)/shard_map/ppermute | solution.py:75
  6.6 6.4 %copy-start.12 = (s32[64]{0:T(128)S(1)}, s32[64]{0:T(128)}, u32[]{:S(2)}) copy-start(s32[64]{0:T(128)} %param.16) | copy-start | bytes 772
  6.6 12.3 %copy-start.1 = (bf16[1,64,8192]{2,1,0:T(8,128)(2,1)S(1)}, bf16[1,64,8192]{2,1,0:T(8,128)(2,1)}, u32[]{:S(2)}) copy-start(bf16[1,64,8192]{2,1,0:T(8,128)(2,1)} %param.10) | copy-start | bytes 3145732
  20.7 2.2 %collective-permute-start.2 = (bf16[32,10240]{1,0:T(8,128)(2,1)S(1)}, bf16[32,10240]{1,0:T(8,128)(2,1)S(1)}, u32[]{:S(2)}, u32[]{:S(2)}) collective-permute-start(bf16[32,10240]{1,0:T(8,128)(2,1)S(1)} %pad_maximum_fusion), channel_id=1, source_target_pairs={{0,1},{1,0},{2,3},{3,2},{4,5},{5,4},{6,7},{7,6},{8,9},{9,8},{10,11... | collective-permute-start | bytes 1966088 | tf_op jit(solution)/shard_map/ppermute | solution.py:75
  22.9 44.4 %copy-start.4 = (bf16[32,10240]{1,0:T(8,128)(2,1)}, bf16[32,10240]{1,0:T(8,128)(2,1)S(1)}, u32[]{:S(2)}) copy-start(bf16[32,10240]{1,0:T(8,128)(2,1)S(1)} %collective-permute-done.2) | copy-start | bytes 1966084
  23.8 12.0 %copy-start = (bf16[64,2048]{1,0:T(8,128)(2,1)S(1)}, bf16[64,2048]{1,0:T(8,128)(2,1)}, u32[]{:S(2)}) copy-start(bf16[64,2048]{1,0:T(8,128)(2,1)} %q_ref.2) | copy-start | bytes 786436
  24.9 31.3 %all-to-all-start = ((bf16[32,8,2176]{2,1,0:T(8,128)(2,1)}), bf16[32,8,2176]{2,1,0:T(8,128)(2,1)S(1)}, u32[]{:S(2)}, u32[]{:S(2)}) async-start(bf16[32,8,2176]{2,1,0:T(8,128)(2,1)} %maximum_bitcast_fusion), calls=%async_computation | async-start | bytes 2228224 | tf_op jit(solution)/shard_map/all_to_all | solution.py:171
  35.8 1.2 %copy-start.2 = (bf16[1024,2,256]{2,1,0:T(2,128)(2,1)S(1)}, bf16[1024,2,256]{2,1,0:T(2,128)(2,1)}, u32[]{:S(2)}) copy-start(bf16[1024,2,256]{2,1,0:T(2,128)(2,1)} %param.15) | copy-start | bytes 3145732
  56.2 4.2 %copy-start.6 = (f32[32,2048]{1,0:T(8,128)S(1)}, f32[32,2048]{1,0:T(8,128)}, u32[]{:S(2)}) copy-start(f32[32,2048]{1,0:T(8,128)} %get-tuple-element.33) | copy-start | bytes 786436
  60.3 1.3 %collective-permute-start.3 = (f32[256,64]{0,1:T(8,128)S(1)}, f32[256,64]{0,1:T(8,128)S(1)}, u32[]{:S(2)}, u32[]{:S(2)}) collective-permute-start(f32[256,64]{0,1:T(8,128)S(1)} %select_reduce_fusion), channel_id=1, source_target_pairs={{0,1},{1,0},{2,3},{3,2},{4,5},{5,4},{6,7},{7,6},{8,9},{9,8},{10,11... | collective-permute-start | bytes 196616 | tf_op jit(solution)/shard_map/ppermute | solution.py:75
  61.7 5.8 %copy-start.3 = (bf16[128,8,2,256]{3,1,2,0:T(8,128)(2,1)S(1)}, bf16[128,8,2,256]{3,1,2,0:T(8,128)(2,1)}, u32[]{:S(2)}) copy-start(bf16[128,8,2,256]{3,1,2,0:T(8,128)(2,1)} %copy.40) | copy-start | bytes 3145732
  61.7 5.7 %collective-permute-start.4 = (f32[256,64]{0,1:T(8,128)S(1)}, f32[256,64]{0,1:T(8,128)S(1)}, u32[]{:S(2)}, u32[]{:S(2)}) collective-permute-start(f32[256,64]{0,1:T(8,128)S(1)} %add.90), channel_id=1, source_target_pairs={{0,2},{1,3},{2,0},{3,1},{4,6},{5,7},{6,4},{7,5},{8,10},{9,11},{10,... | collective-permute-start | bytes 196616 | tf_op jit(solution)/shard_map/ppermute | solution.py:75
  67.3 5.6 %slice-start = ((bf16[32,10240]{1,0:T(8,128)(2,1)}), bf16[32,2048]{1,0:T(8,128)(2,1)S(1)}, s32[]{:S(2)}) async-start(bf16[32,10240]{1,0:T(8,128)(2,1)} %copy-done.4), calls=%async_computation.2 | async-start | bytes 262144 | tf_op jit(solution)/shard_map/slice | solution.py:131
  68.6 15.3 %all-to-all-start.1 = ((bf16[32,8,512]{2,1,0:T(8,128)(2,1)}), bf16[32,8,512]{2,1,0:T(8,128)(2,1)S(1)}, u32[]{:S(2)}, u32[]{:S(2)}) async-start(bf16[32,8,512]{2,1,0:T(8,128)(2,1)} %fusion.3), calls=%async_computation.1 | async-start | bytes 524288 | tf_op jit(solution)/shard_map/all_to_all | solution.py:191
  80.0 5.9 %copy-start.7 = (f32[32,2048]{1,0:T(8,128)S(1)}, f32[32,2048]{1,0:T(8,128)}, u32[]{:S(2)}) copy-start(f32[32,2048]{1,0:T(8,128)} %get-tuple-element.35) | copy-start | bytes 786436
  80.0 5.9 %copy-start.8 = (f32[32,2048]{1,0:T(8,128)S(1)}, f32[32,2048]{1,0:T(8,128)}, u32[]{:S(2)}) copy-start(f32[32,2048]{1,0:T(8,128)} %get-tuple-element.37) | copy-start | bytes 786436
  80.0 5.9 %copy-start.9 = (f32[32,2048]{1,0:T(8,128)S(1)}, f32[32,2048]{1,0:T(8,128)}, u32[]{:S(2)}) copy-start(f32[32,2048]{1,0:T(8,128)} %get-tuple-element.36) | copy-start | bytes 786436
  80.0 5.9 %copy-start.10 = (f32[32,2048]{1,0:T(8,128)S(1)}, f32[32,2048]{1,0:T(8,128)}, u32[]{:S(2)}) copy-start(f32[32,2048]{1,0:T(8,128)} %get-tuple-element.38) | copy-start | bytes 786436
  84.1 3.0 %copy-start.5 = (bf16[64,2,256]{2,1,0:T(2,128)(2,1)}, bf16[64,2,256]{2,1,0:T(2,128)(2,1)S(1)}, u32[]{:S(2)}) copy-start(bf16[64,2,256]{2,1,0:T(2,128)(2,1)S(1)} %reshape.123) | copy-start | bytes 196612

commit v6 on v5

--- a/solution.py
+++ b/solution.py
@@ -168,7 +168,20 @@
         adapt_count, capacity, quarter + ID_LANES
     )
     flattened_up = adapter_up_weight.reshape(adapter_grouped * ADAPTER_RANK, -1)
+    payload, queries_late = lax.optimization_barrier((payload, queries))
     rows_in = lax.all_to_all(payload, "adapter", split_axis=0, concat_axis=0, tiled=True)
+    attention_late = cache_attention(
+        queries_late,
+        key_value_cache,
+        prompt_cache_length,
+        local_heads,
+        FAN,
+        early_prompts,
+        local_prompts - early_prompts,
+    )
+    rows_in, base_kv, attention_late = lax.optimization_barrier(
+        (rows_in, base_kv, attention_late)
+    )
     item_count = rows_in.shape[1]
     rows_in = rows_in.reshape(slot_count, quarter + ID_LANES)
     flattened_rows = rows_in[:, :quarter]
@@ -179,8 +192,7 @@
     ).reshape(-1, adapter_grouped, ADAPTER_RANK)
     partial_low = jnp.sum(jnp.where(adapter_pick[:, :, None], projected_rows, 0.0), axis=1)
     pair_low = partial_low + _swap(partial_low, 1, tensor_count)
-    far_low, base_kv = lax.optimization_barrier((_swap(pair_low, 2, tensor_count), base_kv))
-    reduced_rank_rows = (pair_low + far_low).astype(jnp.bfloat16)
+    reduced_rank_rows = (pair_low + _swap(pair_low, 2, tensor_count)).astype(jnp.bfloat16)
     expanded_rows = jnp.where(
         adapter_pick[:, :, None], reduced_rank_rows[:, None, :], jnp.zeros((), jnp.bfloat16)
     ).reshape(-1, adapter_grouped * ADAPTER_RANK)
@@ -189,17 +201,6 @@
     ).astype(jnp.bfloat16)
     adapter_update = adapter_update.reshape(adapt_count, item_count, -1)
     returned = lax.all_to_all(adapter_update, "adapter", split_axis=0, concat_axis=0, tiled=True)
-    adapter_update, queries_late = lax.optimization_barrier((adapter_update, queries))
-    attention_late = cache_attention(
-        queries_late,
-        key_value_cache,
-        prompt_cache_length,
-        local_heads,
-        FAN,
-        early_prompts,
-        local_prompts - early_prompts,
-    )
-    returned, attention_late = lax.optimization_barrier((returned, attention_late))
     returned = returned.reshape(slot_count, -1)
     update_rows = lax.dot_general(
         slot_matrix, returned, (((0,), (0,)), ((), ())), preferred_element_type=jnp.float32

time: 87.9 us -> 85.3 us (0.970)
  local copies, waits for them, and re-layouts: 5.1 us -> 3.04 us
    all_to_all x1, waiting for transfers between devices: 17.9 us -> 9.09 us  [per_device(): lax.all_to_all(payload, 'adapter', split_axis=0, concat_axis=0, tiled=True)]
    all_to_all x1, waiting for transfers between devices: 3.9 us -> 10.1 us  [per_device(): lax.all_to_all(adapter_update, 'adapter', split_axis=0, concat_axis=0, ti...]
    ppermute x5, waiting for transfers between devices: 10.8 us -> 13.2 us  [_swap(): return lax.ppermute(x, 'tensor', perm=[(i, i ^ mask) for i in range(count)])]
    unnamed x29, local copies, waits for them, and re-layouts: 2.46 us -> 1.36 us
    concatenate x1, local copies, waits for them, and re-layouts: 0.98 us -> 0.02 us  [per_device(): jnp.concatenate([early, late], axis=0)]
where the time goes in v6:
time: 85.3 us; the launch traced here: 84.7 us
  waiting for transfers between devices  32.4 us (38%)
  starting transfers between devices  17.5 us (21%)
  Pallas kernels  12.7 us (15%)
  matrix products  10.8 us (13%)
  other arithmetic  7.11 us (8%)
  local copies, waits for them, and re-layouts  3.04 us (4%)
  between operations  1.03 us (1%)
    ppermute x5, waiting for transfers between devices, _swap(): return lax.ppermute(x, 'tensor', perm=[(i, i ^ mask) for i in range(count)])  13.2 us
    pallas_call x2, Pallas kernels, cache_attention(): pl.pallas_call(kernel, out_shape=(out, out, out), grid_spec=pltpu.Prefetc...  12.7 us
    all_to_all x1, starting transfers between devices, per_device(): lax.all_to_all(payload, 'adapter', split_axis=0, concat_axis=0, tiled=True)  10.9 us
    all_to_all x1, waiting for transfers between devices, per_device(): lax.all_to_all(adapter_update, 'adapter', split_axis=0, concat_axis=0, ti...  10.1 us
    all_to_all x1, waiting for transfers between devices, per_device(): lax.all_to_all(payload, 'adapter', split_axis=0, concat_axis=0, tiled=True)  9.09 us
    dot_general x1, matrix products, per_device(): jnp.einsum('rf,hfd->rhd', normed_full, head_weight, preferred_element_typ...  4.95 us
    all_to_all x1, starting transfers between devices, per_device(): lax.all_to_all(adapter_update, 'adapter', split_axis=0, concat_axis=0, ti...  4.02 us
    dot_general x1, matrix products, per_device(): jnp.dot(flattened_rows, adapter_down_weight, preferred_element_type=jnp.f...  3.97 us
  transfers between devices with their start and end apart: 7, of which 6 were waited for; matrix products, arithmetic and copies ran while one was open for 8% of the time, Pallas kernels for 15%

profile of v6, /device:TPU:0, one launch (start us, length us, event | category | flops | bytes accessed | tf_op | source)
XLA Modules:
  0.0 84.7 jit_solution(11327408220541183997)
XLA Ops:
  0.7 1.1 %dynamic-slice_bitcast_fusion = bf16[32,8192]{1,0:T(8,128)(2,1)S(1)} fusion(bf16[2,32,8192]{2,1,0:T(8,128)(2,1)} %bitcast.53, s32[]{:T(128)S(6)} %select_n.74), kind=kLoop, calls=%fused_computation.39 | loop fusion | bytes 1048580 | tf_op jit(solution)/shard_map/jit(dynamic_index_in_dim)/squeeze | solution.py:103
  1.8 1.9 %collective-permute-done = bf16[32,8192]{1,0:T(8,128)(2,1)S(1)} collective-permute-done((bf16[32,8192]{1,0:T(8,128)(2,1)S(1)}, bf16[32,8192]{1,0:T(8,128)(2,1)S(1)}, u32[]{:S(2)}, u32[]{:S(2)}) %collective-permute-start) | collective-permute-done | bytes 524320 | tf_op jit(solution)/shard_map/ppermute | solution.py:75
  3.7 1.2 %fusion.15 = bf16[32,8192]{1,0:T(8,128)(2,1)S(1)} fusion(bf16[32,8192]{1,0:T(8,128)(2,1)S(1)} %collective-permute-done, bf16[2,32,8192]{2,1,0:T(8,128)(2,1)} %bitcast.54, s32[]{:T(128)S(6)} %select_n.73), kind=kLoop, calls=%fused_computation.23 | loop fusion | flops 1048576 | bytes 1572868 | tf_op jit(solution)/shard_map/convert_element_type | solution.py:106
  4.9 1.7 %collective-permute-start.1 = (bf16[32,8192]{1,0:T(8,128)(2,1)S(1)}, bf16[32,8192]{1,0:T(8,128)(2,1)S(1)}, u32[]{:S(2)}, u32[]{:S(2)}) collective-permute-start(bf16[32,8192]{1,0:T(8,128)(2,1)S(1)} %fusion.15), channel_id=1, source_target_pairs={{0,2},{1,3},{2,0},{3,1},{4,6},{5,7},{6,4},{7,5},{8,10},{9,11},{10,... | collective-permute-start | bytes 1572872 | tf_op jit(solution)/shard_map/ppermute | solution.py:75
  6.6 6.4 %shard_map.121 = (f32[32,2048]{1,0:T(8,128)}, f32[32,2048]{1,0:T(8,128)}, f32[32,2048]{1,0:T(8,128)}) custom-call(s32[8]{0:T(128)} %len_ref.3, bf16[64,2048]{1,0:T(8,128)(2,1)} %q_ref.2, bf16[8,2,1024,256]{3,2,1,0:T(8,128)(2,1)} %v_ref.3, bf16[8,2,1024,256]{3,2,1,0:T(8,128)(2,1)} %v_ref.3), custom_call_target="tpu_custom_call" | custom-call | flops 268435456 | bytes 5111808 | tf_op jit(solution)/shard_map/pallas_call | solution.py:53
  13.0 5.9 %collective-permute-done.1 = bf16[32,8192]{1,0:T(8,128)(2,1)S(1)} collective-permute-done((bf16[32,8192]{1,0:T(8,128)(2,1)S(1)}, bf16[32,8192]{1,0:T(8,128)(2,1)S(1)}, u32[]{:S(2)}, u32[]{:S(2)}) %collective-permute-start.1) | collective-permute-done | bytes 524320 | tf_op jit(solution)/shard_map/ppermute | solution.py:75
  18.9 1.5 %fusion.8 = (f32[32]{0:T(128)S(1)}, bf16[32,8192]{1,0:T(8,128)(2,1)S(1)}) fusion(bf16[32,8192]{1,0:T(8,128)(2,1)S(1)} %collective-permute-done.1, bf16[32,8192]{1,0:T(8,128)(2,1)S(1)} %collective-permute-done, bf16[2,32,8192]{2,1,0:T(8,128)(2,1)S(1)} %bitcast.55, s32[]{:T(128)S(6)} %select_n.73, bf16[2,32,8192]{2,1,0:T(8,128)(2,1)} %bitcast.66), kind=kLoop, calls=%fused_computation.12 | loop fusion | flops 2883552 | bytes 2621572 | tf_op jit(solution)/shard_map/reduce_sum | solution.py:122
  20.5 0.2 fusion.10
  20.8 0.2 convert_reduce_fusion.1
  21.0 0.1 select_reduce_fusion.1
  21.1 1.8 %collective-permute-done.2 = bf16[32,10240]{1,0:T(8,128)(2,1)S(1)} collective-permute-done((bf16[32,10240]{1,0:T(8,128)(2,1)S(1)}, bf16[32,10240]{1,0:T(8,128)(2,1)S(1)}, u32[]{:S(2)}, u32[]{:S(2)}) %collective-permute-start.2) | collective-permute-done | bytes 655392 | tf_op jit(solution)/shard_map/ppermute | solution.py:75
  22.9 0.2 maximum_select_fusion
  23.1 0.5 convolution_convert_fusion
  23.8 1.1 %maximum_bitcast_fusion = bf16[32,8,2176]{2,1,0:T(8,128)(2,1)} fusion(bf16[256,128]{1,0:T(8,128)(2,1)S(1)} %broadcast_in_dim.48, bf16[256,2048]{1,0:T(8,128)(2,1)S(1)} %convolution_convert_fusion), kind=kLoop, calls=%fused_computation.11 | loop fusion | flops 2228224 | bytes 2228224 | tf_op jit(solution)/shard_map/reshape | solution.py:167
  24.8 10.9 %all-to-all-start = ((bf16[32,8,2176]{2,1,0:T(8,128)(2,1)}), bf16[32,8,2176]{2,1,0:T(8,128)(2,1)S(1)}, u32[]{:S(2)}, u32[]{:S(2)}) async-start(bf16[32,8,2176]{2,1,0:T(8,128)(2,1)} %maximum_bitcast_fusion), calls=%async_computation | async-start | bytes 2228224 | tf_op jit(solution)/shard_map/all_to_all | solution.py:172
  35.8 5.0 %fusion.4 = f32[2,8,8,256]{3,2,1,0:T(8,128)S(1)} fusion(bf16[2,8192,256]{2,0,1:T(2,128)(2,1)} %bitcast.67, bf16[64,8192]{1,0:T(8,128)(2,1)S(1)} %maximum_select_fusion), kind=kOutput, calls=%fused_computation.8 | convolution fusion | flops 536870912 | bytes 9568256 | tf_op jit(solution)/shard_map/rf,hfd->rhd/dot_general | solution.py:145
  40.7 6.3 %shard_map.122 = (f32[32,2048]{1,0:T(8,128)}, f32[32,2048]{1,0:T(8,128)}, f32[32,2048]{1,0:T(8,128)}) custom-call(s32[8]{0:T(128)} %len_ref.3, bf16[64,2048]{1,0:T(8,128)(2,1)} %q_ref.2, bf16[8,2,1024,256]{3,2,1,0:T(8,128)(2,1)} %v_ref.3, bf16[8,2,1024,256]{3,2,1,0:T(8,128)(2,1)} %v_ref.3), custom_call_target="tpu_custom_call" | custom-call | flops 268435456 | bytes 5111808 | tf_op jit(solution)/shard_map/pallas_call | solution.py:53
  47.0 9.1 %all-to-all-done = bf16[32,8,2176]{2,1,0:T(8,128)(2,1)S(1)} async-done(((bf16[32,8,2176]{2,1,0:T(8,128)(2,1)}), bf16[32,8,2176]{2,1,0:T(8,128)(2,1)S(1)}, u32[]{:S(2)}, u32[]{:S(2)}) %all-to-all-start) | async-done | bytes 1114144 | tf_op jit(solution)/shard_map/all_to_all | solution.py:172
  56.1 0.1 convert_reduce_fusion
  56.2 4.0 %fusion.11 = f32[256,1024]{0,1:T(8,128)S(1)} fusion(bf16[2048,1024]{1,0:T(8,128)(2,1)} %param.14, bf16[256,2176]{1,0:T(8,128)(2,1)S(1)} %bitcast.60), kind=kOutput, calls=%fused_computation.15 | convolution fusion | flops 1073741824 | bytes 6291456 | tf_op jit(solution)/shard_map/dot_general | solution.py:190
  60.5 1.0 %copy-done.2 = bf16[1024,2,256]{2,1,0:T(2,128)(2,1)S(1)} copy-done((bf16[1024,2,256]{2,1,0:T(2,128)(2,1)S(1)}, bf16[1024,2,256]{2,1,0:T(2,128)(2,1)}, u32[]{:S(2)}) %copy-start.2) | copy-done | bytes 1048600
  61.4 0.2 copy.40
  61.8 0.7 collective-permute-start.4
  62.5 3.6 %collective-permute-done.4 = f32[256,64]{0,1:T(8,128)S(1)} collective-permute-done((f32[256,64]{0,1:T(8,128)S(1)}, f32[256,64]{0,1:T(8,128)S(1)}, u32[]{:S(2)}, u32[]{:S(2)}) %collective-permute-start.4) | collective-permute-done | bytes 65568 | tf_op jit(solution)/shard_map/ppermute | solution.py:75
  66.2 1.2 %fusion.3 = bf16[32,8,512]{2,1,0:T(8,128)(2,1)} fusion(bf16[256,1024]{0,1:T(8,128)(2,1)S(1)} %bitcast.64, bf16[1024,512]{1,0:T(8,128)(2,1)S(1)} %bitcast.62), kind=kOutput, calls=%fused_computation.7 | convolution fusion | flops 268697600 | bytes 1835008 | tf_op jit(solution)/shard_map/dot_general | solution.py:200
  67.4 4.0 %all-to-all-start.1 = ((bf16[32,8,512]{2,1,0:T(8,128)(2,1)}), bf16[32,8,512]{2,1,0:T(8,128)(2,1)S(1)}, u32[]{:S(2)}, u32[]{:S(2)}) async-start(bf16[32,8,512]{2,1,0:T(8,128)(2,1)} %fusion.3), calls=%async_computation.1 | async-start | bytes 524288 | tf_op jit(solution)/shard_map/all_to_all | solution.py:203
  71.4 0.8 maximum_select_fusion.1
  72.2 10.1 %all-to-all-done.1 = bf16[32,8,512]{2,1,0:T(8,128)(2,1)S(1)} async-done(((bf16[32,8,512]{2,1,0:T(8,128)(2,1)}), bf16[32,8,512]{2,1,0:T(8,128)(2,1)S(1)}, u32[]{:S(2)}, u32[]{:S(2)}) %all-to-all-start.1) | async-done | bytes 262176 | tf_op jit(solution)/shard_map/all_to_all | solution.py:203
  82.3 0.2 fusion.7
  82.6 0.3 multiply_reduce_fusion
  83.1 0.2 max.11
  83.4 1.3 %fusion.18 = bf16[64,2048]{1,0:T(8,128)(2,1)} fusion(f32[8,8,16,128]{3,2,1,0:T(8,128)S(1)} %bitcast.57, f32[32,2048]{1,0:T(8,128)S(1)} %copy-done.9, f32[32,2048]{1,0:T(8,128)S(1)} %copy-done.7, f32[64,2048]{1,0:T(8,128)S(1)} %constant_dynamic-update-slice_fusion, f32[32,2048]{1,0:T(8,128)S(1)} %copy-done.10, f32[32,2048]{1,0:T(8,128)S(1)} %copy-done.8, ...), kind=kLoop, calls=%fused_computation.31 | loop fusion | flops 1835008 | bytes 2883584 | tf_op jit(solution)/shard_map/convert_element_type | solution.py:236
  (56 shorter events, 1.2 us)
Async XLA Ops:
  0.6 6.0 %copy-start.11 = (bf16[8192]{0:T(1024)(128)(2,1)S(1)}, bf16[8192]{0:T(1024)(128)(2,1)}, u32[]{:S(2)}) copy-start(bf16[8192]{0:T(1024)(128)(2,1)} %param.12) | copy-start | bytes 49156
  1.7 2.0 %collective-permute-start = (bf16[32,8192]{1,0:T(8,128)(2,1)S(1)}, bf16[32,8192]{1,0:T(8,128)(2,1)S(1)}, u32[]{:S(2)}, u32[]{:S(2)}) collective-permute-start(bf16[32,8192]{1,0:T(8,128)(2,1)S(1)} %dynamic-slice_bitcast_fusion), channel_id=1, source_target_pairs={{0,1},{1,0},{2,3},{3,2},{4,5},{5,4},{6,7},{7,6},{8,9},{9,8},{10,11... | collective-permute-start | bytes 1572872 | tf_op jit(solution)/shard_map/ppermute | solution.py:75
  4.9 14.0 %collective-permute-start.1 = (bf16[32,8192]{1,0:T(8,128)(2,1)S(1)}, bf16[32,8192]{1,0:T(8,128)(2,1)S(1)}, u32[]{:S(2)}, u32[]{:S(2)}) collective-permute-start(bf16[32,8192]{1,0:T(8,128)(2,1)S(1)} %fusion.15), channel_id=1, source_target_pairs={{0,2},{1,3},{2,0},{3,1},{4,6},{5,7},{6,4},{7,5},{8,10},{9,11},{10,... | collective-permute-start | bytes 1572872 | tf_op jit(solution)/shard_map/ppermute | solution.py:75
  6.6 6.4 %copy-start.12 = (s32[64]{0:T(128)S(1)}, s32[64]{0:T(128)}, u32[]{:S(2)}) copy-start(s32[64]{0:T(128)} %param.16) | copy-start | bytes 772
  6.6 12.3 %copy-start.1 = (bf16[1,64,8192]{2,1,0:T(8,128)(2,1)S(1)}, bf16[1,64,8192]{2,1,0:T(8,128)(2,1)}, u32[]{:S(2)}) copy-start(bf16[1,64,8192]{2,1,0:T(8,128)(2,1)} %param.10) | copy-start | bytes 3145732
  20.7 2.2 %collective-permute-start.2 = (bf16[32,10240]{1,0:T(8,128)(2,1)S(1)}, bf16[32,10240]{1,0:T(8,128)(2,1)S(1)}, u32[]{:S(2)}, u32[]{:S(2)}) collective-permute-start(bf16[32,10240]{1,0:T(8,128)(2,1)S(1)} %pad_maximum_fusion), channel_id=1, source_target_pairs={{0,1},{1,0},{2,3},{3,2},{4,5},{5,4},{6,7},{7,6},{8,9},{9,8},{10,11... | collective-permute-start | bytes 1966088 | tf_op jit(solution)/shard_map/ppermute | solution.py:75
  22.9 39.6 %copy-start.3 = (bf16[32,10240]{1,0:T(8,128)(2,1)}, bf16[32,10240]{1,0:T(8,128)(2,1)S(1)}, u32[]{:S(2)}) copy-start(bf16[32,10240]{1,0:T(8,128)(2,1)S(1)} %collective-permute-done.2) | copy-start | bytes 1966084
  24.8 31.3 %all-to-all-start = ((bf16[32,8,2176]{2,1,0:T(8,128)(2,1)}), bf16[32,8,2176]{2,1,0:T(8,128)(2,1)S(1)}, u32[]{:S(2)}, u32[]{:S(2)}) async-start(bf16[32,8,2176]{2,1,0:T(8,128)(2,1)} %maximum_bitcast_fusion), calls=%async_computation | async-start | bytes 2228224 | tf_op jit(solution)/shard_map/all_to_all | solution.py:172
  56.2 4.2 %copy-start = (bf16[64,2048]{1,0:T(8,128)(2,1)S(1)}, bf16[64,2048]{1,0:T(8,128)(2,1)}, u32[]{:S(2)}) copy-start(bf16[64,2048]{1,0:T(8,128)(2,1)} %q_ref.2) | copy-start | bytes 786436
  60.2 1.2 %copy-start.2 = (bf16[1024,2,256]{2,1,0:T(2,128)(2,1)S(1)}, bf16[1024,2,256]{2,1,0:T(2,128)(2,1)}, u32[]{:S(2)}) copy-start(bf16[1024,2,256]{2,1,0:T(2,128)(2,1)} %param.15) | copy-start | bytes 3145732
  60.3 2.2 %copy-start.5 = (f32[32,2048]{1,0:T(8,128)S(1)}, f32[32,2048]{1,0:T(8,128)}, u32[]{:S(2)}) copy-start(f32[32,2048]{1,0:T(8,128)} %get-tuple-element.33) | copy-start | bytes 786436
  60.3 1.4 %collective-permute-start.3 = (f32[256,64]{0,1:T(8,128)S(1)}, f32[256,64]{0,1:T(8,128)S(1)}, u32[]{:S(2)}, u32[]{:S(2)}) collective-permute-start(f32[256,64]{0,1:T(8,128)S(1)} %select_reduce_fusion), channel_id=1, source_target_pairs={{0,1},{1,0},{2,3},{3,2},{4,5},{5,4},{6,7},{7,6},{8,9},{9,8},{10,11... | collective-permute-start | bytes 196616 | tf_op jit(solution)/shard_map/ppermute | solution.py:75
  61.8 4.3 %collective-permute-start.4 = (f32[256,64]{0,1:T(8,128)S(1)}, f32[256,64]{0,1:T(8,128)S(1)}, u32[]{:S(2)}, u32[]{:S(2)}) collective-permute-start(f32[256,64]{0,1:T(8,128)S(1)} %add.90), channel_id=1, source_target_pairs={{0,2},{1,3},{2,0},{3,1},{4,6},{5,7},{6,4},{7,5},{8,10},{9,11},{10,... | collective-permute-start | bytes 196616 | tf_op jit(solution)/shard_map/ppermute | solution.py:75
  62.5 9.7 %copy-start.6 = (f32[32,2048]{1,0:T(8,128)S(1)}, f32[32,2048]{1,0:T(8,128)}, u32[]{:S(2)}) copy-start(f32[32,2048]{1,0:T(8,128)} %get-tuple-element.34) | copy-start | bytes 786436
  62.5 8.9 %slice-start = ((bf16[32,10240]{1,0:T(8,128)(2,1)}), bf16[32,2048]{1,0:T(8,128)(2,1)S(1)}, s32[]{:S(2)}) async-start(bf16[32,10240]{1,0:T(8,128)(2,1)} %copy-done.3), calls=%async_computation.2 | async-start | bytes 262144 | tf_op jit(solution)/shard_map/slice | solution.py:131
  67.4 16.0 %copy-start.7 = (f32[32,2048]{1,0:T(8,128)S(1)}, f32[32,2048]{1,0:T(8,128)}, u32[]{:S(2)}) copy-start(f32[32,2048]{1,0:T(8,128)} %get-tuple-element.35) | copy-start | bytes 786436
  67.4 16.0 %copy-start.8 = (f32[32,2048]{1,0:T(8,128)S(1)}, f32[32,2048]{1,0:T(8,128)}, u32[]{:S(2)}) copy-start(f32[32,2048]{1,0:T(8,128)} %get-tuple-element.37) | copy-start | bytes 786436
  67.4 16.0 %copy-start.9 = (f32[32,2048]{1,0:T(8,128)S(1)}, f32[32,2048]{1,0:T(8,128)}, u32[]{:S(2)}) copy-start(f32[32,2048]{1,0:T(8,128)} %get-tuple-element.36) | copy-start | bytes 786436
  67.4 16.0 %copy-start.10 = (f32[32,2048]{1,0:T(8,128)S(1)}, f32[32,2048]{1,0:T(8,128)}, u32[]{:S(2)}) copy-start(f32[32,2048]{1,0:T(8,128)} %get-tuple-element.38) | copy-start | bytes 786436
  67.4 14.9 %all-to-all-start.1 = ((bf16[32,8,512]{2,1,0:T(8,128)(2,1)}), bf16[32,8,512]{2,1,0:T(8,128)(2,1)S(1)}, u32[]{:S(2)}, u32[]{:S(2)}) async-start(bf16[32,8,512]{2,1,0:T(8,128)(2,1)} %fusion.3), calls=%async_computation.1 | async-start | bytes 524288 | tf_op jit(solution)/shard_map/all_to_all | solution.py:203
  82.6 2.1 %copy-start.4 = (bf16[64,2,256]{2,1,0:T(2,128)(2,1)}, bf16[64,2,256]{2,1,0:T(2,128)(2,1)S(1)}, u32[]{:S(2)}) copy-start(bf16[64,2,256]{2,1,0:T(2,128)(2,1)S(1)} %reshape.123) | copy-start | bytes 196612

commit v7 on v6

--- a/solution.py
+++ b/solution.py
@@ -191,8 +191,10 @@
         flattened_rows, adapter_down_weight, preferred_element_type=jnp.float32
     ).reshape(-1, adapter_grouped, ADAPTER_RANK)
     partial_low = jnp.sum(jnp.where(adapter_pick[:, :, None], projected_rows, 0.0), axis=1)
-    pair_low = partial_low + _swap(partial_low, 1, tensor_count)
-    reduced_rank_rows = (pair_low + _swap(pair_low, 2, tensor_count)).astype(jnp.bfloat16)
+    low_core = _swap(partial_low, 1, tensor_count)
+    low_chip = _swap(partial_low, 2, tensor_count)
+    low_diag = _swap(partial_low, 3, tensor_count)
+    reduced_rank_rows = ((partial_low + low_core) + (low_chip + low_diag)).astype(jnp.bfloat16)
     expanded_rows = jnp.where(
         adapter_pick[:, :, None], reduced_rank_rows[:, None, :], jnp.zeros((), jnp.bfloat16)
     ).reshape(-1, adapter_grouped * ADAPTER_RANK)

time: 85.3 us -> 85.7 us (level)
  waiting for transfers between devices: 32.4 us -> 29.5 us
  starting transfers between devices: 17.5 us -> 19.6 us
  local copies, waits for them, and re-layouts: 3.04 us -> 4.31 us
    all_to_all x1, waiting for transfers between devices: 9.09 us -> 6.5 us  [per_device(): lax.all_to_all(payload, 'adapter', split_axis=0, concat_axis=0, tiled=True)]
    ppermute x5 -> x6, starting transfers between devices: 2.61 us -> 4.07 us  [_swap(): return lax.ppermute(x, 'tensor', perm=[(i, i ^ mask) for i in range(count)])]
    unnamed x29, local copies, waits for them, and re-layouts: 1.36 us -> 2.62 us
    ppermute x5 -> x6, waiting for transfers between devices: 13.2 us -> 12.4 us  [_swap(): return lax.ppermute(x, 'tensor', perm=[(i, i ^ mask) for i in range(count)])]
  transfers between devices with their start and end apart: 7 -> 8, of which waited for: 6 -> 6; matrix products, arithmetic and copies ran while one was open for 8% -> 10% of each run, Pallas kernels for 15% -> 15%
where the time goes in v7:
time: 85.7 us; the launch traced here: 85 us
  waiting for transfers between devices  29.5 us (34%)
  starting transfers between devices  19.6 us (23%)
  Pallas kernels  12.7 us (15%)
  matrix products  10.8 us (13%)
  other arithmetic  7.12 us (8%)
  local copies, waits for them, and re-layouts  4.31 us (5%)
  between operations  0.99 us (1%)
    pallas_call x2, Pallas kernels, cache_attention(): pl.pallas_call(kernel, out_shape=(out, out, out), grid_spec=pltpu.Prefetc...  12.7 us
    ppermute x6, waiting for transfers between devices, _swap(): return lax.ppermute(x, 'tensor', perm=[(i, i ^ mask) for i in range(count)])  12.4 us
    all_to_all x1, starting transfers between devices, per_device(): lax.all_to_all(payload, 'adapter', split_axis=0, concat_axis=0, tiled=True)  11 us
    all_to_all x1, waiting for transfers between devices, per_device(): lax.all_to_all(adapter_update, 'adapter', split_axis=0, concat_axis=0, ti...  10.6 us
    all_to_all x1, waiting for transfers between devices, per_device(): lax.all_to_all(payload, 'adapter', split_axis=0, concat_axis=0, tiled=True)  6.5 us
    dot_general x1, matrix products, per_device(): jnp.einsum('rf,hfd->rhd', normed_full, head_weight, preferred_element_typ...  4.95 us
    all_to_all x1, starting transfers between devices, per_device(): lax.all_to_all(adapter_update, 'adapter', split_axis=0, concat_axis=0, ti...  4.46 us
    ppermute x6, starting transfers between devices, _swap(): return lax.ppermute(x, 'tensor', perm=[(i, i ^ mask) for i in range(count)])  4.07 us
  transfers between devices with their start and end apart: 8, of which 6 were waited for; matrix products, arithmetic and copies ran while one was open for 10% of the time, Pallas kernels for 15%

profile of v7, /device:TPU:0, one launch (start us, length us, event | category | flops | bytes accessed | tf_op | source)
XLA Modules:
  0.0 85.0 jit_solution(9789938153027403374)
XLA Ops:
  0.7 1.1 %dynamic-slice_bitcast_fusion = bf16[32,8192]{1,0:T(8,128)(2,1)S(1)} fusion(bf16[2,32,8192]{2,1,0:T(8,128)(2,1)} %bitcast.53, s32[]{:T(128)S(6)} %select_n.74), kind=kLoop, calls=%fused_computation.39 | loop fusion | bytes 1048580 | tf_op jit(solution)/shard_map/jit(dynamic_index_in_dim)/squeeze | solution.py:103
  1.8 1.9 %collective-permute-done = bf16[32,8192]{1,0:T(8,128)(2,1)S(1)} collective-permute-done((bf16[32,8192]{1,0:T(8,128)(2,1)S(1)}, bf16[32,8192]{1,0:T(8,128)(2,1)S(1)}, u32[]{:S(2)}, u32[]{:S(2)}) %collective-permute-start) | collective-permute-done | bytes 524320 | tf_op jit(solution)/shard_map/ppermute | solution.py:75
  3.7 1.2 %fusion.15 = bf16[32,8192]{1,0:T(8,128)(2,1)S(1)} fusion(bf16[32,8192]{1,0:T(8,128)(2,1)S(1)} %collective-permute-done, bf16[2,32,8192]{2,1,0:T(8,128)(2,1)} %bitcast.54, s32[]{:T(128)S(6)} %select_n.73), kind=kLoop, calls=%fused_computation.23 | loop fusion | flops 1048576 | bytes 1572868 | tf_op jit(solution)/shard_map/convert_element_type | solution.py:106
  4.9 1.7 %collective-permute-start.1 = (bf16[32,8192]{1,0:T(8,128)(2,1)S(1)}, bf16[32,8192]{1,0:T(8,128)(2,1)S(1)}, u32[]{:S(2)}, u32[]{:S(2)}) collective-permute-start(bf16[32,8192]{1,0:T(8,128)(2,1)S(1)} %fusion.15), channel_id=1, source_target_pairs={{0,2},{1,3},{2,0},{3,1},{4,6},{5,7},{6,4},{7,5},{8,10},{9,11},{10,... | collective-permute-start | bytes 1572872 | tf_op jit(solution)/shard_map/ppermute | solution.py:75
  6.6 6.4 %shard_map.121 = (f32[32,2048]{1,0:T(8,128)}, f32[32,2048]{1,0:T(8,128)}, f32[32,2048]{1,0:T(8,128)}) custom-call(s32[8]{0:T(128)} %len_ref.3, bf16[64,2048]{1,0:T(8,128)(2,1)} %q_ref.2, bf16[8,2,1024,256]{3,2,1,0:T(8,128)(2,1)} %v_ref.3, bf16[8,2,1024,256]{3,2,1,0:T(8,128)(2,1)} %v_ref.3), custom_call_target="tpu_custom_call" | custom-call | flops 268435456 | bytes 5111808 | tf_op jit(solution)/shard_map/pallas_call | solution.py:53
  13.0 5.9 %collective-permute-done.1 = bf16[32,8192]{1,0:T(8,128)(2,1)S(1)} collective-permute-done((bf16[32,8192]{1,0:T(8,128)(2,1)S(1)}, bf16[32,8192]{1,0:T(8,128)(2,1)S(1)}, u32[]{:S(2)}, u32[]{:S(2)}) %collective-permute-start.1) | collective-permute-done | bytes 524320 | tf_op jit(solution)/shard_map/ppermute | solution.py:75
  18.9 1.5 %fusion.8 = (f32[32]{0:T(128)S(1)}, bf16[32,8192]{1,0:T(8,128)(2,1)S(1)}) fusion(bf16[32,8192]{1,0:T(8,128)(2,1)S(1)} %collective-permute-done.1, bf16[32,8192]{1,0:T(8,128)(2,1)S(1)} %collective-permute-done, bf16[2,32,8192]{2,1,0:T(8,128)(2,1)S(1)} %bitcast.55, s32[]{:T(128)S(6)} %select_n.73, bf16[2,32,8192]{2,1,0:T(8,128)(2,1)} %bitcast.66), kind=kLoop, calls=%fused_computation.12 | loop fusion | flops 2883552 | bytes 2621572 | tf_op jit(solution)/shard_map/reduce_sum | solution.py:122
  20.5 0.2 fusion.10
  20.8 0.2 convert_reduce_fusion.1
  21.0 0.1 select_reduce_fusion.1
  21.1 1.8 %collective-permute-done.2 = bf16[32,10240]{1,0:T(8,128)(2,1)S(1)} collective-permute-done((bf16[32,10240]{1,0:T(8,128)(2,1)S(1)}, bf16[32,10240]{1,0:T(8,128)(2,1)S(1)}, u32[]{:S(2)}, u32[]{:S(2)}) %collective-permute-start.2) | collective-permute-done | bytes 655392 | tf_op jit(solution)/shard_map/ppermute | solution.py:75
  22.9 0.2 maximum_select_fusion
  23.1 0.5 convolution_convert_fusion
  23.8 1.1 %maximum_bitcast_fusion = bf16[32,8,2176]{2,1,0:T(8,128)(2,1)} fusion(bf16[256,128]{1,0:T(8,128)(2,1)S(1)} %broadcast_in_dim.48, bf16[256,2048]{1,0:T(8,128)(2,1)S(1)} %convolution_convert_fusion), kind=kLoop, calls=%fused_computation.11 | loop fusion | flops 2228224 | bytes 2228224 | tf_op jit(solution)/shard_map/reshape | solution.py:167
  24.9 11.0 %all-to-all-start = ((bf16[32,8,2176]{2,1,0:T(8,128)(2,1)}), bf16[32,8,2176]{2,1,0:T(8,128)(2,1)S(1)}, u32[]{:S(2)}, u32[]{:S(2)}) async-start(bf16[32,8,2176]{2,1,0:T(8,128)(2,1)} %maximum_bitcast_fusion), calls=%async_computation | async-start | bytes 2228224 | tf_op jit(solution)/shard_map/all_to_all | solution.py:172
  35.9 2.5 %copy.40 = bf16[128,8,2,256]{3,1,2,0:T(8,128)(2,1)} copy(bf16[128,8,2,256]{3,2,1,0:T(2,128)(2,1)} %bitcast.61) | data formatting | bytes 2097152
  38.5 5.0 %fusion.4 = f32[2,8,8,256]{3,2,1,0:T(8,128)S(1)} fusion(bf16[2,8192,256]{2,0,1:T(2,128)(2,1)} %bitcast.67, bf16[64,8192]{1,0:T(8,128)(2,1)S(1)} %maximum_select_fusion), kind=kOutput, calls=%fused_computation.8 | convolution fusion | flops 536870912 | bytes 9568256 | tf_op jit(solution)/shard_map/rf,hfd->rhd/dot_general | solution.py:145
  43.5 6.3 %shard_map.122 = (f32[32,2048]{1,0:T(8,128)}, f32[32,2048]{1,0:T(8,128)}, f32[32,2048]{1,0:T(8,128)}) custom-call(s32[8]{0:T(128)} %len_ref.3, bf16[64,2048]{1,0:T(8,128)(2,1)} %q_ref.2, bf16[8,2,1024,256]{3,2,1,0:T(8,128)(2,1)} %v_ref.3, bf16[8,2,1024,256]{3,2,1,0:T(8,128)(2,1)} %v_ref.3), custom_call_target="tpu_custom_call" | custom-call | flops 268435456 | bytes 5111808 | tf_op jit(solution)/shard_map/pallas_call | solution.py:53
  49.7 6.5 %all-to-all-done = bf16[32,8,2176]{2,1,0:T(8,128)(2,1)S(1)} async-done(((bf16[32,8,2176]{2,1,0:T(8,128)(2,1)}), bf16[32,8,2176]{2,1,0:T(8,128)(2,1)S(1)}, u32[]{:S(2)}, u32[]{:S(2)}) %all-to-all-start) | async-done | bytes 1114144 | tf_op jit(solution)/shard_map/all_to_all | solution.py:172
  56.2 0.1 convert_reduce_fusion
  56.4 4.0 %fusion.11 = f32[256,1024]{0,1:T(8,128)S(1)} fusion(bf16[2048,1024]{1,0:T(8,128)(2,1)} %param.14, bf16[256,2176]{1,0:T(8,128)(2,1)S(1)} %bitcast.60), kind=kOutput, calls=%fused_computation.15 | convolution fusion | flops 1073741824 | bytes 6291456 | tf_op jit(solution)/shard_map/dot_general | solution.py:190
  60.5 0.7 collective-permute-start.4
  61.1 1.5 %collective-permute-start.3 = (f32[256,64]{0,1:T(8,128)S(1)}, f32[256,64]{0,1:T(8,128)S(1)}, u32[]{:S(2)}, u32[]{:S(2)}) collective-permute-start(f32[256,64]{0,1:T(8,128)S(1)} %select_reduce_fusion), channel_id=1, source_target_pairs={{0,1},{1,0},{2,3},{3,2},{4,5},{5,4},{6,7},{7,6},{8,9},{9,8},{10,11... | collective-permute-start | bytes 196616 | tf_op jit(solution)/shard_map/ppermute | solution.py:75
  62.7 2.7 %collective-permute-done.4 = f32[256,64]{0,1:T(8,128)S(1)} collective-permute-done((f32[256,64]{0,1:T(8,128)S(1)}, f32[256,64]{0,1:T(8,128)S(1)}, u32[]{:S(2)}, u32[]{:S(2)}) %collective-permute-start.4) | collective-permute-done | bytes 65568 | tf_op jit(solution)/shard_map/ppermute | solution.py:75
  65.6 1.2 %fusion.3 = bf16[32,8,512]{2,1,0:T(8,128)(2,1)} fusion(bf16[256,1024]{0,1:T(8,128)(2,1)S(1)} %bitcast.64, bf16[1024,512]{1,0:T(8,128)(2,1)S(1)} %bitcast.62), kind=kOutput, calls=%fused_computation.7 | convolution fusion | flops 268697600 | bytes 1835008 | tf_op jit(solution)/shard_map/dot_general | solution.py:202
  66.8 4.5 %all-to-all-start.1 = ((bf16[32,8,512]{2,1,0:T(8,128)(2,1)}), bf16[32,8,512]{2,1,0:T(8,128)(2,1)S(1)}, u32[]{:S(2)}, u32[]{:S(2)}) async-start(bf16[32,8,512]{2,1,0:T(8,128)(2,1)} %fusion.3), calls=%async_computation.1 | async-start | bytes 524288 | tf_op jit(solution)/shard_map/all_to_all | solution.py:205
  71.3 0.8 maximum_select_fusion.1
  72.0 10.6 %all-to-all-done.1 = bf16[32,8,512]{2,1,0:T(8,128)(2,1)S(1)} async-done(((bf16[32,8,512]{2,1,0:T(8,128)(2,1)}), bf16[32,8,512]{2,1,0:T(8,128)(2,1)S(1)}, u32[]{:S(2)}, u32[]{:S(2)}) %all-to-all-start.1) | async-done | bytes 262176 | tf_op jit(solution)/shard_map/all_to_all | solution.py:205
  82.7 0.2 fusion.7
  83.0 0.3 multiply_reduce_fusion
  83.5 0.2 max.11
  83.7 1.3 %fusion.18 = bf16[64,2048]{1,0:T(8,128)(2,1)} fusion(f32[8,8,16,128]{3,2,1,0:T(8,128)S(1)} %bitcast.57, f32[32,2048]{1,0:T(8,128)S(1)} %copy-done.9, f32[32,2048]{1,0:T(8,128)S(1)} %copy-done.7, f32[64,2048]{1,0:T(8,128)S(1)} %constant_dynamic-update-slice_fusion, f32[32,2048]{1,0:T(8,128)S(1)} %copy-done.10, f32[32,2048]{1,0:T(8,128)S(1)} %copy-done.8, ...), kind=kLoop, calls=%fused_computation.31 | loop fusion | flops 1835008 | bytes 2883584 | tf_op jit(solution)/shard_map/convert_element_type | solution.py:238
  (57 shorter events, 1.1 us)
Async XLA Ops:
  0.6 6.0 %copy-start.11 = (bf16[8192]{0:T(1024)(128)(2,1)S(1)}, bf16[8192]{0:T(1024)(128)(2,1)}, u32[]{:S(2)}) copy-start(bf16[8192]{0:T(1024)(128)(2,1)} %param.12) | copy-start | bytes 49156
  1.7 2.0 %collective-permute-start = (bf16[32,8192]{1,0:T(8,128)(2,1)S(1)}, bf16[32,8192]{1,0:T(8,128)(2,1)S(1)}, u32[]{:S(2)}, u32[]{:S(2)}) collective-permute-start(bf16[32,8192]{1,0:T(8,128)(2,1)S(1)} %dynamic-slice_bitcast_fusion), channel_id=1, source_target_pairs={{0,1},{1,0},{2,3},{3,2},{4,5},{5,4},{6,7},{7,6},{8,9},{9,8},{10,11... | collective-permute-start | bytes 1572872 | tf_op jit(solution)/shard_map/ppermute | solution.py:75
  4.9 14.0 %collective-permute-start.1 = (bf16[32,8192]{1,0:T(8,128)(2,1)S(1)}, bf16[32,8192]{1,0:T(8,128)(2,1)S(1)}, u32[]{:S(2)}, u32[]{:S(2)}) collective-permute-start(bf16[32,8192]{1,0:T(8,128)(2,1)S(1)} %fusion.15), channel_id=1, source_target_pairs={{0,2},{1,3},{2,0},{3,1},{4,6},{5,7},{6,4},{7,5},{8,10},{9,11},{10,... | collective-permute-start | bytes 1572872 | tf_op jit(solution)/shard_map/ppermute | solution.py:75
  6.6 6.4 %copy-start.12 = (s32[64]{0:T(128)S(1)}, s32[64]{0:T(128)}, u32[]{:S(2)}) copy-start(s32[64]{0:T(128)} %param.16) | copy-start | bytes 772
  6.6 12.3 %copy-start.1 = (bf16[1,64,8192]{2,1,0:T(8,128)(2,1)S(1)}, bf16[1,64,8192]{2,1,0:T(8,128)(2,1)}, u32[]{:S(2)}) copy-start(bf16[1,64,8192]{2,1,0:T(8,128)(2,1)} %param.10) | copy-start | bytes 3145732
  20.7 2.2 %collective-permute-start.2 = (bf16[32,10240]{1,0:T(8,128)(2,1)S(1)}, bf16[32,10240]{1,0:T(8,128)(2,1)S(1)}, u32[]{:S(2)}, u32[]{:S(2)}) collective-permute-start(bf16[32,10240]{1,0:T(8,128)(2,1)S(1)} %pad_maximum_fusion), channel_id=1, source_target_pairs={{0,1},{1,0},{2,3},{3,2},{4,5},{5,4},{6,7},{7,6},{8,9},{9,8},{10,11... | collective-permute-start | bytes 1966088 | tf_op jit(solution)/shard_map/ppermute | solution.py:75
  22.9 39.8 %copy-start.3 = (bf16[32,10240]{1,0:T(8,128)(2,1)}, bf16[32,10240]{1,0:T(8,128)(2,1)S(1)}, u32[]{:S(2)}) copy-start(bf16[32,10240]{1,0:T(8,128)(2,1)S(1)} %collective-permute-done.2) | copy-start | bytes 1966084
  24.9 13.5 %copy-start = (bf16[64,2048]{1,0:T(8,128)(2,1)S(1)}, bf16[64,2048]{1,0:T(8,128)(2,1)}, u32[]{:S(2)}) copy-start(bf16[64,2048]{1,0:T(8,128)(2,1)} %q_ref.2) | copy-start | bytes 786436
  24.9 31.4 %all-to-all-start = ((bf16[32,8,2176]{2,1,0:T(8,128)(2,1)}), bf16[32,8,2176]{2,1,0:T(8,128)(2,1)S(1)}, u32[]{:S(2)}, u32[]{:S(2)}) async-start(bf16[32,8,2176]{2,1,0:T(8,128)(2,1)} %maximum_bitcast_fusion), calls=%async_computation | async-start | bytes 2228224 | tf_op jit(solution)/shard_map/all_to_all | solution.py:172
  56.4 6.3 %copy-start.5 = (f32[32,2048]{1,0:T(8,128)S(1)}, f32[32,2048]{1,0:T(8,128)}, u32[]{:S(2)}) copy-start(f32[32,2048]{1,0:T(8,128)} %get-tuple-element.33) | copy-start | bytes 786436
  60.4 5.2 %copy-start.2 = (bf16[128,8,2,256]{3,1,2,0:T(8,128)(2,1)S(1)}, bf16[128,8,2,256]{3,1,2,0:T(8,128)(2,1)}, u32[]{:S(2)}) copy-start(bf16[128,8,2,256]{3,1,2,0:T(8,128)(2,1)} %copy.40) | copy-start | bytes 3145732
  60.5 5.0 %collective-permute-start.4 = (f32[256,64]{0,1:T(8,128)S(1)}, f32[256,64]{0,1:T(8,128)S(1)}, u32[]{:S(2)}, u32[]{:S(2)}) collective-permute-start(f32[256,64]{0,1:T(8,128)S(1)} %select_reduce_fusion), channel_id=1, source_target_pairs={{0,2},{1,3},{2,0},{3,1},{4,6},{5,7},{6,4},{7,5},{8,10},{9,11},{10,... | collective-permute-start | bytes 196616 | tf_op jit(solution)/shard_map/ppermute | solution.py:75
  61.1 4.4 %collective-permute-start.5 = (f32[256,64]{0,1:T(8,128)S(1)}, f32[256,64]{0,1:T(8,128)S(1)}, u32[]{:S(2)}, u32[]{:S(2)}) collective-permute-start(f32[256,64]{0,1:T(8,128)S(1)} %select_reduce_fusion), channel_id=1, source_target_pairs={{0,3},{1,2},{2,1},{3,0},{4,7},{5,6},{6,5},{7,4},{8,11},{9,10},{10,... | collective-permute-start | bytes 196616 | tf_op jit(solution)/shard_map/ppermute | solution.py:75
  61.1 4.4 %collective-permute-start.3 = (f32[256,64]{0,1:T(8,128)S(1)}, f32[256,64]{0,1:T(8,128)S(1)}, u32[]{:S(2)}, u32[]{:S(2)}) collective-permute-start(f32[256,64]{0,1:T(8,128)S(1)} %select_reduce_fusion), channel_id=1, source_target_pairs={{0,1},{1,0},{2,3},{3,2},{4,5},{5,4},{6,7},{7,6},{8,9},{9,8},{10,11... | collective-permute-start | bytes 196616 | tf_op jit(solution)/shard_map/ppermute | solution.py:75
  62.7 9.3 %copy-start.6 = (f32[32,2048]{1,0:T(8,128)S(1)}, f32[32,2048]{1,0:T(8,128)}, u32[]{:S(2)}) copy-start(f32[32,2048]{1,0:T(8,128)} %get-tuple-element.34) | copy-start | bytes 786436
  62.7 8.5 %slice-start = ((bf16[32,10240]{1,0:T(8,128)(2,1)}), bf16[32,2048]{1,0:T(8,128)(2,1)S(1)}, s32[]{:S(2)}) async-start(bf16[32,10240]{1,0:T(8,128)(2,1)} %copy-done.3), calls=%async_computation.2 | async-start | bytes 262144 | tf_op jit(solution)/shard_map/slice | solution.py:131
  66.8 16.9 %copy-start.7 = (f32[32,2048]{1,0:T(8,128)S(1)}, f32[32,2048]{1,0:T(8,128)}, u32[]{:S(2)}) copy-start(f32[32,2048]{1,0:T(8,128)} %get-tuple-element.35) | copy-start | bytes 786436
  66.8 16.9 %copy-start.8 = (f32[32,2048]{1,0:T(8,128)S(1)}, f32[32,2048]{1,0:T(8,128)}, u32[]{:S(2)}) copy-start(f32[32,2048]{1,0:T(8,128)} %get-tuple-element.37) | copy-start | bytes 786436
  66.8 16.9 %copy-start.9 = (f32[32,2048]{1,0:T(8,128)S(1)}, f32[32,2048]{1,0:T(8,128)}, u32[]{:S(2)}) copy-start(f32[32,2048]{1,0:T(8,128)} %get-tuple-element.36) | copy-start | bytes 786436
  66.8 16.9 %copy-start.10 = (f32[32,2048]{1,0:T(8,128)S(1)}, f32[32,2048]{1,0:T(8,128)}, u32[]{:S(2)}) copy-start(f32[32,2048]{1,0:T(8,128)} %get-tuple-element.38) | copy-start | bytes 786436
  66.8 15.9 %all-to-all-start.1 = ((bf16[32,8,512]{2,1,0:T(8,128)(2,1)}), bf16[32,8,512]{2,1,0:T(8,128)(2,1)S(1)}, u32[]{:S(2)}, u32[]{:S(2)}) async-start(bf16[32,8,512]{2,1,0:T(8,128)(2,1)} %fusion.3), calls=%async_computation.1 | async-start | bytes 524288 | tf_op jit(solution)/shard_map/all_to_all | solution.py:205
  82.9 2.1 %copy-start.4 = (bf16[64,2,256]{2,1,0:T(2,128)(2,1)}, bf16[64,2,256]{2,1,0:T(2,128)(2,1)S(1)}, u32[]{:S(2)}) copy-start(bf16[64,2,256]{2,1,0:T(2,128)(2,1)S(1)} %reshape.123) | copy-start | bytes 196612

commit v8 on v7

--- a/solution.py
+++ b/solution.py
@@ -71,6 +71,36 @@
     )(prompt_cache_length, queries, key_value_cache, key_value_cache)
 
 
+def _down_kernel(rows_ref, weight_ref, out_ref, *, width, groups):
+    ids = rows_ref[:, pl.ds(width, 1)].astype(jnp.float32).astype(jnp.int32)
+    proj = jnp.dot(rows_ref[:, pl.ds(0, width)], weight_ref[...], preferred_element_type=jnp.float32)
+    lane = lax.broadcasted_iota(jnp.int32, (proj.shape[0], 2 * ADAPTER_RANK), 1)
+    upper = (lane >= ADAPTER_RANK).astype(jnp.int32)
+    acc = jnp.zeros((proj.shape[0], 2 * ADAPTER_RANK), jnp.float32)
+    for j in range(groups // 2):
+        block = proj[:, j * 2 * ADAPTER_RANK:(j + 1) * 2 * ADAPTER_RANK]
+        acc = acc + jnp.where(ids == 2 * j + upper, block, 0.0)
+    out_ref[...] = acc
+
+
+def down_project(rows_in, down_weight, width):
+    slots = rows_in.shape[0]
+    groups = down_weight.shape[1] // ADAPTER_RANK
+    kernel = functools.partial(_down_kernel, width=width, groups=groups)
+    folded = pl.pallas_call(
+        kernel,
+        out_shape=jax.ShapeDtypeStruct((slots, 2 * ADAPTER_RANK), jnp.float32),
+        in_specs=[pl.BlockSpec(memory_space=pltpu.VMEM), pl.BlockSpec(memory_space=pltpu.VMEM)],
+        out_specs=pl.BlockSpec(memory_space=pltpu.VMEM),
+        cost_estimate=pl.CostEstimate(
+            flops=2 * slots * width * down_weight.shape[1],
+            transcendentals=0,
+            bytes_accessed=rows_in.size * 2 + down_weight.size * 2 + slots * 512,
+        ),
+    )(rows_in, down_weight)
+    return folded[:, :ADAPTER_RANK] + folded[:, ADAPTER_RANK:]
+
+
 def _swap(x, mask, count):
     return lax.ppermute(x, "tensor", perm=[(i, i ^ mask) for i in range(count)])
 
@@ -184,13 +214,9 @@
     )
     item_count = rows_in.shape[1]
     rows_in = rows_in.reshape(slot_count, quarter + ID_LANES)
-    flattened_rows = rows_in[:, :quarter]
     ids_in = rows_in[:, quarter].astype(jnp.int32)
     adapter_pick = ids_in[:, None] == jnp.arange(adapter_grouped)[None, :]
-    projected_rows = jnp.dot(
-        flattened_rows, adapter_down_weight, preferred_element_type=jnp.float32
-    ).reshape(-1, adapter_grouped, ADAPTER_RANK)
-    partial_low = jnp.sum(jnp.where(adapter_pick[:, :, None], projected_rows, 0.0), axis=1)
+    partial_low = down_project(rows_in, adapter_down_weight, quarter)
     low_core = _swap(partial_low, 1, tensor_count)
     low_chip = _swap(partial_low, 2, tensor_count)
     low_diag = _swap(partial_low, 3, tensor_count)

time: 85.7 us -> 92.7 us (1.082)
  Pallas kernels: 12.7 us -> 17.2 us
  matrix products: 10.8 us -> 6.86 us
  local copies, waits for them, and re-layouts: 4.31 us -> 6.87 us
  other arithmetic: 7.12 us -> 9.18 us
  waiting for transfers between devices: 29.5 us -> 31 us
    pallas_call x0 -> x1, Pallas kernels: none -> 4.52 us  [down_project(): pl.pallas_call(kernel, out_shape=jax.ShapeDtypeStruct((slots, 2 * ADAPTER...]
    dot_general x1 -> x0, matrix products: 3.97 us -> none  [per_device(): jnp.dot(flattened_rows, adapter_down_weight, preferred_element_type=jnp.f...]
    all_to_all x1, waiting for transfers between devices: 6.5 us -> 7.96 us  [per_device(): lax.all_to_all(payload, 'adapter', split_axis=0, concat_axis=0, tiled=True)]
    unnamed x29, local copies, waits for them, and re-layouts: 2.62 us -> 4.06 us
    add x0 -> x1, other arithmetic: none -> 1.07 us  [down_project(): return folded[:, :ADAPTER_RANK] + folded[:, ADAPTER_RANK:]]
    convert_element_type x1, other arithmetic: 0.02 us -> 1.08 us  [per_device(): (partial_low + low_core + (low_chip + low_diag)).astype(jnp.bfloat16)]
    concatenate x1, local copies, waits for them, and re-layouts: 0.02 us -> 0.97 us  [per_device(): jnp.concatenate([early, late], axis=0)]
  transfers between devices with their start and end apart: 8 -> 8, of which waited for: 6 -> 6; matrix products, arithmetic and copies ran while one was open for 10% -> 10% of each run, Pallas kernels for 15% -> 14%
where the time goes in v8:
time: 92.7 us; the launch traced here: 91.5 us
  waiting for transfers between devices  31 us (33%)
  starting transfers between devices  19.4 us (21%)
  Pallas kernels  17.2 us (19%)
  other arithmetic  9.18 us (10%)
  local copies, waits for them, and re-layouts  6.87 us (7%)
  matrix products  6.86 us (7%)
  between operations  0.98 us (1%)
    pallas_call x2, Pallas kernels, cache_attention(): pl.pallas_call(kernel, out_shape=(out, out, out), grid_spec=pltpu.Prefetc...  12.7 us
    ppermute x6, waiting for transfers between devices, _swap(): return lax.ppermute(x, 'tensor', perm=[(i, i ^ mask) for i in range(count)])  12.6 us
    all_to_all x1, starting transfers between devices, per_device(): lax.all_to_all(payload, 'adapter', split_axis=0, concat_axis=0, tiled=True)  10.9 us
    all_to_all x1, waiting for transfers between devices, per_device(): lax.all_to_all(adapter_update, 'adapter', split_axis=0, concat_axis=0, ti...  10.4 us
    all_to_all x1, waiting for transfers between devices, per_device(): lax.all_to_all(payload, 'adapter', split_axis=0, concat_axis=0, tiled=True)  7.96 us
    dot_general x1, matrix products, per_device(): jnp.einsum('rf,hfd->rhd', normed_full, head_weight, preferred_element_typ...  4.95 us
    pallas_call x1, Pallas kernels, down_project(): pl.pallas_call(kernel, out_shape=jax.ShapeDtypeStruct((slots, 2 * ADAPTER...  4.52 us
    all_to_all x1, starting transfers between devices, per_device(): lax.all_to_all(adapter_update, 'adapter', split_axis=0, concat_axis=0, ti...  4.46 us
  transfers between devices with their start and end apart: 8, of which 6 were waited for; matrix products, arithmetic and copies ran while one was open for 10% of the time, Pallas kernels for 14%

profile of v8, /device:TPU:0, one launch (start us, length us, event | category | flops | bytes accessed | tf_op | source)
XLA Modules:
  0.0 91.5 jit_solution(17576551310992688282)
XLA Ops:
  0.7 1.2 %dynamic-slice_bitcast_fusion = bf16[32,8192]{1,0:T(8,128)(2,1)S(1)} fusion(bf16[2,32,8192]{2,1,0:T(8,128)(2,1)} %bitcast.53, s32[]{:T(128)S(6)} %select_n.70), kind=kLoop, calls=%fused_computation.36 | loop fusion | bytes 1048580 | tf_op jit(solution)/shard_map/jit(dynamic_index_in_dim)/squeeze | solution.py:133
  1.9 1.9 %collective-permute-done = bf16[32,8192]{1,0:T(8,128)(2,1)S(1)} collective-permute-done((bf16[32,8192]{1,0:T(8,128)(2,1)S(1)}, bf16[32,8192]{1,0:T(8,128)(2,1)S(1)}, u32[]{:S(2)}, u32[]{:S(2)}) %collective-permute-start) | collective-permute-done | bytes 524320 | tf_op jit(solution)/shard_map/ppermute | solution.py:105
  3.8 1.2 %fusion.13 = bf16[32,8192]{1,0:T(8,128)(2,1)S(1)} fusion(bf16[32,8192]{1,0:T(8,128)(2,1)S(1)} %collective-permute-done, bf16[2,32,8192]{2,1,0:T(8,128)(2,1)} %bitcast.54, s32[]{:T(128)S(6)} %select_n.69), kind=kLoop, calls=%fused_computation.20 | loop fusion | flops 1048576 | bytes 1572868 | tf_op jit(solution)/shard_map/convert_element_type | solution.py:136
  5.0 1.7 %collective-permute-start.1 = (bf16[32,8192]{1,0:T(8,128)(2,1)S(1)}, bf16[32,8192]{1,0:T(8,128)(2,1)S(1)}, u32[]{:S(2)}, u32[]{:S(2)}) collective-permute-start(bf16[32,8192]{1,0:T(8,128)(2,1)S(1)} %fusion.13), channel_id=1, source_target_pairs={{0,2},{1,3},{2,0},{3,1},{4,6},{5,7},{6,4},{7,5},{8,10},{9,11},{10,... | collective-permute-start | bytes 1572872 | tf_op jit(solution)/shard_map/ppermute | solution.py:105
  6.7 1.2 %copy.34 = bf16[128,8,2,256]{3,1,2,0:T(8,128)(2,1)} copy(bf16[128,8,2,256]{3,2,1,0:T(2,128)(2,1)S(1)} %bitcast.59) | data formatting | bytes 2097152
  7.9 6.4 %shard_map.121 = (f32[32,2048]{1,0:T(8,128)}, f32[32,2048]{1,0:T(8,128)}, f32[32,2048]{1,0:T(8,128)}) custom-call(s32[8]{0:T(128)} %len_ref.3, bf16[64,2048]{1,0:T(8,128)(2,1)} %q_ref.2, bf16[8,2,1024,256]{3,2,1,0:T(8,128)(2,1)} %v_ref.3, bf16[8,2,1024,256]{3,2,1,0:T(8,128)(2,1)} %v_ref.3), custom_call_target="tpu_custom_call" | custom-call | flops 268435456 | bytes 5111808 | tf_op jit(solution)/shard_map/pallas_call | solution.py:53
  14.3 4.7 %collective-permute-done.1 = bf16[32,8192]{1,0:T(8,128)(2,1)S(1)} collective-permute-done((bf16[32,8192]{1,0:T(8,128)(2,1)S(1)}, bf16[32,8192]{1,0:T(8,128)(2,1)S(1)}, u32[]{:S(2)}, u32[]{:S(2)}) %collective-permute-start.1) | collective-permute-done | bytes 524320 | tf_op jit(solution)/shard_map/ppermute | solution.py:105
  19.0 1.5 %fusion.8 = (f32[32]{0:T(128)S(1)}, bf16[32,8192]{1,0:T(8,128)(2,1)S(1)}) fusion(bf16[32,8192]{1,0:T(8,128)(2,1)S(1)} %collective-permute-done.1, bf16[32,8192]{1,0:T(8,128)(2,1)S(1)} %collective-permute-done, bf16[2,32,8192]{2,1,0:T(8,128)(2,1)S(1)} %bitcast.55, s32[]{:T(128)S(6)} %select_n.69, bf16[2,32,8192]{2,1,0:T(8,128)(2,1)} %bitcast.63), kind=kLoop, calls=%fused_computation.12 | loop fusion | flops 2883552 | bytes 2621572 | tf_op jit(solution)/shard_map/reduce_sum | solution.py:152
  21.2 1.8 %collective-permute-done.2 = bf16[32,10240]{1,0:T(8,128)(2,1)S(1)} collective-permute-done((bf16[32,10240]{1,0:T(8,128)(2,1)S(1)}, bf16[32,10240]{1,0:T(8,128)(2,1)S(1)}, u32[]{:S(2)}, u32[]{:S(2)}) %collective-permute-start.2) | collective-permute-done | bytes 655392 | tf_op jit(solution)/shard_map/ppermute | solution.py:105
  23.0 0.8 copy-done.5
  24.0 0.5 convolution_convert_fusion
  24.7 1.1 %maximum_bitcast_fusion = bf16[32,8,2176]{2,1,0:T(8,128)(2,1)} fusion(bf16[256,128]{1,0:T(8,128)(2,1)S(1)} %broadcast_in_dim.31, bf16[256,2048]{1,0:T(8,128)(2,1)S(1)} %convolution_convert_fusion), kind=kLoop, calls=%fused_computation.11 | loop fusion | flops 2228224 | bytes 2228224 | tf_op jit(solution)/shard_map/reshape | solution.py:197
  25.8 10.9 %all-to-all-start = ((bf16[32,8,2176]{2,1,0:T(8,128)(2,1)}), bf16[32,8,2176]{2,1,0:T(8,128)(2,1)S(1)}, u32[]{:S(2)}, u32[]{:S(2)}) async-start(bf16[32,8,2176]{2,1,0:T(8,128)(2,1)} %maximum_bitcast_fusion), calls=%async_computation | async-start | bytes 2228224 | tf_op jit(solution)/shard_map/all_to_all | solution.py:202
  36.9 1.0 %constant_dynamic-update-slice_fusion.1 = f32[64,2048]{1,0:T(8,128)S(1)} fusion(f32[32,2048]{1,0:T(8,128)} %get-tuple-element.33), kind=kLoop, calls=%fused_computation.56 | loop fusion | bytes 524288
  37.9 5.0 %fusion.4 = f32[2,8,8,256]{3,2,1,0:T(8,128)S(1)} fusion(bf16[2,8192,256]{2,0,1:T(2,128)(2,1)} %bitcast.64, bf16[64,8192]{1,0:T(8,128)(2,1)S(1)} %maximum_select_fusion), kind=kOutput, calls=%fused_computation.8 | convolution fusion | flops 536870912 | bytes 9568256 | tf_op jit(solution)/shard_map/rf,hfd->rhd/dot_general | solution.py:175
  42.8 6.3 %shard_map.122 = (f32[32,2048]{1,0:T(8,128)}, f32[32,2048]{1,0:T(8,128)}, f32[32,2048]{1,0:T(8,128)}) custom-call(s32[8]{0:T(128)} %len_ref.3, bf16[64,2048]{1,0:T(8,128)(2,1)} %q_ref.2, bf16[8,2,1024,256]{3,2,1,0:T(8,128)(2,1)} %v_ref.3, bf16[8,2,1024,256]{3,2,1,0:T(8,128)(2,1)} %v_ref.3), custom_call_target="tpu_custom_call" | custom-call | flops 268435456 | bytes 5111808 | tf_op jit(solution)/shard_map/pallas_call | solution.py:53
  49.1 8.0 %all-to-all-done = bf16[32,8,2176]{2,1,0:T(8,128)(2,1)S(1)} async-done(((bf16[32,8,2176]{2,1,0:T(8,128)(2,1)}), bf16[32,8,2176]{2,1,0:T(8,128)(2,1)S(1)}, u32[]{:S(2)}, u32[]{:S(2)}) %all-to-all-start) | async-done | bytes 1114144 | tf_op jit(solution)/shard_map/all_to_all | solution.py:202
  57.2 0.9 copy-done
  58.1 4.5 %shard_map.123 = f32[256,128]{1,0:T(8,128)} custom-call(bf16[256,2176]{1,0:T(8,128)(2,1)} %bitcast.52, bf16[2048,1024]{1,0:T(8,128)(2,1)} %weight_ref.1), custom_call_target="tpu_custom_call" | custom-call | flops 1073741824 | bytes 5439488 | tf_op jit(solution)/shard_map/pallas_call | solution.py:90
  62.6 1.1 %slice_add_fusion = f32[256,64]{1,0:T(8,128)S(1)} fusion(f32[256,128]{1,0:T(8,128)} %shard_map.123), kind=kLoop, calls=%fused_computation.41 | loop fusion | flops 16384 | bytes 196608 | tf_op jit(solution)/shard_map/add | solution.py:101
  63.7 0.7 collective-permute-start.4
  64.4 1.5 %collective-permute-start.3 = (f32[256,64]{1,0:T(8,128)S(1)}, f32[256,64]{1,0:T(8,128)S(1)}, u32[]{:S(2)}, u32[]{:S(2)}) collective-permute-start(f32[256,64]{1,0:T(8,128)S(1)} %slice_add_fusion), channel_id=1, source_target_pairs={{0,1},{1,0},{2,3},{3,2},{4,5},{5,4},{6,7},{7,6},{8,9},{9,8},{10,11... | collective-permute-start | bytes 196616 | tf_op jit(solution)/shard_map/ppermute | solution.py:105
  65.9 4.2 %collective-permute-done.4 = f32[256,64]{1,0:T(8,128)S(1)} collective-permute-done((f32[256,64]{1,0:T(8,128)S(1)}, f32[256,64]{1,0:T(8,128)S(1)}, u32[]{:S(2)}, u32[]{:S(2)}) %collective-permute-start.4) | collective-permute-done | bytes 65568 | tf_op jit(solution)/shard_map/ppermute | solution.py:105
  70.2 1.1 %add_convert_fusion = bf16[256,64]{1,0:T(8,128)(2,1)S(1)} fusion(f32[256,64]{1,0:T(8,128)S(1)} %collective-permute-done.4, f32[256,64]{1,0:T(8,128)S(1)} %collective-permute-done.5, f32[256,64]{1,0:T(8,128)S(1)} %collective-permute-done.3, f32[256,128]{1,0:T(8,128)} %shard_map.123), kind=kLoop, calls=%fused_computation.43 | loop fusion | flops 81920 | bytes 360448 | tf_op jit(solution)/shard_map/convert_element_type | solution.py:223
  71.4 1.2 %fusion.3 = bf16[32,8,512]{2,1,0:T(8,128)(2,1)} fusion(bf16[256,1024]{0,1:T(8,128)(2,1)S(1)} %bitcast.61, bf16[1024,512]{1,0:T(8,128)(2,1)S(1)} %bitcast.60), kind=kOutput, calls=%fused_computation.7 | convolution fusion | flops 268697600 | bytes 1835008 | tf_op jit(solution)/shard_map/dot_general | solution.py:228
  72.6 4.5 %all-to-all-start.1 = ((bf16[32,8,512]{2,1,0:T(8,128)(2,1)}), bf16[32,8,512]{2,1,0:T(8,128)(2,1)S(1)}, u32[]{:S(2)}, u32[]{:S(2)}) async-start(bf16[32,8,512]{2,1,0:T(8,128)(2,1)} %fusion.3), calls=%async_computation.1 | async-start | bytes 524288 | tf_op jit(solution)/shard_map/all_to_all | solution.py:231
  77.1 0.8 maximum_select_fusion.1
  77.8 1.0 %constant_dynamic-update-slice_fusion = f32[64,2048]{1,0:T(8,128)S(1)} fusion(f32[64,2048]{1,0:T(8,128)S(1)} %constant_dynamic-update-slice_fusion.1, f32[32,2048]{1,0:T(8,128)} %get-tuple-element.34), kind=kLoop, calls=%fused_computation.55 | loop fusion | bytes 524288 | tf_op jit(solution)/shard_map/concatenate | solution.py:243
  78.8 10.4 %all-to-all-done.1 = bf16[32,8,512]{2,1,0:T(8,128)(2,1)S(1)} async-done(((bf16[32,8,512]{2,1,0:T(8,128)(2,1)}), bf16[32,8,512]{2,1,0:T(8,128)(2,1)S(1)}, u32[]{:S(2)}, u32[]{:S(2)}) %all-to-all-start.1) | async-done | bytes 262176 | tf_op jit(solution)/shard_map/all_to_all | solution.py:231
  89.2 0.2 fusion.7
  89.5 0.3 multiply_reduce_fusion
  90.2 1.3 %fusion.16 = bf16[64,2048]{1,0:T(8,128)(2,1)} fusion(f32[8,8,16,128]{3,2,1,0:T(8,128)S(1)} %bitcast.57, f32[32,2048]{1,0:T(8,128)S(1)} %copy-done.9, f32[32,2048]{1,0:T(8,128)S(1)} %copy-done.7, f32[64,2048]{1,0:T(8,128)S(1)} %constant_dynamic-update-slice_fusion, f32[32,2048]{1,0:T(8,128)S(1)} %copy-done.10, f32[32,2048]{1,0:T(8,128)S(1)} %copy-done.8, ...), kind=kLoop, calls=%fused_computation.28 | loop fusion | flops 1835008 | bytes 2883584 | tf_op jit(solution)/shard_map/convert_element_type | solution.py:264
  (58 shorter events, 2.0 us)
Async XLA Ops:
  0.6 6.0 %copy-start.11 = (bf16[8192]{0:T(1024)(128)(2,1)S(1)}, bf16[8192]{0:T(1024)(128)(2,1)}, u32[]{:S(2)}) copy-start(bf16[8192]{0:T(1024)(128)(2,1)} %param.12) | copy-start | bytes 49156
  0.6 6.0 %copy-start.3 = (bf16[1024,2,256]{2,1,0:T(2,128)(2,1)S(1)}, bf16[1024,2,256]{2,1,0:T(2,128)(2,1)}, u32[]{:S(2)}) copy-start(bf16[1024,2,256]{2,1,0:T(2,128)(2,1)} %param.15) | copy-start | bytes 3145732
  1.8 2.0 %collective-permute-start = (bf16[32,8192]{1,0:T(8,128)(2,1)S(1)}, bf16[32,8192]{1,0:T(8,128)(2,1)S(1)}, u32[]{:S(2)}, u32[]{:S(2)}) collective-permute-start(bf16[32,8192]{1,0:T(8,128)(2,1)S(1)} %dynamic-slice_bitcast_fusion), channel_id=1, source_target_pairs={{0,1},{1,0},{2,3},{3,2},{4,5},{5,4},{6,7},{7,6},{8,9},{9,8},{10,11... | collective-permute-start | bytes 1572872 | tf_op jit(solution)/shard_map/ppermute | solution.py:105
  5.0 14.0 %collective-permute-start.1 = (bf16[32,8192]{1,0:T(8,128)(2,1)S(1)}, bf16[32,8192]{1,0:T(8,128)(2,1)S(1)}, u32[]{:S(2)}, u32[]{:S(2)}) collective-permute-start(bf16[32,8192]{1,0:T(8,128)(2,1)S(1)} %fusion.13), channel_id=1, source_target_pairs={{0,2},{1,3},{2,0},{3,1},{4,6},{5,7},{6,4},{7,5},{8,10},{9,11},{10,... | collective-permute-start | bytes 1572872 | tf_op jit(solution)/shard_map/ppermute | solution.py:105
  7.9 6.4 %copy-start.12 = (s32[64]{0:T(128)S(1)}, s32[64]{0:T(128)}, u32[]{:S(2)}) copy-start(s32[64]{0:T(128)} %param.16) | copy-start | bytes 772
  7.9 11.1 %copy-start.2 = (bf16[1,64,8192]{2,1,0:T(8,128)(2,1)S(1)}, bf16[1,64,8192]{2,1,0:T(8,128)(2,1)}, u32[]{:S(2)}) copy-start(bf16[1,64,8192]{2,1,0:T(8,128)(2,1)} %param.10) | copy-start | bytes 3145732
  20.8 2.2 %collective-permute-start.2 = (bf16[32,10240]{1,0:T(8,128)(2,1)S(1)}, bf16[32,10240]{1,0:T(8,128)(2,1)S(1)}, u32[]{:S(2)}, u32[]{:S(2)}) collective-permute-start(bf16[32,10240]{1,0:T(8,128)(2,1)S(1)} %pad_maximum_fusion), channel_id=1, source_target_pairs={{0,1},{1,0},{2,3},{3,2},{4,5},{5,4},{6,7},{7,6},{8,9},{9,8},{10,11... | collective-permute-start | bytes 1966088 | tf_op jit(solution)/shard_map/ppermute | solution.py:105
  23.0 0.8 copy-start.5
  24.7 12.0 %copy-start.1 = (bf16[64,2048]{1,0:T(8,128)(2,1)S(1)}, bf16[64,2048]{1,0:T(8,128)(2,1)}, u32[]{:S(2)}) copy-start(bf16[64,2048]{1,0:T(8,128)(2,1)} %q_ref.2) | copy-start | bytes 786436
  25.8 31.3 %all-to-all-start = ((bf16[32,8,2176]{2,1,0:T(8,128)(2,1)}), bf16[32,8,2176]{2,1,0:T(8,128)(2,1)S(1)}, u32[]{:S(2)}, u32[]{:S(2)}) async-start(bf16[32,8,2176]{2,1,0:T(8,128)(2,1)} %maximum_bitcast_fusion), calls=%async_computation | async-start | bytes 2228224 | tf_op jit(solution)/shard_map/all_to_all | solution.py:202
  57.1 1.0 %copy-start = (bf16[32,8,2176]{2,1,0:T(8,128)(2,1)}, bf16[32,8,2176]{2,1,0:T(8,128)(2,1)S(1)}, u32[]{:S(2)}) copy-start(bf16[32,8,2176]{2,1,0:T(8,128)(2,1)S(1)} %all-to-all-done) | copy-start | bytes 3342340
  58.1 13.3 %copy-start.4 = (bf16[128,8,2,256]{3,1,2,0:T(8,128)(2,1)S(1)}, bf16[128,8,2,256]{3,1,2,0:T(8,128)(2,1)}, u32[]{:S(2)}) copy-start(bf16[128,8,2,256]{3,1,2,0:T(8,128)(2,1)} %copy.34) | copy-start | bytes 3145732
  63.7 13.4 %slice-start = ((bf16[32,10240]{1,0:T(8,128)(2,1)}), bf16[32,2048]{1,0:T(8,128)(2,1)S(1)}, s32[]{:S(2)}) async-start(bf16[32,10240]{1,0:T(8,128)(2,1)} %copy-done.5), calls=%async_computation.2 | async-start | bytes 262144 | tf_op jit(solution)/shard_map/slice | solution.py:161
  63.7 6.4 %collective-permute-start.4 = (f32[256,64]{1,0:T(8,128)S(1)}, f32[256,64]{1,0:T(8,128)S(1)}, u32[]{:S(2)}, u32[]{:S(2)}) collective-permute-start(f32[256,64]{1,0:T(8,128)S(1)} %slice_add_fusion), channel_id=1, source_target_pairs={{0,2},{1,3},{2,0},{3,1},{4,6},{5,7},{6,4},{7,5},{8,10},{9,11},{10,... | collective-permute-start | bytes 196616 | tf_op jit(solution)/shard_map/ppermute | solution.py:105
  64.4 5.8 %collective-permute-start.5 = (f32[256,64]{1,0:T(8,128)S(1)}, f32[256,64]{1,0:T(8,128)S(1)}, u32[]{:S(2)}, u32[]{:S(2)}) collective-permute-start(f32[256,64]{1,0:T(8,128)S(1)} %slice_add_fusion), channel_id=1, source_target_pairs={{0,3},{1,2},{2,1},{3,0},{4,7},{5,6},{6,5},{7,4},{8,11},{9,10},{10,... | collective-permute-start | bytes 196616 | tf_op jit(solution)/shard_map/ppermute | solution.py:105
  64.4 5.8 %collective-permute-start.3 = (f32[256,64]{1,0:T(8,128)S(1)}, f32[256,64]{1,0:T(8,128)S(1)}, u32[]{:S(2)}, u32[]{:S(2)}) collective-permute-start(f32[256,64]{1,0:T(8,128)S(1)} %slice_add_fusion), channel_id=1, source_target_pairs={{0,1},{1,0},{2,3},{3,2},{4,5},{5,4},{6,7},{7,6},{8,9},{9,8},{10,11... | collective-permute-start | bytes 196616 | tf_op jit(solution)/shard_map/ppermute | solution.py:105
  72.6 17.6 %copy-start.7 = (f32[32,2048]{1,0:T(8,128)S(1)}, f32[32,2048]{1,0:T(8,128)}, u32[]{:S(2)}) copy-start(f32[32,2048]{1,0:T(8,128)} %get-tuple-element.35) | copy-start | bytes 786436
  72.6 17.6 %copy-start.8 = (f32[32,2048]{1,0:T(8,128)S(1)}, f32[32,2048]{1,0:T(8,128)}, u32[]{:S(2)}) copy-start(f32[32,2048]{1,0:T(8,128)} %get-tuple-element.37) | copy-start | bytes 786436
  72.6 17.6 %copy-start.9 = (f32[32,2048]{1,0:T(8,128)S(1)}, f32[32,2048]{1,0:T(8,128)}, u32[]{:S(2)}) copy-start(f32[32,2048]{1,0:T(8,128)} %get-tuple-element.36) | copy-start | bytes 786436
  72.6 17.6 %copy-start.10 = (f32[32,2048]{1,0:T(8,128)S(1)}, f32[32,2048]{1,0:T(8,128)}, u32[]{:S(2)}) copy-start(f32[32,2048]{1,0:T(8,128)} %get-tuple-element.38) | copy-start | bytes 786436
  72.6 16.6 %all-to-all-start.1 = ((bf16[32,8,512]{2,1,0:T(8,128)(2,1)}), bf16[32,8,512]{2,1,0:T(8,128)(2,1)S(1)}, u32[]{:S(2)}, u32[]{:S(2)}) async-start(bf16[32,8,512]{2,1,0:T(8,128)(2,1)} %fusion.3), calls=%async_computation.1 | async-start | bytes 524288 | tf_op jit(solution)/shard_map/all_to_all | solution.py:231
  89.4 2.1 %copy-start.6 = (bf16[64,2,256]{2,1,0:T(2,128)(2,1)}, bf16[64,2,256]{2,1,0:T(2,128)(2,1)S(1)}, u32[]{:S(2)}) copy-start(bf16[64,2,256]{2,1,0:T(2,128)(2,1)S(1)} %reshape.119) | copy-start | bytes 196612

commit v9 on v7

--- a/solution.py
+++ b/solution.py
@@ -123,25 +123,34 @@
     normed_half = (
         hidden_wide * lax.rsqrt(mean_sq + EPSILON) * attention_norm_gain.astype(jnp.float32)
     ).astype(jnp.bfloat16)
-    partner_quarter = lax.dynamic_slice_in_dim(
-        hidden_half, (tensor_index ^ 1) * quarter, quarter, 1
-    )
-    swap_in = _swap(jnp.concatenate([normed_half, partner_quarter], axis=1), 1, tensor_count)
-    normed_other = swap_in[:, :model_width]
-    hidden_other = swap_in[:, model_width:]
-    hidden_mine = lax.dynamic_slice_in_dim(hidden_half, tensor_index * quarter, quarter, 1)
+    partner_cols = (tensor_index ^ 1) * quarter
+    to_partner = jnp.concatenate(
+        [
+            lax.dynamic_slice_in_dim(normed_half, partner_cols, quarter, 1),
+            lax.dynamic_slice_in_dim(hidden_half, partner_cols, quarter, 1),
+        ],
+        axis=1,
+    )
+    from_partner = _swap(to_partner, 1, tensor_count)
+    normed_other_full = _swap(normed_half, 1, tensor_count)
+    own_cols = tensor_index * quarter
+    normed_mine = lax.dynamic_slice_in_dim(normed_half, own_cols, quarter, 1)
+    hidden_mine = lax.dynamic_slice_in_dim(hidden_half, own_cols, quarter, 1)
+    normed_other = from_partner[:, :quarter]
+    hidden_other = from_partner[:, quarter:]
+
     first = core == 0
-    hidden_part = jnp.where(
-        first,
-        jnp.concatenate([hidden_mine, hidden_other], axis=0),
-        jnp.concatenate([hidden_other, hidden_mine], axis=0),
-    )
-    normed_full = jnp.where(
-        first,
-        jnp.concatenate([normed_half, normed_other], axis=0),
-        jnp.concatenate([normed_other, normed_half], axis=0),
-    )
-    normed_part = lax.dynamic_slice_in_dim(normed_full, tensor_index * quarter, quarter, 1)
+
+    def by_core(mine, other):
+        return jnp.where(
+            first,
+            jnp.concatenate([mine, other], axis=0),
+            jnp.concatenate([other, mine], axis=0),
+        )
+
+    hidden_part = by_core(hidden_mine, hidden_other)
+    normed_part = by_core(normed_mine, normed_other)
+    normed_full = by_core(normed_half, normed_other_full)
     base_kv = jnp.einsum(
         "rf,hfd->rhd", normed_full, head_weight, preferred_element_type=jnp.float32
     ).reshape(row_dev, -1)
@@ -159,13 +168,17 @@
     row_slot = owner_index * capacity + slot_rank
     row_to_slot = jnp.arange(slot_count)[:, None] == row_slot[None, :]
     slot_matrix = row_to_slot.astype(jnp.bfloat16)
-    send_rows = jnp.dot(slot_matrix, normed_part, preferred_element_type=jnp.float32).astype(
-        jnp.bfloat16
-    )
-    send_ids = jnp.sum(jnp.where(row_to_slot, local_id[None, :] + 1, 0), axis=1) - 1
-    id_block = jnp.broadcast_to(send_ids.astype(jnp.bfloat16)[:, None], (slot_count, ID_LANES))
-    payload = jnp.concatenate([send_rows, id_block], axis=1).reshape(
-        adapt_count, capacity, quarter + ID_LANES
+    id_block = jnp.broadcast_to(
+        (local_id + 1).astype(jnp.bfloat16)[:, None], (row_dev, ID_LANES)
+    )
+    payload = (
+        jnp.dot(
+            slot_matrix,
+            jnp.concatenate([normed_part, id_block], axis=1),
+            preferred_element_type=jnp.float32,
+        )
+        .astype(jnp.bfloat16)
+        .reshape(adapt_count, capacity, quarter + ID_LANES)
     )
     flattened_up = adapter_up_weight.reshape(adapter_grouped * ADAPTER_RANK, -1)
     payload, queries_late = lax.optimization_barrier((payload, queries))
@@ -185,7 +198,7 @@
     item_count = rows_in.shape[1]
     rows_in = rows_in.reshape(slot_count, quarter + ID_LANES)
     flattened_rows = rows_in[:, :quarter]
-    ids_in = rows_in[:, quarter].astype(jnp.int32)
+    ids_in = rows_in[:, quarter].astype(jnp.int32) - 1
     adapter_pick = ids_in[:, None] == jnp.arange(adapter_grouped)[None, :]
     projected_rows = jnp.dot(
         flattened_rows, adapter_down_weight, preferred_element_type=jnp.float32

time: 85.7 us -> 84.7 us (0.988)
  other arithmetic: 7.12 us -> 5.72 us
  matrix products: 10.8 us -> 12.1 us
  local copies, waits for them, and re-layouts: 4.31 us -> 3.06 us
    unnamed x29, local copies, waits for them, and re-layouts: 2.62 us -> 1.39 us
    reshape x1 -> x0, other arithmetic: 1.09 us -> none  [per_device(): jnp.concatenate([send_rows, id_block], axis=1)]
    ppermute x6 -> x7, waiting for transfers between devices: 12.4 us -> 11.4 us  [_swap(): return lax.ppermute(x, 'tensor', perm=[(i, i ^ mask) for i in range(count)])]
    dot_general x1, matrix products: 0.54 us -> 1.44 us  [per_device(): jnp.dot(slot_matrix, jnp.concatenate([normed_part, id_block], axis=1), pr...]
    all_to_all x1, waiting for transfers between devices: 6.5 us -> 7.37 us  [per_device(): lax.all_to_all(payload, 'adapter', split_axis=0, concat_axis=0, tiled=True)]
    ppermute x6 -> x7, starting transfers between devices: 4.07 us -> 4.65 us  [_swap(): return lax.ppermute(x, 'tensor', perm=[(i, i ^ mask) for i in range(count)])]
  transfers between devices with their start and end apart: 8 -> 9, of which waited for: 6 -> 6; matrix products, arithmetic and copies ran while one was open for 10% -> 11% of each run, Pallas kernels for 15% -> 15%
where the time goes in v9:
time: 84.7 us; the launch traced here: 84.1 us
  waiting for transfers between devices  29.4 us (35%)
  starting transfers between devices  20.2 us (24%)
  Pallas kernels  12.7 us (15%)
  matrix products  12.1 us (14%)
  other arithmetic  5.72 us (7%)
  local copies, waits for them, and re-layouts  3.06 us (4%)
  between operations  0.98 us (1%)
    pallas_call x2, Pallas kernels, cache_attention(): pl.pallas_call(kernel, out_shape=(out, out, out), grid_spec=pltpu.Prefetc...  12.7 us
    ppermute x7, waiting for transfers between devices, _swap(): return lax.ppermute(x, 'tensor', perm=[(i, i ^ mask) for i in range(count)])  11.4 us
    all_to_all x1, starting transfers between devices, per_device(): lax.all_to_all(payload, 'adapter', split_axis=0, concat_axis=0, tiled=True)  11 us
    all_to_all x1, waiting for transfers between devices, per_device(): lax.all_to_all(adapter_update, 'adapter', split_axis=0, concat_axis=0, ti...  10.6 us
    all_to_all x1, waiting for transfers between devices, per_device(): lax.all_to_all(payload, 'adapter', split_axis=0, concat_axis=0, tiled=True)  7.37 us
    dot_general x1, matrix products, per_device(): jnp.einsum('rf,hfd->rhd', normed_full, head_weight, preferred_element_typ...  5.3 us
    ppermute x7, starting transfers between devices, _swap(): return lax.ppermute(x, 'tensor', perm=[(i, i ^ mask) for i in range(count)])  4.65 us
    all_to_all x1, starting transfers between devices, per_device(): lax.all_to_all(adapter_update, 'adapter', split_axis=0, concat_axis=0, ti...  4.46 us
  transfers between devices with their start and end apart: 9, of which 6 were waited for; matrix products, arithmetic and copies ran while one was open for 11% of the time, Pallas kernels for 15%

profile of v9, /device:TPU:0, one launch (start us, length us, event | category | flops | bytes accessed | tf_op | source)
XLA Modules:
  0.0 84.1 jit_solution(1619094383106553963)
XLA Ops:
  0.7 1.1 %dynamic-slice_bitcast_fusion = bf16[32,8192]{1,0:T(8,128)(2,1)S(1)} fusion(bf16[2,32,8192]{2,1,0:T(8,128)(2,1)} %bitcast.53, s32[]{:T(128)S(6)} %select_n.75), kind=kLoop, calls=%fused_computation.44 | loop fusion | bytes 1048580 | tf_op jit(solution)/shard_map/jit(dynamic_index_in_dim)/squeeze | solution.py:103
  1.8 1.9 %collective-permute-done = bf16[32,8192]{1,0:T(8,128)(2,1)S(1)} collective-permute-done((bf16[32,8192]{1,0:T(8,128)(2,1)S(1)}, bf16[32,8192]{1,0:T(8,128)(2,1)S(1)}, u32[]{:S(2)}, u32[]{:S(2)}) %collective-permute-start) | collective-permute-done | bytes 524320 | tf_op jit(solution)/shard_map/ppermute | solution.py:75
  3.7 1.2 %fusion.23 = bf16[32,8192]{1,0:T(8,128)(2,1)S(1)} fusion(bf16[32,8192]{1,0:T(8,128)(2,1)S(1)} %collective-permute-done, bf16[2,32,8192]{2,1,0:T(8,128)(2,1)} %bitcast.54, s32[]{:T(128)S(6)} %select_n.74), kind=kLoop, calls=%fused_computation.29 | loop fusion | flops 1048576 | bytes 1572868 | tf_op jit(solution)/shard_map/convert_element_type | solution.py:106
  4.9 1.7 %collective-permute-start.1 = (bf16[32,8192]{1,0:T(8,128)(2,1)S(1)}, bf16[32,8192]{1,0:T(8,128)(2,1)S(1)}, u32[]{:S(2)}, u32[]{:S(2)}) collective-permute-start(bf16[32,8192]{1,0:T(8,128)(2,1)S(1)} %fusion.23), channel_id=1, source_target_pairs={{0,2},{1,3},{2,0},{3,1},{4,6},{5,7},{6,4},{7,5},{8,10},{9,11},{10,... | collective-permute-start | bytes 1572872 | tf_op jit(solution)/shard_map/ppermute | solution.py:75
  6.6 6.4 %shard_map.121 = (f32[32,2048]{1,0:T(8,128)}, f32[32,2048]{1,0:T(8,128)}, f32[32,2048]{1,0:T(8,128)}) custom-call(s32[8]{0:T(128)} %len_ref.3, bf16[64,2048]{1,0:T(8,128)(2,1)} %q_ref.2, bf16[8,2,1024,256]{3,2,1,0:T(8,128)(2,1)} %v_ref.3, bf16[8,2,1024,256]{3,2,1,0:T(8,128)(2,1)} %v_ref.3), custom_call_target="tpu_custom_call" | custom-call | flops 268435456 | bytes 5111808 | tf_op jit(solution)/shard_map/pallas_call | solution.py:53
  13.0 5.9 %collective-permute-done.1 = bf16[32,8192]{1,0:T(8,128)(2,1)S(1)} collective-permute-done((bf16[32,8192]{1,0:T(8,128)(2,1)S(1)}, bf16[32,8192]{1,0:T(8,128)(2,1)S(1)}, u32[]{:S(2)}, u32[]{:S(2)}) %collective-permute-start.1) | collective-permute-done | bytes 524320 | tf_op jit(solution)/shard_map/ppermute | solution.py:75
  18.9 1.5 %fusion.9 = (f32[32]{0:T(128)S(1)}, bf16[32,8192]{1,0:T(8,128)(2,1)S(1)}) fusion(bf16[32,8192]{1,0:T(8,128)(2,1)S(1)} %collective-permute-done.1, bf16[32,8192]{1,0:T(8,128)(2,1)S(1)} %collective-permute-done, bf16[2,32,8192]{2,1,0:T(8,128)(2,1)S(1)} %bitcast.55, s32[]{:T(128)S(6)} %select_n.74, bf16[2,32,8192]{2,1,0:T(8,128)(2,1)} %bitcast.66), kind=kLoop, calls=%fused_computation.12 | loop fusion | flops 2883552 | bytes 2621572 | tf_op jit(solution)/shard_map/reduce_sum | solution.py:122
  20.4 0.2 fusion.11
  20.8 0.2 convert_reduce_fusion
  21.0 0.6 collective-permute-start.3
  21.6 0.8 collective-permute-done.2
  22.5 1.4 %fusion.2 = bf16[32,8,2176]{2,1,0:T(8,128)(2,1)} fusion(bf16[64,128]{1,0:T(8,128)(2,1)S(1)} %broadcast_in_dim.27, bf16[64,2048]{1,0:T(8,128)(2,1)S(1)} %maximum_select_fusion.2, s32[64]{0:T(128)S(1)} %multiply_add_fusion), kind=kOutput, calls=%fused_computation.3 | convolution fusion | flops 72433664 | bytes 1392896 | tf_op jit(solution)/shard_map/dot_general | solution.py:175
  23.9 11.0 %all-to-all-start = ((bf16[32,8,2176]{2,1,0:T(8,128)(2,1)}), bf16[32,8,2176]{2,1,0:T(8,128)(2,1)S(1)}, u32[]{:S(2)}, u32[]{:S(2)}) async-start(bf16[32,8,2176]{2,1,0:T(8,128)(2,1)} %fusion.2), calls=%async_computation | async-start | bytes 2228224 | tf_op jit(solution)/shard_map/all_to_all | solution.py:185
  35.0 1.2 %copy.40 = bf16[128,8,2,256]{3,1,2,0:T(8,128)(2,1)} copy(bf16[128,8,2,256]{3,2,1,0:T(2,128)(2,1)S(1)} %bitcast.61) | data formatting | bytes 2097152
  36.3 0.1 copy.41
  36.4 6.3 %shard_map.122 = (f32[32,2048]{1,0:T(8,128)}, f32[32,2048]{1,0:T(8,128)}, f32[32,2048]{1,0:T(8,128)}) custom-call(s32[8]{0:T(128)} %len_ref.3, bf16[64,2048]{1,0:T(8,128)(2,1)} %q_ref.2, bf16[8,2,1024,256]{3,2,1,0:T(8,128)(2,1)} %v_ref.3, bf16[8,2,1024,256]{3,2,1,0:T(8,128)(2,1)} %v_ref.3), custom_call_target="tpu_custom_call" | custom-call | flops 268435456 | bytes 5111808 | tf_op jit(solution)/shard_map/pallas_call | solution.py:53
  42.6 5.3 %fusion.5 = f32[2,8,8,256]{3,2,1,0:T(8,128)S(1)} fusion(bf16[2,8192,256]{2,0,1:T(2,128)(2,1)} %bitcast.67, bf16[32,8192]{1,0:T(8,128)(2,1)} %collective-permute-done.3, bf16[32,8192]{1,0:T(8,128)(2,1)S(1)} %fusion.11, pred[]{:T(512)S(6)} %eq.50), kind=kOutput, calls=%fused_computation.9 | convolution fusion | flops 541589504 | bytes 9568257 | tf_op jit(solution)/shard_map/rf,hfd->rhd/dot_general | solution.py:154
  48.0 7.4 %all-to-all-done = bf16[32,8,2176]{2,1,0:T(8,128)(2,1)S(1)} async-done(((bf16[32,8,2176]{2,1,0:T(8,128)(2,1)}), bf16[32,8,2176]{2,1,0:T(8,128)(2,1)S(1)}, u32[]{:S(2)}, u32[]{:S(2)}) %all-to-all-start) | async-done | bytes 1114144 | tf_op jit(solution)/shard_map/all_to_all | solution.py:185
  55.3 0.1 add_reduce_fusion
  55.5 4.0 %fusion.12 = f32[256,1024]{0,1:T(8,128)S(1)} fusion(bf16[2048,1024]{1,0:T(8,128)(2,1)} %param.14, bf16[256,2176]{1,0:T(8,128)(2,1)S(1)} %bitcast.60), kind=kOutput, calls=%fused_computation.15 | convolution fusion | flops 1073741824 | bytes 6291456 | tf_op jit(solution)/shard_map/dot_general | solution.py:203
  59.5 0.1 select_reduce_fusion
  59.6 0.7 collective-permute-start.5
  60.3 1.5 %collective-permute-start.4 = (f32[256,64]{0,1:T(8,128)S(1)}, f32[256,64]{0,1:T(8,128)S(1)}, u32[]{:S(2)}, u32[]{:S(2)}) collective-permute-start(f32[256,64]{0,1:T(8,128)S(1)} %select_reduce_fusion), channel_id=1, source_target_pairs={{0,1},{1,0},{2,3},{3,2},{4,5},{5,4},{6,7},{7,6},{8,9},{9,8},{10,11... | collective-permute-start | bytes 196616 | tf_op jit(solution)/shard_map/ppermute | solution.py:75
  61.8 2.8 %collective-permute-done.5 = f32[256,64]{0,1:T(8,128)S(1)} collective-permute-done((f32[256,64]{0,1:T(8,128)S(1)}, f32[256,64]{0,1:T(8,128)S(1)}, u32[]{:S(2)}, u32[]{:S(2)}) %collective-permute-start.5) | collective-permute-done | bytes 65568 | tf_op jit(solution)/shard_map/ppermute | solution.py:75
  64.7 1.2 %fusion.4 = bf16[32,8,512]{2,1,0:T(8,128)(2,1)} fusion(bf16[256,1024]{0,1:T(8,128)(2,1)S(1)} %bitcast.64, bf16[1024,512]{1,0:T(8,128)(2,1)S(1)} %bitcast.62), kind=kOutput, calls=%fused_computation.8 | convolution fusion | flops 268697600 | bytes 1835008 | tf_op jit(solution)/shard_map/dot_general | solution.py:215
  65.9 4.5 %all-to-all-start.1 = ((bf16[32,8,512]{2,1,0:T(8,128)(2,1)}), bf16[32,8,512]{2,1,0:T(8,128)(2,1)S(1)}, u32[]{:S(2)}, u32[]{:S(2)}) async-start(bf16[32,8,512]{2,1,0:T(8,128)(2,1)} %fusion.4), calls=%async_computation.1 | async-start | bytes 524288 | tf_op jit(solution)/shard_map/all_to_all | solution.py:218
  70.4 0.8 maximum_select_fusion.1
  71.2 10.6 %all-to-all-done.1 = bf16[32,8,512]{2,1,0:T(8,128)(2,1)S(1)} async-done(((bf16[32,8,512]{2,1,0:T(8,128)(2,1)}), bf16[32,8,512]{2,1,0:T(8,128)(2,1)S(1)}, u32[]{:S(2)}, u32[]{:S(2)}) %all-to-all-start.1) | async-done | bytes 262176 | tf_op jit(solution)/shard_map/all_to_all | solution.py:218
  81.8 0.2 fusion.8
  82.1 0.3 multiply_reduce_fusion
  82.6 0.2 max.11
  82.8 1.2 %fusion.26 = bf16[64,2048]{1,0:T(8,128)(2,1)} fusion(f32[8,8,16,128]{3,2,1,0:T(8,128)S(1)} %bitcast.57, f32[32,2048]{1,0:T(8,128)S(1)} %copy-done.9, f32[32,2048]{1,0:T(8,128)S(1)} %copy-done.7, f32[64,2048]{1,0:T(8,128)S(1)} %constant_dynamic-update-slice_fusion, f32[32,2048]{1,0:T(8,128)S(1)} %copy-done.10, f32[32,2048]{1,0:T(8,128)S(1)} %copy-done.8, ...), kind=kLoop, calls=%fused_computation.36 | loop fusion | flops 1835008 | bytes 2883584 | tf_op jit(solution)/shard_map/convert_element_type | solution.py:251
  (54 shorter events, 0.9 us)
Async XLA Ops:
  0.6 6.0 %copy-start.11 = (bf16[8192]{0:T(1024)(128)(2,1)S(1)}, bf16[8192]{0:T(1024)(128)(2,1)}, u32[]{:S(2)}) copy-start(bf16[8192]{0:T(1024)(128)(2,1)} %param.12) | copy-start | bytes 49156
  1.7 2.0 %collective-permute-start = (bf16[32,8192]{1,0:T(8,128)(2,1)S(1)}, bf16[32,8192]{1,0:T(8,128)(2,1)S(1)}, u32[]{:S(2)}, u32[]{:S(2)}) collective-permute-start(bf16[32,8192]{1,0:T(8,128)(2,1)S(1)} %dynamic-slice_bitcast_fusion), channel_id=1, source_target_pairs={{0,1},{1,0},{2,3},{3,2},{4,5},{5,4},{6,7},{7,6},{8,9},{9,8},{10,11... | collective-permute-start | bytes 1572872 | tf_op jit(solution)/shard_map/ppermute | solution.py:75
  4.9 14.0 %collective-permute-start.1 = (bf16[32,8192]{1,0:T(8,128)(2,1)S(1)}, bf16[32,8192]{1,0:T(8,128)(2,1)S(1)}, u32[]{:S(2)}, u32[]{:S(2)}) collective-permute-start(bf16[32,8192]{1,0:T(8,128)(2,1)S(1)} %fusion.23), channel_id=1, source_target_pairs={{0,2},{1,3},{2,0},{3,1},{4,6},{5,7},{6,4},{7,5},{8,10},{9,11},{10,... | collective-permute-start | bytes 1572872 | tf_op jit(solution)/shard_map/ppermute | solution.py:75
  6.6 6.4 %copy-start.12 = (s32[64]{0:T(128)S(1)}, s32[64]{0:T(128)}, u32[]{:S(2)}) copy-start(s32[64]{0:T(128)} %param.16) | copy-start | bytes 772
  6.6 12.3 %copy-start.1 = (bf16[1,64,8192]{2,1,0:T(8,128)(2,1)S(1)}, bf16[1,64,8192]{2,1,0:T(8,128)(2,1)}, u32[]{:S(2)}) copy-start(bf16[1,64,8192]{2,1,0:T(8,128)(2,1)} %param.10) | copy-start | bytes 3145732
  20.7 1.6 %collective-permute-start.2 = (bf16[32,4096]{1,0:T(8,128)(2,1)S(1)}, bf16[32,4096]{1,0:T(8,128)(2,1)S(1)}, u32[]{:S(2)}, u32[]{:S(2)}) collective-permute-start(bf16[32,4096]{1,0:T(8,128)(2,1)S(1)} %pad_maximum_fusion), channel_id=1, source_target_pairs={{0,1},{1,0},{2,3},{3,2},{4,5},{5,4},{6,7},{7,6},{8,9},{9,8},{10,11... | collective-permute-start | bytes 786440 | tf_op jit(solution)/shard_map/ppermute | solution.py:75
  21.0 21.6 %collective-permute-start.3 = (bf16[32,8192]{1,0:T(8,128)(2,1)S(1)}, bf16[32,8192]{1,0:T(8,128)(2,1)}, u32[]{:S(2)}, u32[]{:S(2)}) collective-permute-start(bf16[32,8192]{1,0:T(8,128)(2,1)S(1)} %fusion.11), channel_id=1, source_target_pairs={{0,1},{1,0},{2,3},{3,2},{4,5},{5,4},{6,7},{7,6},{8,9},{9,8},{10,11... | collective-permute-start | bytes 1572872 | tf_op jit(solution)/shard_map/ppermute | solution.py:75
  22.4 12.6 %copy-start.2 = (bf16[1024,2,256]{2,1,0:T(2,128)(2,1)S(1)}, bf16[1024,2,256]{2,1,0:T(2,128)(2,1)}, u32[]{:S(2)}) copy-start(bf16[1024,2,256]{2,1,0:T(2,128)(2,1)} %param.15) | copy-start | bytes 3145732
  23.9 12.3 %copy-start = (bf16[64,2048]{1,0:T(8,128)(2,1)S(1)}, bf16[64,2048]{1,0:T(8,128)(2,1)}, u32[]{:S(2)}) copy-start(bf16[64,2048]{1,0:T(8,128)(2,1)} %q_ref.2) | copy-start | bytes 786436
  23.9 31.4 %all-to-all-start = ((bf16[32,8,2176]{2,1,0:T(8,128)(2,1)}), bf16[32,8,2176]{2,1,0:T(8,128)(2,1)S(1)}, u32[]{:S(2)}, u32[]{:S(2)}) async-start(bf16[32,8,2176]{2,1,0:T(8,128)(2,1)} %fusion.2), calls=%async_computation | async-start | bytes 2228224 | tf_op jit(solution)/shard_map/all_to_all | solution.py:185
  55.5 6.3 %copy-start.5 = (f32[32,2048]{1,0:T(8,128)S(1)}, f32[32,2048]{1,0:T(8,128)}, u32[]{:S(2)}) copy-start(f32[32,2048]{1,0:T(8,128)} %get-tuple-element.33) | copy-start | bytes 786436
  59.5 5.2 %copy-start.3 = (bf16[128,8,2,256]{3,1,2,0:T(8,128)(2,1)S(1)}, bf16[128,8,2,256]{3,1,2,0:T(8,128)(2,1)}, u32[]{:S(2)}) copy-start(bf16[128,8,2,256]{3,1,2,0:T(8,128)(2,1)} %copy.40) | copy-start | bytes 3145732
  59.6 5.0 %collective-permute-start.5 = (f32[256,64]{0,1:T(8,128)S(1)}, f32[256,64]{0,1:T(8,128)S(1)}, u32[]{:S(2)}, u32[]{:S(2)}) collective-permute-start(f32[256,64]{0,1:T(8,128)S(1)} %select_reduce_fusion), channel_id=1, source_target_pairs={{0,2},{1,3},{2,0},{3,1},{4,6},{5,7},{6,4},{7,5},{8,10},{9,11},{10,... | collective-permute-start | bytes 196616 | tf_op jit(solution)/shard_map/ppermute | solution.py:75
  60.3 4.4 %collective-permute-start.6 = (f32[256,64]{0,1:T(8,128)S(1)}, f32[256,64]{0,1:T(8,128)S(1)}, u32[]{:S(2)}, u32[]{:S(2)}) collective-permute-start(f32[256,64]{0,1:T(8,128)S(1)} %select_reduce_fusion), channel_id=1, source_target_pairs={{0,3},{1,2},{2,1},{3,0},{4,7},{5,6},{6,5},{7,4},{8,11},{9,10},{10,... | collective-permute-start | bytes 196616 | tf_op jit(solution)/shard_map/ppermute | solution.py:75
  60.3 4.4 %collective-permute-start.4 = (f32[256,64]{0,1:T(8,128)S(1)}, f32[256,64]{0,1:T(8,128)S(1)}, u32[]{:S(2)}, u32[]{:S(2)}) collective-permute-start(f32[256,64]{0,1:T(8,128)S(1)} %select_reduce_fusion), channel_id=1, source_target_pairs={{0,1},{1,0},{2,3},{3,2},{4,5},{5,4},{6,7},{7,6},{8,9},{9,8},{10,11... | collective-permute-start | bytes 196616 | tf_op jit(solution)/shard_map/ppermute | solution.py:75
  61.8 9.3 %copy-start.6 = (f32[32,2048]{1,0:T(8,128)S(1)}, f32[32,2048]{1,0:T(8,128)}, u32[]{:S(2)}) copy-start(f32[32,2048]{1,0:T(8,128)} %get-tuple-element.34) | copy-start | bytes 786436
  65.9 16.9 %copy-start.7 = (f32[32,2048]{1,0:T(8,128)S(1)}, f32[32,2048]{1,0:T(8,128)}, u32[]{:S(2)}) copy-start(f32[32,2048]{1,0:T(8,128)} %get-tuple-element.35) | copy-start | bytes 786436
  65.9 16.9 %copy-start.8 = (f32[32,2048]{1,0:T(8,128)S(1)}, f32[32,2048]{1,0:T(8,128)}, u32[]{:S(2)}) copy-start(f32[32,2048]{1,0:T(8,128)} %get-tuple-element.37) | copy-start | bytes 786436
  65.9 16.9 %copy-start.9 = (f32[32,2048]{1,0:T(8,128)S(1)}, f32[32,2048]{1,0:T(8,128)}, u32[]{:S(2)}) copy-start(f32[32,2048]{1,0:T(8,128)} %get-tuple-element.36) | copy-start | bytes 786436
  65.9 16.9 %copy-start.10 = (f32[32,2048]{1,0:T(8,128)S(1)}, f32[32,2048]{1,0:T(8,128)}, u32[]{:S(2)}) copy-start(f32[32,2048]{1,0:T(8,128)} %get-tuple-element.38) | copy-start | bytes 786436
  65.9 15.9 %all-to-all-start.1 = ((bf16[32,8,512]{2,1,0:T(8,128)(2,1)}), bf16[32,8,512]{2,1,0:T(8,128)(2,1)S(1)}, u32[]{:S(2)}, u32[]{:S(2)}) async-start(bf16[32,8,512]{2,1,0:T(8,128)(2,1)} %fusion.4), calls=%async_computation.1 | async-start | bytes 524288 | tf_op jit(solution)/shard_map/all_to_all | solution.py:218
  82.0 2.0 %copy-start.4 = (bf16[64,2,256]{2,1,0:T(2,128)(2,1)}, bf16[64,2,256]{2,1,0:T(2,128)(2,1)S(1)}, u32[]{:S(2)}) copy-start(bf16[64,2,256]{2,1,0:T(2,128)(2,1)S(1)} %reshape.117) | copy-start | bytes 196612

commit v10 on v9

--- a/solution.py
+++ b/solution.py
@@ -181,20 +181,8 @@
         .reshape(adapt_count, capacity, quarter + ID_LANES)
     )
     flattened_up = adapter_up_weight.reshape(adapter_grouped * ADAPTER_RANK, -1)
-    payload, queries_late = lax.optimization_barrier((payload, queries))
     rows_in = lax.all_to_all(payload, "adapter", split_axis=0, concat_axis=0, tiled=True)
-    attention_late = cache_attention(
-        queries_late,
-        key_value_cache,
-        prompt_cache_length,
-        local_heads,
-        FAN,
-        early_prompts,
-        local_prompts - early_prompts,
-    )
-    rows_in, base_kv, attention_late = lax.optimization_barrier(
-        (rows_in, base_kv, attention_late)
-    )
+    rows_in, base_kv = lax.optimization_barrier((rows_in, base_kv))
     item_count = rows_in.shape[1]
     rows_in = rows_in.reshape(slot_count, quarter + ID_LANES)
     flattened_rows = rows_in[:, :quarter]
@@ -215,7 +203,18 @@
         ADAPTER_SCALE * jnp.dot(expanded_rows, flattened_up, preferred_element_type=jnp.float32)
     ).astype(jnp.bfloat16)
     adapter_update = adapter_update.reshape(adapt_count, item_count, -1)
+    adapter_update, queries_late = lax.optimization_barrier((adapter_update, queries))
     returned = lax.all_to_all(adapter_update, "adapter", split_axis=0, concat_axis=0, tiled=True)
+    attention_late = cache_attention(
+        queries_late,
+        key_value_cache,
+        prompt_cache_length,
+        local_heads,
+        FAN,
+        early_prompts,
+        local_prompts - early_prompts,
+    )
+    returned, attention_late = lax.optimization_barrier((returned, attention_late))
     returned = returned.reshape(slot_count, -1)
     update_rows = lax.dot_general(
         slot_matrix, returned, (((0,), (0,)), ((), ())), preferred_element_type=jnp.float32

time: 84.7 us -> 85.8 us (1.013)
  local copies, waits for them, and re-layouts: 3.06 us -> 4.01 us
    all_to_all x1, waiting for transfers between devices: 7.37 us -> 13.6 us  [per_device(): lax.all_to_all(payload, 'adapter', split_axis=0, concat_axis=0, tiled=True)]
    all_to_all x1, waiting for transfers between devices: 10.6 us -> 4.53 us  [per_device(): lax.all_to_all(adapter_update, 'adapter', split_axis=0, concat_axis=0, ti...]
    concatenate x1, local copies, waits for them, and re-layouts: 0.02 us -> 0.98 us  [per_device(): jnp.concatenate([early, late], axis=0)]
  transfers between devices with their start and end apart: 9 -> 9, of which waited for: 6 -> 7; matrix products, arithmetic and copies ran while one was open for 11% -> 11% of each run, Pallas kernels for 15% -> 15%
where the time goes in v10:
time: 85.8 us; the launch traced here: 85.1 us
  waiting for transfers between devices  30.2 us (35%)
  starting transfers between devices  19.4 us (23%)
  Pallas kernels  12.6 us (15%)
  matrix products  12.1 us (14%)
  other arithmetic  5.77 us (7%)
  local copies, waits for them, and re-layouts  4.01 us (5%)
  between operations  1.01 us (1%)
    all_to_all x1, waiting for transfers between devices, per_device(): lax.all_to_all(payload, 'adapter', split_axis=0, concat_axis=0, tiled=True)  13.6 us
    pallas_call x2, Pallas kernels, cache_attention(): pl.pallas_call(kernel, out_shape=(out, out, out), grid_spec=pltpu.Prefetc...  12.6 us
    ppermute x7, waiting for transfers between devices, _swap(): return lax.ppermute(x, 'tensor', perm=[(i, i ^ mask) for i in range(count)])  12 us
    all_to_all x1, starting transfers between devices, per_device(): lax.all_to_all(payload, 'adapter', split_axis=0, concat_axis=0, tiled=True)  11 us
    dot_general x1, matrix products, per_device(): jnp.einsum('rf,hfd->rhd', normed_full, head_weight, preferred_element_typ...  5.29 us
    all_to_all x1, waiting for transfers between devices, per_device(): lax.all_to_all(adapter_update, 'adapter', split_axis=0, concat_axis=0, ti...  4.53 us
    ppermute x7, starting transfers between devices, _swap(): return lax.ppermute(x, 'tensor', perm=[(i, i ^ mask) for i in range(count)])  4.36 us
    all_to_all x1, starting transfers between devices, per_device(): lax.all_to_all(adapter_update, 'adapter', split_axis=0, concat_axis=0, ti...  4.04 us
  transfers between devices with their start and end apart: 9, of which 7 were waited for; matrix products, arithmetic and copies ran while one was open for 11% of the time, Pallas kernels for 15%

profile of v10, /device:TPU:0, one launch (start us, length us, event | category | flops | bytes accessed | tf_op | source)
XLA Modules:
  0.0 85.1 jit_solution(13622397499214226873)
XLA Ops:
  0.7 1.1 %dynamic-slice_bitcast_fusion = bf16[32,8192]{1,0:T(8,128)(2,1)S(1)} fusion(bf16[2,32,8192]{2,1,0:T(8,128)(2,1)} %bitcast.53, s32[]{:T(128)S(6)} %select_n.75), kind=kLoop, calls=%fused_computation.44 | loop fusion | bytes 1048580 | tf_op jit(solution)/shard_map/jit(dynamic_index_in_dim)/squeeze | solution.py:103
  1.8 1.9 %collective-permute-done = bf16[32,8192]{1,0:T(8,128)(2,1)S(1)} collective-permute-done((bf16[32,8192]{1,0:T(8,128)(2,1)S(1)}, bf16[32,8192]{1,0:T(8,128)(2,1)S(1)}, u32[]{:S(2)}, u32[]{:S(2)}) %collective-permute-start) | collective-permute-done | bytes 524320 | tf_op jit(solution)/shard_map/ppermute | solution.py:75
  3.7 1.2 %fusion.23 = bf16[32,8192]{1,0:T(8,128)(2,1)S(1)} fusion(bf16[32,8192]{1,0:T(8,128)(2,1)S(1)} %collective-permute-done, bf16[2,32,8192]{2,1,0:T(8,128)(2,1)} %bitcast.54, s32[]{:T(128)S(6)} %select_n.74), kind=kLoop, calls=%fused_computation.29 | loop fusion | flops 1048576 | bytes 1572868 | tf_op jit(solution)/shard_map/convert_element_type | solution.py:106
  4.9 1.7 %collective-permute-start.1 = (bf16[32,8192]{1,0:T(8,128)(2,1)S(1)}, bf16[32,8192]{1,0:T(8,128)(2,1)S(1)}, u32[]{:S(2)}, u32[]{:S(2)}) collective-permute-start(bf16[32,8192]{1,0:T(8,128)(2,1)S(1)} %fusion.23), channel_id=1, source_target_pairs={{0,2},{1,3},{2,0},{3,1},{4,6},{5,7},{6,4},{7,5},{8,10},{9,11},{10,... | collective-permute-start | bytes 1572872 | tf_op jit(solution)/shard_map/ppermute | solution.py:75
  6.6 6.4 %shard_map.121 = (f32[32,2048]{1,0:T(8,128)}, f32[32,2048]{1,0:T(8,128)}, f32[32,2048]{1,0:T(8,128)}) custom-call(s32[8]{0:T(128)} %len_ref.3, bf16[64,2048]{1,0:T(8,128)(2,1)} %q_ref.2, bf16[8,2,1024,256]{3,2,1,0:T(8,128)(2,1)} %v_ref.3, bf16[8,2,1024,256]{3,2,1,0:T(8,128)(2,1)} %v_ref.3), custom_call_target="tpu_custom_call" | custom-call | flops 268435456 | bytes 5111808 | tf_op jit(solution)/shard_map/pallas_call | solution.py:53
  13.0 5.9 %collective-permute-done.1 = bf16[32,8192]{1,0:T(8,128)(2,1)S(1)} collective-permute-done((bf16[32,8192]{1,0:T(8,128)(2,1)S(1)}, bf16[32,8192]{1,0:T(8,128)(2,1)S(1)}, u32[]{:S(2)}, u32[]{:S(2)}) %collective-permute-start.1) | collective-permute-done | bytes 524320 | tf_op jit(solution)/shard_map/ppermute | solution.py:75
  18.9 1.5 %fusion.9 = (f32[32]{0:T(128)S(1)}, bf16[32,8192]{1,0:T(8,128)(2,1)S(1)}) fusion(bf16[32,8192]{1,0:T(8,128)(2,1)S(1)} %collective-permute-done.1, bf16[32,8192]{1,0:T(8,128)(2,1)S(1)} %collective-permute-done, bf16[2,32,8192]{2,1,0:T(8,128)(2,1)S(1)} %bitcast.55, s32[]{:T(128)S(6)} %select_n.74, bf16[2,32,8192]{2,1,0:T(8,128)(2,1)} %bitcast.66), kind=kLoop, calls=%fused_computation.12 | loop fusion | flops 2883552 | bytes 2621572 | tf_op jit(solution)/shard_map/reduce_sum | solution.py:122
  20.4 0.2 fusion.11
  20.8 0.2 convert_reduce_fusion
  21.0 0.6 collective-permute-start.3
  21.6 0.8 collective-permute-done.2
  22.5 1.4 %fusion.2 = bf16[32,8,2176]{2,1,0:T(8,128)(2,1)} fusion(bf16[64,128]{1,0:T(8,128)(2,1)S(1)} %broadcast_in_dim.27, bf16[64,2048]{1,0:T(8,128)(2,1)S(1)} %maximum_select_fusion.2, s32[64]{0:T(128)S(1)} %multiply_add_fusion), kind=kOutput, calls=%fused_computation.3 | convolution fusion | flops 72433664 | bytes 1392896 | tf_op jit(solution)/shard_map/dot_general | solution.py:175
  23.9 11.0 %all-to-all-start = ((bf16[32,8,2176]{2,1,0:T(8,128)(2,1)}), bf16[32,8,2176]{2,1,0:T(8,128)(2,1)S(1)}, u32[]{:S(2)}, u32[]{:S(2)}) async-start(bf16[32,8,2176]{2,1,0:T(8,128)(2,1)} %fusion.2), calls=%async_computation | async-start | bytes 2228224 | tf_op jit(solution)/shard_map/all_to_all | solution.py:184
  35.0 1.2 %copy.40 = bf16[128,8,2,256]{3,1,2,0:T(8,128)(2,1)} copy(bf16[128,8,2,256]{3,2,1,0:T(2,128)(2,1)S(1)} %bitcast.61) | data formatting | bytes 2097152
  36.4 5.3 %fusion.5 = f32[2,8,8,256]{3,2,1,0:T(8,128)S(1)} fusion(bf16[2,8192,256]{2,0,1:T(2,128)(2,1)} %bitcast.67, bf16[32,8192]{1,0:T(8,128)(2,1)} %collective-permute-done.3, bf16[32,8192]{1,0:T(8,128)(2,1)S(1)} %fusion.11, pred[]{:T(512)S(6)} %eq.50), kind=kOutput, calls=%fused_computation.9 | convolution fusion | flops 541589504 | bytes 9568257 | tf_op jit(solution)/shard_map/rf,hfd->rhd/dot_general | solution.py:154
  41.7 13.6 %all-to-all-done = bf16[32,8,2176]{2,1,0:T(8,128)(2,1)S(1)} async-done(((bf16[32,8,2176]{2,1,0:T(8,128)(2,1)}), bf16[32,8,2176]{2,1,0:T(8,128)(2,1)S(1)}, u32[]{:S(2)}, u32[]{:S(2)}) %all-to-all-start) | async-done | bytes 1114144 | tf_op jit(solution)/shard_map/all_to_all | solution.py:184
  55.3 0.1 add_reduce_fusion
  55.4 4.0 %fusion.12 = f32[256,1024]{0,1:T(8,128)S(1)} fusion(bf16[2048,1024]{1,0:T(8,128)(2,1)} %param.14, bf16[256,2176]{1,0:T(8,128)(2,1)S(1)} %bitcast.60), kind=kOutput, calls=%fused_computation.15 | convolution fusion | flops 1073741824 | bytes 6291456 | tf_op jit(solution)/shard_map/dot_general | solution.py:191
  59.6 0.7 collective-permute-start.5
  60.3 1.2 %collective-permute-start.6 = (f32[256,64]{0,1:T(8,128)S(1)}, f32[256,64]{0,1:T(8,128)S(1)}, u32[]{:S(2)}, u32[]{:S(2)}) collective-permute-start(f32[256,64]{0,1:T(8,128)S(1)} %select_reduce_fusion), channel_id=1, source_target_pairs={{0,3},{1,2},{2,1},{3,0},{4,7},{5,6},{6,5},{7,4},{8,11},{9,10},{10,... | collective-permute-start | bytes 196616 | tf_op jit(solution)/shard_map/ppermute | solution.py:75
  61.5 3.2 %collective-permute-done.5 = f32[256,64]{0,1:T(8,128)S(1)} collective-permute-done((f32[256,64]{0,1:T(8,128)S(1)}, f32[256,64]{0,1:T(8,128)S(1)}, u32[]{:S(2)}, u32[]{:S(2)}) %collective-permute-start.5) | collective-permute-done | bytes 65568 | tf_op jit(solution)/shard_map/ppermute | solution.py:75
  64.7 0.3 collective-permute-done.6
  65.1 1.2 %fusion.4 = bf16[32,8,512]{2,1,0:T(8,128)(2,1)} fusion(bf16[256,1024]{0,1:T(8,128)(2,1)S(1)} %bitcast.64, bf16[1024,512]{1,0:T(8,128)(2,1)S(1)} %bitcast.62), kind=kOutput, calls=%fused_computation.8 | convolution fusion | flops 268697600 | bytes 1835008 | tf_op jit(solution)/shard_map/dot_general | solution.py:203
  66.2 4.0 %all-to-all-start.1 = ((bf16[32,8,512]{2,1,0:T(8,128)(2,1)}), bf16[32,8,512]{2,1,0:T(8,128)(2,1)S(1)}, u32[]{:S(2)}, u32[]{:S(2)}) async-start(bf16[32,8,512]{2,1,0:T(8,128)(2,1)} %fusion.4), calls=%async_computation.1 | async-start | bytes 524288 | tf_op jit(solution)/shard_map/all_to_all | solution.py:207
  70.3 0.8 maximum_select_fusion.1
  71.0 6.3 %shard_map.122 = (f32[32,2048]{1,0:T(8,128)}, f32[32,2048]{1,0:T(8,128)}, f32[32,2048]{1,0:T(8,128)}) custom-call(s32[8]{0:T(128)} %len_ref.3, bf16[64,2048]{1,0:T(8,128)(2,1)} %q_ref.2, bf16[8,2,1024,256]{3,2,1,0:T(8,128)(2,1)} %v_ref.3, bf16[8,2,1024,256]{3,2,1,0:T(8,128)(2,1)} %v_ref.3), custom_call_target="tpu_custom_call" | custom-call | flops 268435456 | bytes 5111808 | tf_op jit(solution)/shard_map/pallas_call | solution.py:53
  77.3 4.5 %all-to-all-done.1 = bf16[32,8,512]{2,1,0:T(8,128)(2,1)S(1)} async-done(((bf16[32,8,512]{2,1,0:T(8,128)(2,1)}), bf16[32,8,512]{2,1,0:T(8,128)(2,1)S(1)}, u32[]{:S(2)}, u32[]{:S(2)}) %all-to-all-start.1) | async-done | bytes 262176 | tf_op jit(solution)/shard_map/all_to_all | solution.py:207
  81.8 0.2 fusion.8
  82.1 0.3 multiply_reduce_fusion
  82.6 1.0 %constant_dynamic-update-slice_fusion = f32[64,2048]{1,0:T(8,128)S(1)} fusion(f32[64,2048]{1,0:T(8,128)S(1)} %constant_dynamic-update-slice_fusion.1, f32[32,2048]{1,0:T(8,128)} %get-tuple-element.36), kind=kLoop, calls=%fused_computation.65 | loop fusion | bytes 524288 | tf_op jit(solution)/shard_map/concatenate | solution.py:229
  83.6 0.2 max.11
  83.8 1.3 %fusion.26 = bf16[64,2048]{1,0:T(8,128)(2,1)} fusion(f32[8,8,16,128]{3,2,1,0:T(8,128)S(1)} %bitcast.58, f32[32,2048]{1,0:T(8,128)S(1)} %copy-done.8, f32[32,2048]{1,0:T(8,128)S(1)} %copy-done.6, f32[64,2048]{1,0:T(8,128)S(1)} %constant_dynamic-update-slice_fusion, f32[32,2048]{1,0:T(8,128)S(1)} %copy-done.9, f32[32,2048]{1,0:T(8,128)S(1)} %copy-done.7, ...), kind=kLoop, calls=%fused_computation.36 | loop fusion | flops 1835008 | bytes 2883584 | tf_op jit(solution)/shard_map/convert_element_type | solution.py:250
  (52 shorter events, 1.1 us)
Async XLA Ops:
  0.6 6.0 %copy-start.10 = (bf16[8192]{0:T(1024)(128)(2,1)S(1)}, bf16[8192]{0:T(1024)(128)(2,1)}, u32[]{:S(2)}) copy-start(bf16[8192]{0:T(1024)(128)(2,1)} %param.12) | copy-start | bytes 49156
  1.7 2.0 %collective-permute-start = (bf16[32,8192]{1,0:T(8,128)(2,1)S(1)}, bf16[32,8192]{1,0:T(8,128)(2,1)S(1)}, u32[]{:S(2)}, u32[]{:S(2)}) collective-permute-start(bf16[32,8192]{1,0:T(8,128)(2,1)S(1)} %dynamic-slice_bitcast_fusion), channel_id=1, source_target_pairs={{0,1},{1,0},{2,3},{3,2},{4,5},{5,4},{6,7},{7,6},{8,9},{9,8},{10,11... | collective-permute-start | bytes 1572872 | tf_op jit(solution)/shard_map/ppermute | solution.py:75
  4.9 14.0 %collective-permute-start.1 = (bf16[32,8192]{1,0:T(8,128)(2,1)S(1)}, bf16[32,8192]{1,0:T(8,128)(2,1)S(1)}, u32[]{:S(2)}, u32[]{:S(2)}) collective-permute-start(bf16[32,8192]{1,0:T(8,128)(2,1)S(1)} %fusion.23), channel_id=1, source_target_pairs={{0,2},{1,3},{2,0},{3,1},{4,6},{5,7},{6,4},{7,5},{8,10},{9,11},{10,... | collective-permute-start | bytes 1572872 | tf_op jit(solution)/shard_map/ppermute | solution.py:75
  6.6 6.4 %copy-start.11 = (s32[64]{0:T(128)S(1)}, s32[64]{0:T(128)}, u32[]{:S(2)}) copy-start(s32[64]{0:T(128)} %param.16) | copy-start | bytes 772
  6.6 12.3 %copy-start.1 = (bf16[1,64,8192]{2,1,0:T(8,128)(2,1)S(1)}, bf16[1,64,8192]{2,1,0:T(8,128)(2,1)}, u32[]{:S(2)}) copy-start(bf16[1,64,8192]{2,1,0:T(8,128)(2,1)} %param.10) | copy-start | bytes 3145732
  20.7 1.6 %collective-permute-start.2 = (bf16[32,4096]{1,0:T(8,128)(2,1)S(1)}, bf16[32,4096]{1,0:T(8,128)(2,1)S(1)}, u32[]{:S(2)}, u32[]{:S(2)}) collective-permute-start(bf16[32,4096]{1,0:T(8,128)(2,1)S(1)} %pad_maximum_fusion), channel_id=1, source_target_pairs={{0,1},{1,0},{2,3},{3,2},{4,5},{5,4},{6,7},{7,6},{8,9},{9,8},{10,11... | collective-permute-start | bytes 786440 | tf_op jit(solution)/shard_map/ppermute | solution.py:75
  21.0 15.3 %collective-permute-start.3 = (bf16[32,8192]{1,0:T(8,128)(2,1)S(1)}, bf16[32,8192]{1,0:T(8,128)(2,1)}, u32[]{:S(2)}, u32[]{:S(2)}) collective-permute-start(bf16[32,8192]{1,0:T(8,128)(2,1)S(1)} %fusion.11), channel_id=1, source_target_pairs={{0,1},{1,0},{2,3},{3,2},{4,5},{5,4},{6,7},{7,6},{8,9},{9,8},{10,11... | collective-permute-start | bytes 1572872 | tf_op jit(solution)/shard_map/ppermute | solution.py:75
  22.4 12.6 %copy-start.2 = (bf16[1024,2,256]{2,1,0:T(2,128)(2,1)S(1)}, bf16[1024,2,256]{2,1,0:T(2,128)(2,1)}, u32[]{:S(2)}) copy-start(bf16[1024,2,256]{2,1,0:T(2,128)(2,1)} %param.15) | copy-start | bytes 3145732
  23.9 12.3 %copy-start = (bf16[64,2048]{1,0:T(8,128)(2,1)S(1)}, bf16[64,2048]{1,0:T(8,128)(2,1)}, u32[]{:S(2)}) copy-start(bf16[64,2048]{1,0:T(8,128)(2,1)} %q_ref.2) | copy-start | bytes 786436
  23.9 31.4 %all-to-all-start = ((bf16[32,8,2176]{2,1,0:T(8,128)(2,1)}), bf16[32,8,2176]{2,1,0:T(8,128)(2,1)S(1)}, u32[]{:S(2)}, u32[]{:S(2)}) async-start(bf16[32,8,2176]{2,1,0:T(8,128)(2,1)} %fusion.2), calls=%async_computation | async-start | bytes 2228224 | tf_op jit(solution)/shard_map/all_to_all | solution.py:184
  55.4 6.1 %copy-start.5 = (f32[32,2048]{1,0:T(8,128)S(1)}, f32[32,2048]{1,0:T(8,128)}, u32[]{:S(2)}) copy-start(f32[32,2048]{1,0:T(8,128)} %get-tuple-element.35) | copy-start | bytes 786436
  59.4 5.6 %copy-start.3 = (bf16[128,8,2,256]{3,1,2,0:T(8,128)(2,1)S(1)}, bf16[128,8,2,256]{3,1,2,0:T(8,128)(2,1)}, u32[]{:S(2)}) copy-start(bf16[128,8,2,256]{3,1,2,0:T(8,128)(2,1)} %copy.40) | copy-start | bytes 3145732
  59.5 2.0 %collective-permute-start.4 = (f32[256,64]{0,1:T(8,128)S(1)}, f32[256,64]{0,1:T(8,128)S(1)}, u32[]{:S(2)}, u32[]{:S(2)}) collective-permute-start(f32[256,64]{0,1:T(8,128)S(1)} %select_reduce_fusion), channel_id=1, source_target_pairs={{0,1},{1,0},{2,3},{3,2},{4,5},{5,4},{6,7},{7,6},{8,9},{9,8},{10,11... | collective-permute-start | bytes 196616 | tf_op jit(solution)/shard_map/ppermute | solution.py:75
  59.6 5.0 %collective-permute-start.5 = (f32[256,64]{0,1:T(8,128)S(1)}, f32[256,64]{0,1:T(8,128)S(1)}, u32[]{:S(2)}, u32[]{:S(2)}) collective-permute-start(f32[256,64]{0,1:T(8,128)S(1)} %select_reduce_fusion), channel_id=1, source_target_pairs={{0,2},{1,3},{2,0},{3,1},{4,6},{5,7},{6,4},{7,5},{8,10},{9,11},{10,... | collective-permute-start | bytes 196616 | tf_op jit(solution)/shard_map/ppermute | solution.py:75
  60.3 4.7 %collective-permute-start.6 = (f32[256,64]{0,1:T(8,128)S(1)}, f32[256,64]{0,1:T(8,128)S(1)}, u32[]{:S(2)}, u32[]{:S(2)}) collective-permute-start(f32[256,64]{0,1:T(8,128)S(1)} %select_reduce_fusion), channel_id=1, source_target_pairs={{0,3},{1,2},{2,1},{3,0},{4,7},{5,6},{6,5},{7,4},{8,11},{9,10},{10,... | collective-permute-start | bytes 196616 | tf_op jit(solution)/shard_map/ppermute | solution.py:75
  66.2 15.6 %all-to-all-start.1 = ((bf16[32,8,512]{2,1,0:T(8,128)(2,1)}), bf16[32,8,512]{2,1,0:T(8,128)(2,1)S(1)}, u32[]{:S(2)}, u32[]{:S(2)}) async-start(bf16[32,8,512]{2,1,0:T(8,128)(2,1)} %fusion.4), calls=%async_computation.1 | async-start | bytes 524288 | tf_op jit(solution)/shard_map/all_to_all | solution.py:207
  77.3 6.5 %copy-start.6 = (f32[32,2048]{1,0:T(8,128)S(1)}, f32[32,2048]{1,0:T(8,128)}, u32[]{:S(2)}) copy-start(f32[32,2048]{1,0:T(8,128)} %get-tuple-element.37) | copy-start | bytes 786436
  77.3 6.5 %copy-start.7 = (f32[32,2048]{1,0:T(8,128)S(1)}, f32[32,2048]{1,0:T(8,128)}, u32[]{:S(2)}) copy-start(f32[32,2048]{1,0:T(8,128)} %get-tuple-element.39) | copy-start | bytes 786436
  77.3 6.5 %copy-start.8 = (f32[32,2048]{1,0:T(8,128)S(1)}, f32[32,2048]{1,0:T(8,128)}, u32[]{:S(2)}) copy-start(f32[32,2048]{1,0:T(8,128)} %get-tuple-element.38) | copy-start | bytes 786436
  77.3 6.5 %copy-start.9 = (f32[32,2048]{1,0:T(8,128)S(1)}, f32[32,2048]{1,0:T(8,128)}, u32[]{:S(2)}) copy-start(f32[32,2048]{1,0:T(8,128)} %get-tuple-element.40) | copy-start | bytes 786436
  82.1 3.1 %copy-start.4 = (bf16[64,2,256]{2,1,0:T(2,128)(2,1)}, bf16[64,2,256]{2,1,0:T(2,128)(2,1)S(1)}, u32[]{:S(2)}) copy-start(bf16[64,2,256]{2,1,0:T(2,128)(2,1)S(1)} %reshape.117) | copy-start | bytes 196612

commit v11 on v10

--- a/solution.py
+++ b/solution.py
@@ -138,7 +138,6 @@
     hidden_mine = lax.dynamic_slice_in_dim(hidden_half, own_cols, quarter, 1)
     normed_other = from_partner[:, :quarter]
     hidden_other = from_partner[:, quarter:]
-
     first = core == 0
 
     def by_core(mine, other):
@@ -182,7 +181,6 @@
     )
     flattened_up = adapter_up_weight.reshape(adapter_grouped * ADAPTER_RANK, -1)
     rows_in = lax.all_to_all(payload, "adapter", split_axis=0, concat_axis=0, tiled=True)
-    rows_in, base_kv = lax.optimization_barrier((rows_in, base_kv))
     item_count = rows_in.shape[1]
     rows_in = rows_in.reshape(slot_count, quarter + ID_LANES)
     flattened_rows = rows_in[:, :quarter]
@@ -192,10 +190,9 @@
         flattened_rows, adapter_down_weight, preferred_element_type=jnp.float32
     ).reshape(-1, adapter_grouped, ADAPTER_RANK)
     partial_low = jnp.sum(jnp.where(adapter_pick[:, :, None], projected_rows, 0.0), axis=1)
-    low_core = _swap(partial_low, 1, tensor_count)
-    low_chip = _swap(partial_low, 2, tensor_count)
-    low_diag = _swap(partial_low, 3, tensor_count)
-    reduced_rank_rows = ((partial_low + low_core) + (low_chip + low_diag)).astype(jnp.bfloat16)
+    pair_low = partial_low + _swap(partial_low, 1, tensor_count)
+    far_low, base_kv = lax.optimization_barrier((_swap(pair_low, 2, tensor_count), base_kv))
+    reduced_rank_rows = (pair_low + far_low).astype(jnp.bfloat16)
     expanded_rows = jnp.where(
         adapter_pick[:, :, None], reduced_rank_rows[:, None, :], jnp.zeros((), jnp.bfloat16)
     ).reshape(-1, adapter_grouped * ADAPTER_RANK)
@@ -203,10 +200,9 @@
         ADAPTER_SCALE * jnp.dot(expanded_rows, flattened_up, preferred_element_type=jnp.float32)
     ).astype(jnp.bfloat16)
     adapter_update = adapter_update.reshape(adapt_count, item_count, -1)
-    adapter_update, queries_late = lax.optimization_barrier((adapter_update, queries))
     returned = lax.all_to_all(adapter_update, "adapter", split_axis=0, concat_axis=0, tiled=True)
     attention_late = cache_attention(
-        queries_late,
+        queries,
         key_value_cache,
         prompt_cache_length,
         local_heads,
@@ -230,24 +226,25 @@
         for early, late in zip(attention_early, attention_late)
     ]
     view = (row_dev, local_heads, group_size, HEAD_SIZE)
-    flat = (row_dev, local_heads * group_size, HEAD_SIZE)
-    query_wide = queries.reshape(view).astype(jnp.float32)
-    own_key = new_kv[:, :, :HEAD_SIZE].astype(jnp.float32)[:, :, None, :]
-    own_value = jnp.broadcast_to(
-        new_kv[:, :, HEAD_SIZE:].astype(jnp.float32)[:, :, None, :], view
-    ).reshape(flat)
-    own_score = (jnp.sum(query_wide * own_key, axis=-1) * score_scale).reshape(
-        row_dev, local_heads * group_size, 1
-    )
-    cache_weighted = num_c.reshape(flat)
-    cache_top = top_c.reshape(flat)
-    cache_total = tot_c.reshape(flat)
+    cache_weighted = num_c.reshape(view)
+    cache_top = top_c.reshape(view)[..., 0]
+    cache_total = tot_c.reshape(view)[..., 0]
+    query_heads = queries.reshape(view)
+    own_key = new_kv[:, :, :HEAD_SIZE]
+    own_value = new_kv[:, :, HEAD_SIZE:]
+    own_score = (
+        jnp.einsum("rkgd,rkd->rkg", query_heads, own_key, preferred_element_type=jnp.float32)
+        * score_scale
+    )
     score_top = jnp.maximum(cache_top, own_score)
     rescale = jnp.exp(cache_top - score_top)
     own_weight = jnp.exp(own_score - score_top).astype(jnp.bfloat16).astype(jnp.float32)
     weight_total = rescale * cache_total + own_weight
-    weighted = rescale * cache_weighted + own_weight * own_value
-    attended = (weighted / weight_total).astype(jnp.bfloat16).reshape(row_dev, -1)
+    weighted = (
+        rescale[..., None] * cache_weighted
+        + own_weight[..., None] * own_value.astype(jnp.float32)[:, :, None, :]
+    )
+    attended = (weighted / weight_total[..., None]).astype(jnp.bfloat16).reshape(row_dev, -1)
     return (hidden_part, new_kv, attended)
 
 

time: 85.8 us -> 88.5 us (1.031)
  waiting for transfers between devices: 30.2 us -> 33.7 us
  starting transfers between devices: 19.4 us -> 17.9 us
  other arithmetic: 5.77 us -> 6.72 us
    all_to_all x1, waiting for transfers between devices: 13.6 us -> 20.3 us  [per_device(): lax.all_to_all(payload, 'adapter', split_axis=0, concat_axis=0, tiled=True)]
    ppermute x7 -> x6, waiting for transfers between devices: 12 us -> 9.72 us  [_swap(): return lax.ppermute(x, 'tensor', perm=[(i, i ^ mask) for i in range(count)])]
    ppermute x7 -> x6, starting transfers between devices: 4.36 us -> 2.69 us  [_swap(): return lax.ppermute(x, 'tensor', perm=[(i, i ^ mask) for i in range(count)])]
    unnamed x1, other arithmetic: 0.04 us -> 1.1 us
    concatenate x1 -> x0, local copies, waits for them, and re-layouts: 0.98 us -> none  [per_device(): jnp.concatenate([early, late], axis=0)]
  transfers between devices with their start and end apart: 9 -> 8, of which waited for: 7 -> 6; matrix products, arithmetic and copies ran while one was open for 11% -> 12% of each run, Pallas kernels for 15% -> 15%
where the time goes in v11:
time: 88.5 us; the launch traced here: 87.8 us
  waiting for transfers between devices  33.7 us (38%)
  starting transfers between devices  17.9 us (20%)
  Pallas kernels  12.8 us (14%)
  matrix products  12.1 us (14%)
  other arithmetic  6.72 us (8%)
  local copies, waits for them, and re-layouts  3.49 us (4%)
  between operations  1.04 us (1%)
    all_to_all x1, waiting for transfers between devices, per_device(): lax.all_to_all(payload, 'adapter', split_axis=0, concat_axis=0, tiled=True)  20.3 us
    pallas_call x2, Pallas kernels, cache_attention(): pl.pallas_call(kernel, out_shape=(out, out, out), grid_spec=pltpu.Prefetc...  12.8 us
    all_to_all x1, starting transfers between devices, per_device(): lax.all_to_all(payload, 'adapter', split_axis=0, concat_axis=0, tiled=True)  10.9 us
    ppermute x6, waiting for transfers between devices, _swap(): return lax.ppermute(x, 'tensor', perm=[(i, i ^ mask) for i in range(count)])  9.72 us
    dot_general x1, matrix products, per_device(): jnp.einsum('rf,hfd->rhd', normed_full, head_weight, preferred_element_typ...  4.97 us
    all_to_all x1, starting transfers between devices, per_device(): lax.all_to_all(adapter_update, 'adapter', split_axis=0, concat_axis=0, ti...  4.32 us
    dot_general x1, matrix products, per_device(): jnp.dot(flattened_rows, adapter_down_weight, preferred_element_type=jnp.f...  4.03 us
    all_to_all x1, waiting for transfers between devices, per_device(): lax.all_to_all(adapter_update, 'adapter', split_axis=0, concat_axis=0, ti...  3.78 us
  transfers between devices with their start and end apart: 8, of which 6 were waited for; matrix products, arithmetic and copies ran while one was open for 12% of the time, Pallas kernels for 15%

profile of v11, /device:TPU:0, one launch (start us, length us, event | category | flops | bytes accessed | tf_op | source)
XLA Modules:
  0.0 87.8 jit_solution(13439118262839570931)
XLA Ops:
  0.7 1.1 %dynamic-slice_bitcast_fusion = bf16[32,8192]{1,0:T(8,128)(2,1)S(1)} fusion(bf16[2,32,8192]{2,1,0:T(8,128)(2,1)} %bitcast.91, s32[]{:T(128)S(6)} %select_n.75), kind=kLoop, calls=%fused_computation.34 | loop fusion | bytes 1048580 | tf_op jit(solution)/shard_map/jit(dynamic_index_in_dim)/squeeze | solution.py:103
  1.8 1.9 %collective-permute-done = bf16[32,8192]{1,0:T(8,128)(2,1)S(1)} collective-permute-done((bf16[32,8192]{1,0:T(8,128)(2,1)S(1)}, bf16[32,8192]{1,0:T(8,128)(2,1)S(1)}, u32[]{:S(2)}, u32[]{:S(2)}) %collective-permute-start) | collective-permute-done | bytes 524320 | tf_op jit(solution)/shard_map/ppermute | solution.py:75
  3.7 1.2 %fusion.22 = bf16[32,8192]{1,0:T(8,128)(2,1)S(1)} fusion(bf16[32,8192]{1,0:T(8,128)(2,1)S(1)} %collective-permute-done, bf16[2,32,8192]{2,1,0:T(8,128)(2,1)} %bitcast.92, s32[]{:T(128)S(6)} %select_n.74), kind=kLoop, calls=%fused_computation.27 | loop fusion | flops 1048576 | bytes 1572868 | tf_op jit(solution)/shard_map/convert_element_type | solution.py:106
  4.9 1.7 %collective-permute-start.1 = (bf16[32,8192]{1,0:T(8,128)(2,1)S(1)}, bf16[32,8192]{1,0:T(8,128)(2,1)S(1)}, u32[]{:S(2)}, u32[]{:S(2)}) collective-permute-start(bf16[32,8192]{1,0:T(8,128)(2,1)S(1)} %fusion.22), channel_id=1, source_target_pairs={{0,2},{1,3},{2,0},{3,1},{4,6},{5,7},{6,4},{7,5},{8,10},{9,11},{10,... | collective-permute-start | bytes 1572872 | tf_op jit(solution)/shard_map/ppermute | solution.py:75
  6.6 6.4 %shard_map.121 = (f32[32,2048]{1,0:T(8,128)}, f32[32,2048]{1,0:T(8,128)}, f32[32,2048]{1,0:T(8,128)}) custom-call(s32[8]{0:T(128)} %len_ref.3, bf16[64,2048]{1,0:T(8,128)(2,1)} %q_ref.3, bf16[8,2,1024,256]{3,2,1,0:T(8,128)(2,1)} %v_ref.3, bf16[8,2,1024,256]{3,2,1,0:T(8,128)(2,1)} %v_ref.3), custom_call_target="tpu_custom_call" | custom-call | flops 268435456 | bytes 5111808 | tf_op jit(solution)/shard_map/pallas_call | solution.py:53
  13.0 5.9 %collective-permute-done.1 = bf16[32,8192]{1,0:T(8,128)(2,1)S(1)} collective-permute-done((bf16[32,8192]{1,0:T(8,128)(2,1)S(1)}, bf16[32,8192]{1,0:T(8,128)(2,1)S(1)}, u32[]{:S(2)}, u32[]{:S(2)}) %collective-permute-start.1) | collective-permute-done | bytes 524320 | tf_op jit(solution)/shard_map/ppermute | solution.py:75
  18.9 1.5 %fusion.8 = (f32[32]{0:T(128)S(1)}, bf16[32,8192]{1,0:T(8,128)(2,1)S(1)}) fusion(bf16[32,8192]{1,0:T(8,128)(2,1)S(1)} %collective-permute-done.1, bf16[32,8192]{1,0:T(8,128)(2,1)S(1)} %collective-permute-done, bf16[2,32,8192]{2,1,0:T(8,128)(2,1)S(1)} %bitcast.93, s32[]{:T(128)S(6)} %select_n.74, bf16[2,32,8192]{2,1,0:T(8,128)(2,1)} %bitcast.106), kind=kLoop, calls=%fused_computation.10 | loop fusion | flops 2883552 | bytes 2621572 | tf_op jit(solution)/shard_map/reduce_sum | solution.py:122
  20.4 0.2 fusion.10
  21.0 1.3 %collective-permute-done.2 = bf16[32,4096]{1,0:T(8,128)(2,1)S(1)} collective-permute-done((bf16[32,4096]{1,0:T(8,128)(2,1)S(1)}, bf16[32,4096]{1,0:T(8,128)(2,1)S(1)}, u32[]{:S(2)}, u32[]{:S(2)}) %collective-permute-start.2) | collective-permute-done | bytes 262176 | tf_op jit(solution)/shard_map/ppermute | solution.py:75
  22.5 1.5 %fusion.2 = bf16[32,8,2176]{2,1,0:T(8,128)(2,1)} fusion(bf16[64,128]{1,0:T(8,128)(2,1)S(1)} %broadcast_in_dim.25, bf16[64,2048]{1,0:T(8,128)(2,1)S(1)} %maximum_select_fusion.2, s32[64]{0:T(128)S(1)} %multiply_add_fusion), kind=kOutput, calls=%fused_computation.3 | convolution fusion | flops 72433664 | bytes 1392896 | tf_op jit(solution)/shard_map/dot_general | solution.py:174
  24.0 10.9 %all-to-all-start = ((bf16[32,8,2176]{2,1,0:T(8,128)(2,1)}), bf16[32,8,2176]{2,1,0:T(8,128)(2,1)S(1)}, u32[]{:S(2)}, u32[]{:S(2)}) async-start(bf16[32,8,2176]{2,1,0:T(8,128)(2,1)} %fusion.2), calls=%async_computation | async-start | bytes 2228224 | tf_op jit(solution)/shard_map/all_to_all | solution.py:183
  35.0 20.3 %all-to-all-done = bf16[32,8,2176]{2,1,0:T(8,128)(2,1)S(1)} async-done(((bf16[32,8,2176]{2,1,0:T(8,128)(2,1)}), bf16[32,8,2176]{2,1,0:T(8,128)(2,1)S(1)}, u32[]{:S(2)}, u32[]{:S(2)}) %all-to-all-start) | async-done | bytes 1114144 | tf_op jit(solution)/shard_map/all_to_all | solution.py:183
  55.2 4.0 %fusion.11 = f32[256,1024]{0,1:T(8,128)S(1)} fusion(bf16[2048,1024]{1,0:T(8,128)(2,1)} %param.14, bf16[256,2176]{1,0:T(8,128)(2,1)S(1)} %bitcast.99), kind=kOutput, calls=%fused_computation.13 | convolution fusion | flops 1073741824 | bytes 6291456 | tf_op jit(solution)/shard_map/dot_general | solution.py:189
  59.6 0.2 copy.46
  59.8 0.4 copy-done
  60.3 0.6 collective-permute-done.3
  60.9 0.7 collective-permute-start.4
  61.5 5.0 %fusion.5 = f32[2,8,8,256]{3,2,1,0:T(8,128)S(1)} fusion(bf16[2,8192,256]{2,0,1:T(2,128)(2,1)} %bitcast.108, bf16[32,8192]{1,0:T(8,128)(2,1)S(1)} %collective-permute-done.5, bf16[32,8192]{1,0:T(8,128)(2,1)S(1)} %fusion.10, pred[]{:T(512)S(6)} %eq.50), kind=kOutput, calls=%fused_computation.9 | convolution fusion | flops 541589504 | bytes 9568257 | tf_op jit(solution)/shard_map/rf,hfd->rhd/dot_general | solution.py:153
  66.6 1.2 %fusion.4 = bf16[32,8,512]{2,1,0:T(8,128)(2,1)} fusion(bf16[256,1024]{0,1:T(8,128)(2,1)S(1)} %bitcast.104, bf16[1024,512]{1,0:T(8,128)(2,1)S(1)} %bitcast.102), kind=kOutput, calls=%fused_computation.8 | convolution fusion | flops 268697600 | bytes 1835008 | tf_op jit(solution)/shard_map/dot_general | solution.py:200
  67.8 4.3 %all-to-all-start.1 = ((bf16[32,8,512]{2,1,0:T(8,128)(2,1)}), bf16[32,8,512]{2,1,0:T(8,128)(2,1)S(1)}, u32[]{:S(2)}, u32[]{:S(2)}) async-start(bf16[32,8,512]{2,1,0:T(8,128)(2,1)} %fusion.4), calls=%async_computation.1 | async-start | bytes 524288 | tf_op jit(solution)/shard_map/all_to_all | solution.py:203
  72.1 6.4 %shard_map.122 = (f32[32,2048]{1,0:T(8,128)}, f32[32,2048]{1,0:T(8,128)}, f32[32,2048]{1,0:T(8,128)}) custom-call(s32[8]{0:T(128)} %len_ref.3, bf16[64,2048]{1,0:T(8,128)(2,1)} %q_ref.3, bf16[8,2,1024,256]{3,2,1,0:T(8,128)(2,1)} %v_ref.3, bf16[8,2,1024,256]{3,2,1,0:T(8,128)(2,1)} %v_ref.3), custom_call_target="tpu_custom_call" | custom-call | flops 268435456 | bytes 5111808 | tf_op jit(solution)/shard_map/pallas_call | solution.py:53
  78.5 0.8 maximum_select_fusion.1
  79.3 3.8 %all-to-all-done.1 = bf16[32,8,512]{2,1,0:T(8,128)(2,1)S(1)} async-done(((bf16[32,8,512]{2,1,0:T(8,128)(2,1)}), bf16[32,8,512]{2,1,0:T(8,128)(2,1)S(1)}, u32[]{:S(2)}, u32[]{:S(2)}) %all-to-all-start.1) | async-done | bytes 262176 | tf_op jit(solution)/shard_map/all_to_all | solution.py:203
  83.1 1.1 %maximum_bitcast_fusion = (f32[8,8,16,128]{3,1,2,0:T(8,128)S(1)}, f32[8,8,16,128]{3,1,2,0:T(8,128)S(1)}) fusion(f32[32,2048]{1,0:T(8,128)} %get-tuple-element.32, f32[32,2048]{1,0:T(8,128)S(1)} %copy-done.6, f32[32,2048]{1,0:T(8,128)} %get-tuple-element.36, f32[32,2048]{1,0:T(8,128)S(1)} %copy-done.7), kind=kLoop, calls=%fused_computation.32 | loop fusion | flops 262144 | bytes 2097152
  84.3 0.3 copy.43
  84.7 0.3 copy.44
  85.0 0.2 fusion.27
  85.3 0.3 fusion.31
  86.0 0.2 broadcast_multiply_fusion
  86.2 0.2 mul.87
  86.4 0.2 div.35
  86.6 1.2 %fusion.23 = bf16[64,2048]{1,0:T(8,128)(2,1)} fusion(f32[8,8,16,128]{3,2,1,0:T(8,128)S(1)} %bitcast.98, f32[8,8,16,128]{3,2,1,0:T(8,128)S(1)} %bitcast.94, f32[8,8,16,128]{3,2,1,0:T(8,128)S(1)} %bitcast.97, f32[32,2048]{1,0:T(8,128)S(1)} %copy-done.4, f32[32,2048]{1,0:T(8,128)S(1)} %copy-done.3), kind=kLoop, calls=%fused_computation.29 | loop fusion | flops 655360 | bytes 2359296 | tf_op jit(solution)/shard_map/convert_element_type | solution.py:247
  (54 shorter events, 1.8 us)
Async XLA Ops:
  0.6 6.0 %copy-start.8 = (bf16[8192]{0:T(1024)(128)(2,1)S(1)}, bf16[8192]{0:T(1024)(128)(2,1)}, u32[]{:S(2)}) copy-start(bf16[8192]{0:T(1024)(128)(2,1)} %param.12) | copy-start | bytes 49156
  1.7 2.0 %collective-permute-start = (bf16[32,8192]{1,0:T(8,128)(2,1)S(1)}, bf16[32,8192]{1,0:T(8,128)(2,1)S(1)}, u32[]{:S(2)}, u32[]{:S(2)}) collective-permute-start(bf16[32,8192]{1,0:T(8,128)(2,1)S(1)} %dynamic-slice_bitcast_fusion), channel_id=1, source_target_pairs={{0,1},{1,0},{2,3},{3,2},{4,5},{5,4},{6,7},{7,6},{8,9},{9,8},{10,11... | collective-permute-start | bytes 1572872 | tf_op jit(solution)/shard_map/ppermute | solution.py:75
  4.9 14.0 %collective-permute-start.1 = (bf16[32,8192]{1,0:T(8,128)(2,1)S(1)}, bf16[32,8192]{1,0:T(8,128)(2,1)S(1)}, u32[]{:S(2)}, u32[]{:S(2)}) collective-permute-start(bf16[32,8192]{1,0:T(8,128)(2,1)S(1)} %fusion.22), channel_id=1, source_target_pairs={{0,2},{1,3},{2,0},{3,1},{4,6},{5,7},{6,4},{7,5},{8,10},{9,11},{10,... | collective-permute-start | bytes 1572872 | tf_op jit(solution)/shard_map/ppermute | solution.py:75
  6.6 6.4 %copy-start.9 = (s32[64]{0:T(128)S(1)}, s32[64]{0:T(128)}, u32[]{:S(2)}) copy-start(s32[64]{0:T(128)} %param.16) | copy-start | bytes 772
  6.6 12.3 %copy-start.1 = (bf16[1,64,8192]{2,1,0:T(8,128)(2,1)S(1)}, bf16[1,64,8192]{2,1,0:T(8,128)(2,1)}, u32[]{:S(2)}) copy-start(bf16[1,64,8192]{2,1,0:T(8,128)(2,1)} %param.10) | copy-start | bytes 3145732
  20.7 1.6 %collective-permute-start.2 = (bf16[32,4096]{1,0:T(8,128)(2,1)S(1)}, bf16[32,4096]{1,0:T(8,128)(2,1)S(1)}, u32[]{:S(2)}, u32[]{:S(2)}) collective-permute-start(bf16[32,4096]{1,0:T(8,128)(2,1)S(1)} %pad_maximum_fusion), channel_id=1, source_target_pairs={{0,1},{1,0},{2,3},{3,2},{4,5},{5,4},{6,7},{7,6},{8,9},{9,8},{10,11... | collective-permute-start | bytes 786440 | tf_op jit(solution)/shard_map/ppermute | solution.py:75
  24.0 31.3 %all-to-all-start = ((bf16[32,8,2176]{2,1,0:T(8,128)(2,1)}), bf16[32,8,2176]{2,1,0:T(8,128)(2,1)S(1)}, u32[]{:S(2)}, u32[]{:S(2)}) async-start(bf16[32,8,2176]{2,1,0:T(8,128)(2,1)} %fusion.2), calls=%async_computation | async-start | bytes 2228224 | tf_op jit(solution)/shard_map/all_to_all | solution.py:183
  34.9 26.7 %collective-permute-start.5 = (bf16[32,8192]{1,0:T(8,128)(2,1)S(1)}, bf16[32,8192]{1,0:T(8,128)(2,1)S(1)}, u32[]{:S(2)}, u32[]{:S(2)}) collective-permute-start(bf16[32,8192]{1,0:T(8,128)(2,1)S(1)} %fusion.10), channel_id=1, source_target_pairs={{0,1},{1,0},{2,3},{3,2},{4,5},{5,4},{6,7},{7,6},{8,9},{9,8},{10,11... | collective-permute-start | bytes 1572872 | tf_op jit(solution)/shard_map/ppermute | solution.py:75
  55.2 4.4 %copy-start.2 = (bf16[1024,2,256]{2,1,0:T(2,128)(2,1)S(1)}, bf16[1024,2,256]{2,1,0:T(2,128)(2,1)}, u32[]{:S(2)}) copy-start(bf16[1024,2,256]{2,1,0:T(2,128)(2,1)} %param.15) | copy-start | bytes 3145732
  59.3 1.0 %copy-start = (bf16[64,2048]{1,0:T(8,128)(2,1)S(1)}, bf16[64,2048]{1,0:T(8,128)(2,1)}, u32[]{:S(2)}) copy-start(bf16[64,2048]{1,0:T(8,128)(2,1)} %q_ref.3) | copy-start | bytes 786436
  59.5 1.3 %collective-permute-start.3 = (f32[256,64]{0,1:T(8,128)S(1)}, f32[256,64]{0,1:T(8,128)S(1)}, u32[]{:S(2)}, u32[]{:S(2)}) collective-permute-start(f32[256,64]{0,1:T(8,128)S(1)} %select_reduce_fusion), channel_id=1, source_target_pairs={{0,1},{1,0},{2,3},{3,2},{4,5},{5,4},{6,7},{7,6},{8,9},{9,8},{10,11... | collective-permute-start | bytes 196616 | tf_op jit(solution)/shard_map/ppermute | solution.py:75
  60.9 5.7 %collective-permute-start.4 = (f32[256,64]{0,1:T(8,128)S(1)}, f32[256,64]{0,1:T(8,128)S(1)}, u32[]{:S(2)}, u32[]{:S(2)}) collective-permute-start(f32[256,64]{0,1:T(8,128)S(1)} %add.86), channel_id=1, source_target_pairs={{0,2},{1,3},{2,0},{3,1},{4,6},{5,7},{6,4},{7,5},{8,10},{9,11},{10,... | collective-permute-start | bytes 196616 | tf_op jit(solution)/shard_map/ppermute | solution.py:75
  67.8 15.3 %all-to-all-start.1 = ((bf16[32,8,512]{2,1,0:T(8,128)(2,1)}), bf16[32,8,512]{2,1,0:T(8,128)(2,1)S(1)}, u32[]{:S(2)}, u32[]{:S(2)}) async-start(bf16[32,8,512]{2,1,0:T(8,128)(2,1)} %fusion.4), calls=%async_computation.1 | async-start | bytes 524288 | tf_op jit(solution)/shard_map/all_to_all | solution.py:203
  72.1 11.0 %copy-start.6 = (f32[32,2048]{1,0:T(8,128)S(1)}, f32[32,2048]{1,0:T(8,128)}, u32[]{:S(2)}) copy-start(f32[32,2048]{1,0:T(8,128)} %get-tuple-element.31) | copy-start | bytes 786436
  72.1 11.0 %copy-start.7 = (f32[32,2048]{1,0:T(8,128)S(1)}, f32[32,2048]{1,0:T(8,128)}, u32[]{:S(2)}) copy-start(f32[32,2048]{1,0:T(8,128)} %get-tuple-element.35) | copy-start | bytes 786436
  84.6 2.0 %copy-start.3 = (f32[32,2048]{1,0:T(8,128)S(1)}, f32[32,2048]{1,0:T(8,128)}, u32[]{:S(2)}) copy-start(f32[32,2048]{1,0:T(8,128)} %get-tuple-element.33) | copy-start | bytes 786436
  84.7 2.0 %copy-start.4 = (f32[32,2048]{1,0:T(8,128)S(1)}, f32[32,2048]{1,0:T(8,128)}, u32[]{:S(2)}) copy-start(f32[32,2048]{1,0:T(8,128)} %get-tuple-element.34) | copy-start | bytes 786436
  85.2 2.6 %copy-start.5 = (bf16[64,2,256]{2,1,0:T(2,128)(2,1)}, bf16[64,2,256]{2,1,0:T(2,128)(2,1)S(1)}, u32[]{:S(2)}) copy-start(bf16[64,2,256]{2,1,0:T(2,128)(2,1)S(1)} %reshape.114) | copy-start | bytes 196612

commit v12 on v3

--- a/solution.py
+++ b/solution.py
@@ -159,20 +159,24 @@
     row_slot = owner_index * capacity + slot_rank
     row_to_slot = jnp.arange(slot_count)[:, None] == row_slot[None, :]
     slot_matrix = row_to_slot.astype(jnp.bfloat16)
-    send_rows = jnp.dot(slot_matrix, normed_part, preferred_element_type=jnp.float32).astype(
-        jnp.bfloat16
-    )
-    send_ids = jnp.sum(jnp.where(row_to_slot, local_id[None, :] + 1, 0), axis=1) - 1
-    id_block = jnp.broadcast_to(send_ids.astype(jnp.bfloat16)[:, None], (slot_count, ID_LANES))
-    payload = jnp.concatenate([send_rows, id_block], axis=1).reshape(
-        adapt_count, capacity, quarter + ID_LANES
+    id_block = jnp.broadcast_to(
+        (local_id + 1).astype(jnp.bfloat16)[:, None], (row_dev, ID_LANES)
+    )
+    payload = (
+        jnp.dot(
+            slot_matrix,
+            jnp.concatenate([normed_part, id_block], axis=1),
+            preferred_element_type=jnp.float32,
+        )
+        .astype(jnp.bfloat16)
+        .reshape(adapt_count, capacity, quarter + ID_LANES)
     )
     flattened_up = adapter_up_weight.reshape(adapter_grouped * ADAPTER_RANK, -1)
     rows_in = lax.all_to_all(payload, "adapter", split_axis=0, concat_axis=0, tiled=True)
     item_count = rows_in.shape[1]
     rows_in = rows_in.reshape(slot_count, quarter + ID_LANES)
     flattened_rows = rows_in[:, :quarter]
-    ids_in = rows_in[:, quarter].astype(jnp.int32)
+    ids_in = rows_in[:, quarter].astype(jnp.int32) - 1
     adapter_pick = ids_in[:, None] == jnp.arange(adapter_grouped)[None, :]
     projected_rows = jnp.dot(
         flattened_rows, adapter_down_weight, preferred_element_type=jnp.float32

time: 84.2 us -> 84 us (level)
  no operation moved by 1% of the time
where the time goes in v12:
time: 84 us; the launch traced here: 83.5 us
  blocking collectives  31.3 us (37%)
  waiting for transfers between devices  15.7 us (19%)
  Pallas kernels  12.8 us (15%)
  other arithmetic  6.84 us (8%)
  starting transfers between devices  6.48 us (8%)
  matrix products  5.38 us (6%)
  local copies, waits for them, and re-layouts  3.87 us (5%)
  between operations  1.05 us (1%)
    all_to_all x1, blocking collectives, per_device(): lax.all_to_all(payload, 'adapter', split_axis=0, concat_axis=0, tiled=True)  31.3 us
    pallas_call x2, Pallas kernels, cache_attention(): pl.pallas_call(kernel, out_shape=(out, out, out), grid_spec=pltpu.Prefetc...  12.8 us
    ppermute x5, waiting for transfers between devices, _swap(): return lax.ppermute(x, 'tensor', perm=[(i, i ^ mask) for i in range(count)])  12 us
    all_to_all x1, starting transfers between devices, per_device(): lax.all_to_all(adapter_update, 'adapter', split_axis=0, concat_axis=0, ti...  3.87 us
    all_to_all x1, waiting for transfers between devices, per_device(): lax.all_to_all(adapter_update, 'adapter', split_axis=0, concat_axis=0, ti...  3.73 us
    ppermute x5, starting transfers between devices, _swap(): return lax.ppermute(x, 'tensor', perm=[(i, i ^ mask) for i in range(count)])  2.61 us
    unnamed x32, local copies, waits for them, and re-layouts  1.8 us
    dot_general x1, matrix products, per_device(): jnp.dot(flattened_rows, adapter_down_weight, preferred_element_type=jnp.f...  1.74 us
  transfers between devices with their start and end apart: 6, of which 6 were waited for; matrix products, arithmetic and copies ran while one was open for 3% of the time, Pallas kernels for 15%

profile of v12, /device:TPU:0, one launch (start us, length us, event | category | flops | bytes accessed | tf_op | source)
XLA Modules:
  0.0 83.5 jit_solution(11149646834202788021)
XLA Ops:
  0.7 1.1 %dynamic-slice_bitcast_fusion = bf16[32,8192]{1,0:T(8,128)(2,1)S(1)} fusion(bf16[2,32,8192]{2,1,0:T(8,128)(2,1)} %bitcast.91, s32[]{:T(128)S(6)} %select_n.70), kind=kLoop, calls=%fused_computation.29 | loop fusion | bytes 1048580 | tf_op jit(solution)/shard_map/jit(dynamic_index_in_dim)/squeeze | solution.py:103
  1.8 1.9 %collective-permute-done = bf16[32,8192]{1,0:T(8,128)(2,1)S(1)} collective-permute-done((bf16[32,8192]{1,0:T(8,128)(2,1)S(1)}, bf16[32,8192]{1,0:T(8,128)(2,1)S(1)}, u32[]{:S(2)}, u32[]{:S(2)}) %collective-permute-start) | collective-permute-done | bytes 524320 | tf_op jit(solution)/shard_map/ppermute | solution.py:75
  3.7 1.2 %fusion.15 = bf16[32,8192]{1,0:T(8,128)(2,1)S(1)} fusion(bf16[32,8192]{1,0:T(8,128)(2,1)S(1)} %collective-permute-done, bf16[2,32,8192]{2,1,0:T(8,128)(2,1)} %bitcast.92, s32[]{:T(128)S(6)} %select_n.69), kind=kLoop, calls=%fused_computation.21 | loop fusion | flops 1048576 | bytes 1572868 | tf_op jit(solution)/shard_map/convert_element_type | solution.py:106
  4.9 1.7 %collective-permute-start.1 = (bf16[32,8192]{1,0:T(8,128)(2,1)S(1)}, bf16[32,8192]{1,0:T(8,128)(2,1)S(1)}, u32[]{:S(2)}, u32[]{:S(2)}) collective-permute-start(bf16[32,8192]{1,0:T(8,128)(2,1)S(1)} %fusion.15), channel_id=1, source_target_pairs={{0,2},{1,3},{2,0},{3,1},{4,6},{5,7},{6,4},{7,5},{8,10},{9,11},{10,... | collective-permute-start | bytes 1572872 | tf_op jit(solution)/shard_map/ppermute | solution.py:75
  6.6 6.4 %shard_map.121 = (f32[32,2048]{1,0:T(8,128)}, f32[32,2048]{1,0:T(8,128)}, f32[32,2048]{1,0:T(8,128)}) custom-call(s32[8]{0:T(128)} %len_ref.3, bf16[64,2048]{1,0:T(8,128)(2,1)} %q_ref.3, bf16[8,2,1024,256]{3,2,1,0:T(8,128)(2,1)} %v_ref.3, bf16[8,2,1024,256]{3,2,1,0:T(8,128)(2,1)} %v_ref.3), custom_call_target="tpu_custom_call" | custom-call | flops 268435456 | bytes 5111808 | tf_op jit(solution)/shard_map/pallas_call | solution.py:53
  13.0 6.0 %collective-permute-done.1 = bf16[32,8192]{1,0:T(8,128)(2,1)S(1)} collective-permute-done((bf16[32,8192]{1,0:T(8,128)(2,1)S(1)}, bf16[32,8192]{1,0:T(8,128)(2,1)S(1)}, u32[]{:S(2)}, u32[]{:S(2)}) %collective-permute-start.1) | collective-permute-done | bytes 524320 | tf_op jit(solution)/shard_map/ppermute | solution.py:75
  18.9 1.5 %fusion.8 = (f32[32]{0:T(128)S(1)}, bf16[32,8192]{1,0:T(8,128)(2,1)S(1)}) fusion(bf16[32,8192]{1,0:T(8,128)(2,1)S(1)} %collective-permute-done.1, bf16[32,8192]{1,0:T(8,128)(2,1)S(1)} %collective-permute-done, bf16[2,32,8192]{2,1,0:T(8,128)(2,1)S(1)} %bitcast.93, s32[]{:T(128)S(6)} %select_n.69, bf16[2,32,8192]{2,1,0:T(8,128)(2,1)} %bitcast.106), kind=kLoop, calls=%fused_computation.10 | loop fusion | flops 2883552 | bytes 2621572 | tf_op jit(solution)/shard_map/reduce_sum | solution.py:122
  20.8 0.3 copy-done.10
  21.3 1.6 %collective-permute-done.2 = bf16[32,10240]{1,0:T(8,128)(2,1)S(1)} collective-permute-done((bf16[32,10240]{1,0:T(8,128)(2,1)S(1)}, bf16[32,10240]{1,0:T(8,128)(2,1)S(1)}, u32[]{:S(2)}, u32[]{:S(2)}) %collective-permute-start.2) | collective-permute-done | bytes 655392 | tf_op jit(solution)/shard_map/ppermute | solution.py:75
  23.2 0.4 fusion.2
  23.7 31.3 %all_to_all.10 = bf16[32,8,2176]{2,1,0:T(8,128)(2,1)S(1)} all-to-all(bf16[32,8,2176]{2,1,0:T(8,128)(2,1)S(1)} %fusion.2), channel_id=1, replica_groups=mesh['adapter'=32,'tensor'=4] {'adapter'}, dimensions={0} | all-to-all | bytes 2228224 | tf_op jit(solution)/shard_map/all_to_all | solution.py:175
  55.2 1.7 %fusion.11 = f32[256,1024]{0,1:T(8,128)S(1)} fusion(bf16[2048,1024]{1,0:T(8,128)(2,1)S(1)} %copy-done.9, bf16[256,2176]{1,0:T(8,128)(2,1)S(1)} %bitcast.100), kind=kOutput, calls=%fused_computation.13 | convolution fusion | flops 1073741824 | bytes 6291456 | tf_op jit(solution)/shard_map/dot_general | solution.py:181
  57.1 0.2 copy.46
  57.4 0.5 copy-done
  57.9 0.5 collective-permute-done.3
  58.4 0.7 collective-permute-start.4
  59.1 1.6 %fusion.5 = f32[2,8,8,256]{3,2,1,0:T(8,128)S(1)} fusion(bf16[2,8192,256]{2,0,1:T(2,128)(2,1)S(1)} %bitcast.110, bf16[64,8192]{1,0:T(8,128)(2,1)S(1)} %maximum_select_fusion), kind=kOutput, calls=%fused_computation.9 | convolution fusion | flops 536870912 | bytes 9568256 | tf_op jit(solution)/shard_map/rf,hfd->rhd/dot_general | solution.py:145
  60.7 2.1 %collective-permute-done.4 = f32[256,64]{0,1:T(8,128)S(1)} collective-permute-done((f32[256,64]{0,1:T(8,128)S(1)}, f32[256,64]{0,1:T(8,128)S(1)}, u32[]{:S(2)}, u32[]{:S(2)}) %collective-permute-start.4) | collective-permute-done | bytes 65568 | tf_op jit(solution)/shard_map/ppermute | solution.py:75
  62.8 1.2 %fusion.4 = bf16[32,8,512]{2,1,0:T(8,128)(2,1)} fusion(bf16[256,1024]{0,1:T(8,128)(2,1)S(1)} %bitcast.104, bf16[1024,512]{1,0:T(8,128)(2,1)S(1)} %bitcast.102), kind=kOutput, calls=%fused_computation.8 | convolution fusion | flops 268697600 | bytes 1835008 | tf_op jit(solution)/shard_map/dot_general | solution.py:192
  64.0 3.9 %all-to-all-start.1 = ((bf16[32,8,512]{2,1,0:T(8,128)(2,1)}), bf16[32,8,512]{2,1,0:T(8,128)(2,1)S(1)}, u32[]{:S(2)}, u32[]{:S(2)}) async-start(bf16[32,8,512]{2,1,0:T(8,128)(2,1)} %fusion.4), calls=%async_computation.1 | async-start | bytes 524288 | tf_op jit(solution)/shard_map/all_to_all | solution.py:195
  67.9 6.4 %shard_map.122 = (f32[32,2048]{1,0:T(8,128)}, f32[32,2048]{1,0:T(8,128)}, f32[32,2048]{1,0:T(8,128)}) custom-call(s32[8]{0:T(128)} %len_ref.3, bf16[64,2048]{1,0:T(8,128)(2,1)} %q_ref.3, bf16[8,2,1024,256]{3,2,1,0:T(8,128)(2,1)} %v_ref.3, bf16[8,2,1024,256]{3,2,1,0:T(8,128)(2,1)} %v_ref.3), custom_call_target="tpu_custom_call" | custom-call | flops 268435456 | bytes 5111808 | tf_op jit(solution)/shard_map/pallas_call | solution.py:53
  74.3 0.8 maximum_select_fusion.1
  75.0 3.7 %all-to-all-done.1 = bf16[32,8,512]{2,1,0:T(8,128)(2,1)S(1)} async-done(((bf16[32,8,512]{2,1,0:T(8,128)(2,1)}), bf16[32,8,512]{2,1,0:T(8,128)(2,1)S(1)}, u32[]{:S(2)}, u32[]{:S(2)}) %all-to-all-start.1) | async-done | bytes 262176 | tf_op jit(solution)/shard_map/all_to_all | solution.py:195
  78.8 1.1 %maximum_bitcast_fusion = (f32[8,8,16,128]{3,1,2,0:T(8,128)S(1)}, f32[8,8,16,128]{3,1,2,0:T(8,128)S(1)}) fusion(f32[32,2048]{1,0:T(8,128)} %get-tuple-element.32, f32[32,2048]{1,0:T(8,128)S(1)} %copy-done.6, f32[32,2048]{1,0:T(8,128)} %get-tuple-element.36, f32[32,2048]{1,0:T(8,128)S(1)} %copy-done.7), kind=kLoop, calls=%fused_computation.27 | loop fusion | flops 262144 | bytes 2097152
  80.0 0.3 copy.43
  80.4 0.3 copy.44
  80.6 0.2 fusion.20
  81.0 0.3 fusion.24
  81.7 0.2 broadcast_multiply_fusion
  81.9 0.2 mul.88
  82.1 0.2 div.35
  82.3 1.2 %fusion.16 = bf16[64,2048]{1,0:T(8,128)(2,1)} fusion(f32[8,8,16,128]{3,2,1,0:T(8,128)S(1)} %bitcast.98, f32[8,8,16,128]{3,2,1,0:T(8,128)S(1)} %bitcast.94, f32[8,8,16,128]{3,2,1,0:T(8,128)S(1)} %bitcast.97, f32[32,2048]{1,0:T(8,128)S(1)} %copy-done.4, f32[32,2048]{1,0:T(8,128)S(1)} %copy-done.3), kind=kLoop, calls=%fused_computation.24 | loop fusion | flops 655360 | bytes 2359296 | tf_op jit(solution)/shard_map/convert_element_type | solution.py:239
  (59 shorter events, 2.1 us)
Async XLA Ops:
  0.6 6.0 %copy-start.8 = (bf16[8192]{0:T(1024)(128)(2,1)S(1)}, bf16[8192]{0:T(1024)(128)(2,1)}, u32[]{:S(2)}) copy-start(bf16[8192]{0:T(1024)(128)(2,1)} %param.12) | copy-start | bytes 49156
  1.7 2.0 %collective-permute-start = (bf16[32,8192]{1,0:T(8,128)(2,1)S(1)}, bf16[32,8192]{1,0:T(8,128)(2,1)S(1)}, u32[]{:S(2)}, u32[]{:S(2)}) collective-permute-start(bf16[32,8192]{1,0:T(8,128)(2,1)S(1)} %dynamic-slice_bitcast_fusion), channel_id=1, source_target_pairs={{0,1},{1,0},{2,3},{3,2},{4,5},{5,4},{6,7},{7,6},{8,9},{9,8},{10,11... | collective-permute-start | bytes 1572872 | tf_op jit(solution)/shard_map/ppermute | solution.py:75
  4.9 14.0 %collective-permute-start.1 = (bf16[32,8192]{1,0:T(8,128)(2,1)S(1)}, bf16[32,8192]{1,0:T(8,128)(2,1)S(1)}, u32[]{:S(2)}, u32[]{:S(2)}) collective-permute-start(bf16[32,8192]{1,0:T(8,128)(2,1)S(1)} %fusion.15), channel_id=1, source_target_pairs={{0,2},{1,3},{2,0},{3,1},{4,6},{5,7},{6,4},{7,5},{8,10},{9,11},{10,... | collective-permute-start | bytes 1572872 | tf_op jit(solution)/shard_map/ppermute | solution.py:75
  6.6 12.4 %copy-start.1 = (bf16[1,64,8192]{2,1,0:T(8,128)(2,1)S(1)}, bf16[1,64,8192]{2,1,0:T(8,128)(2,1)}, u32[]{:S(2)}) copy-start(bf16[1,64,8192]{2,1,0:T(8,128)(2,1)} %param.10) | copy-start | bytes 3145732
  20.4 0.7 copy-start.10
  20.7 2.2 %collective-permute-start.2 = (bf16[32,10240]{1,0:T(8,128)(2,1)S(1)}, bf16[32,10240]{1,0:T(8,128)(2,1)S(1)}, u32[]{:S(2)}, u32[]{:S(2)}) collective-permute-start(bf16[32,10240]{1,0:T(8,128)(2,1)S(1)} %pad_maximum_fusion), channel_id=1, source_target_pairs={{0,1},{1,0},{2,3},{3,2},{4,5},{5,4},{6,7},{7,6},{8,9},{9,8},{10,11... | collective-permute-start | bytes 1966088 | tf_op jit(solution)/shard_map/ppermute | solution.py:75
  22.9 32.2 %copy-start.9 = (bf16[2048,1024]{1,0:T(8,128)(2,1)S(1)}, bf16[2048,1024]{1,0:T(8,128)(2,1)}, u32[]{:S(2)}) copy-start(bf16[2048,1024]{1,0:T(8,128)(2,1)} %param.14) | copy-start | bytes 12582916
  22.9 36.1 %slice-start = ((s8[8388608]{0:T(1024)(128)(4,1)}), s8[4194304]{0:T(1024)(128)(4,1)S(1)}, s32[]{:S(2)}) async-start(s8[8388608]{0:T(1024)(128)(4,1)} %bitcast.108), calls=%async_computation.2 | async-start | bytes 8388608
  55.1 2.0 %copy-start.2 = (bf16[1024,2,256]{2,1,0:T(2,128)(2,1)S(1)}, bf16[1024,2,256]{2,1,0:T(2,128)(2,1)}, u32[]{:S(2)}) copy-start(bf16[1024,2,256]{2,1,0:T(2,128)(2,1)} %param.15) | copy-start | bytes 3145732
  55.2 3.9 %slice-start.1 = ((s8[8388608]{0:T(1024)(128)(4,1)}), s8[4194304]{0:T(1024)(128)(4,1)S(1)}, s32[]{:S(2)}) async-start(s8[8388608]{0:T(1024)(128)(4,1)} %bitcast.108), calls=%async_computation.3 | async-start | bytes 8388608
  56.9 1.0 %copy-start = (bf16[64,2048]{1,0:T(8,128)(2,1)S(1)}, bf16[64,2048]{1,0:T(8,128)(2,1)}, u32[]{:S(2)}) copy-start(bf16[64,2048]{1,0:T(8,128)(2,1)} %q_ref.3) | copy-start | bytes 786436
  57.0 1.3 %collective-permute-start.3 = (f32[256,64]{0,1:T(8,128)S(1)}, f32[256,64]{0,1:T(8,128)S(1)}, u32[]{:S(2)}, u32[]{:S(2)}) collective-permute-start(f32[256,64]{0,1:T(8,128)S(1)} %select_reduce_fusion), channel_id=1, source_target_pairs={{0,1},{1,0},{2,3},{3,2},{4,5},{5,4},{6,7},{7,6},{8,9},{9,8},{10,11... | collective-permute-start | bytes 196616 | tf_op jit(solution)/shard_map/ppermute | solution.py:75
  58.4 4.3 %collective-permute-start.4 = (f32[256,64]{0,1:T(8,128)S(1)}, f32[256,64]{0,1:T(8,128)S(1)}, u32[]{:S(2)}, u32[]{:S(2)}) collective-permute-start(f32[256,64]{0,1:T(8,128)S(1)} %add.85), channel_id=1, source_target_pairs={{0,2},{1,3},{2,0},{3,1},{4,6},{5,7},{6,4},{7,5},{8,10},{9,11},{10,... | collective-permute-start | bytes 196616 | tf_op jit(solution)/shard_map/ppermute | solution.py:75
  64.0 14.8 %all-to-all-start.1 = ((bf16[32,8,512]{2,1,0:T(8,128)(2,1)}), bf16[32,8,512]{2,1,0:T(8,128)(2,1)S(1)}, u32[]{:S(2)}, u32[]{:S(2)}) async-start(bf16[32,8,512]{2,1,0:T(8,128)(2,1)} %fusion.4), calls=%async_computation.1 | async-start | bytes 524288 | tf_op jit(solution)/shard_map/all_to_all | solution.py:195
  67.8 10.9 %copy-start.6 = (f32[32,2048]{1,0:T(8,128)S(1)}, f32[32,2048]{1,0:T(8,128)}, u32[]{:S(2)}) copy-start(f32[32,2048]{1,0:T(8,128)} %get-tuple-element.31) | copy-start | bytes 786436
  67.8 10.9 %copy-start.7 = (f32[32,2048]{1,0:T(8,128)S(1)}, f32[32,2048]{1,0:T(8,128)}, u32[]{:S(2)}) copy-start(f32[32,2048]{1,0:T(8,128)} %get-tuple-element.35) | copy-start | bytes 786436
  80.3 1.9 %copy-start.3 = (f32[32,2048]{1,0:T(8,128)S(1)}, f32[32,2048]{1,0:T(8,128)}, u32[]{:S(2)}) copy-start(f32[32,2048]{1,0:T(8,128)} %get-tuple-element.33) | copy-start | bytes 786436
  80.4 1.9 %copy-start.4 = (f32[32,2048]{1,0:T(8,128)S(1)}, f32[32,2048]{1,0:T(8,128)}, u32[]{:S(2)}) copy-start(f32[32,2048]{1,0:T(8,128)} %get-tuple-element.34) | copy-start | bytes 786436
  80.9 2.6 %copy-start.5 = (bf16[64,2,256]{2,1,0:T(2,128)(2,1)}, bf16[64,2,256]{2,1,0:T(2,128)(2,1)S(1)}, u32[]{:S(2)}) copy-start(bf16[64,2,256]{2,1,0:T(2,128)(2,1)S(1)} %reshape.114) | copy-start | bytes 196612
